TPU v7x, 32 devices: a whole 2x2x4 slice. The times are simulated.
32 devices in a mesh: groups: 2 (over x), tm: 8 (over z, y), pair: 2 (over core).
Axes of the slice: x: 2, y: 2, z: 4, core: 2. Of those that a mesh axis runs over, the one named last changes fastest.
Arguments:
- recording: bfloat16 [2048, 65536], P(('groups', 'pair'), 'tm'), parts along dimension 0
- fir_taps: bfloat16 [256], replicated, may hold values from -0.375 to 0.375
- kept_windows: int32 [16], P('groups'), parts along dimension 0, may hold values from 4 to 16, as said below
- pair_blocks: int32 [32, 2], P(('groups', 'pair')), parts along dimension 0, may hold values from 0 to 7
Outputs:
- cross_spectra: float32 [32, 128, 2, 128, 128], P(('groups', 'pair'), 'tm'), parts along dimension 0
There are 2 independent parts, one for each index of `groups`. A program takes and returns all parts, laid end to end along the dimension named above; an argument that names none is the same for every part. Nothing has to cross between parts.
Inputs may be any that keep to these rules, and one draw needn't show every extreme that they name: Section s keeps its first kept_windows[s] windows; at least one section keeps all 16.
All inputs are finite; a program needn't handle non-finite values.
Results may differ from a plain program's by a relative error of at most 0.0056.
Values may be sent and summed in bfloat16 or wider, within the bound.
No kernel may reach another device: no remote copies, remote signals or barrier semaphores. Data moves between devices by JAX's collectives and lax.ppermute only.
A program may use at most 192 MiB of HBM per device.

v0:
```python
import functools
import math

import jax
import jax.numpy as jnp
from jax import lax
from jax.experimental import pallas as pl
from jax.experimental.pallas import tpu as pltpu
from jax.sharding import PartitionSpec as P

CH_BLK = 128
WIN = 512
NF = 128
FLO = 8


whiten_eps = 1e-06


def from_behind(array, axis, by):
    count = lax.axis_size(axis)
    pairs = [(i, i + by) for i in range(count) if 0 <= i + by < count]
    return lax.ppermute(array, axis, pairs)


def toeplitz(fir_taps):
    length = fir_taps.shape[0]
    reversed_taps = fir_taps[::-1]
    base_column = jnp.concatenate(
        [jnp.zeros((1,), fir_taps.dtype), reversed_taps, jnp.zeros((length,), fir_taps.dtype)]
    )
    flattened = jnp.tile(base_column, length)[: 2 * length * length]
    return flattened.reshape(length, 2 * length).T


def bandpass(recording, fir_taps, tail_rows):
    channels, length = recording.shape
    width = fir_taps.shape[0]
    current = recording.reshape(channels, length // width, width)
    previous = jnp.concatenate([tail_rows[:, None, :], current[:, :-1, :]], axis=1)
    extended = jnp.concatenate([previous, current], axis=2).reshape(
        channels * (length // width), 2 * width
    )
    product = jnp.dot(extended, toeplitz(fir_taps), preferred_element_type=jnp.float32)
    return product.reshape(channels, length).astype(jnp.bfloat16)


def dft_table(length, bins, lowest):
    samples = jnp.arange(length, dtype=jnp.int32)
    indices = lowest + jnp.arange(bins, dtype=jnp.int32)
    phase = (samples[:, None] * indices[None, :] % length).astype(jnp.float32) * (
        2.0 * math.pi / length
    )
    basis_table = jnp.stack([jnp.cos(phase), -jnp.sin(phase)], axis=2)
    return basis_table.reshape(length, 2 * bins).astype(jnp.bfloat16)


def stack_kernel(blocks_per_half, pb_ref, kw_ref, a_ref, b_ref, o_ref):
    sections = kw_ref.shape[0]
    total = kw_ref[0]
    for s in range(1, sections):
        total = total + kw_ref[s]
    scale = 1.0 / jnp.sqrt(jnp.full((1, 1), total, jnp.int32).astype(jnp.float32))
    segs, bins, _, wins, blk = a_ref.shape

    def one_bin(jl, carry):
        left = a_ref[:, jl].reshape(segs * 2 * wins, blk)
        right = b_ref[:, jl]
        swapped = jnp.concatenate([right[:, 1:2], -right[:, 0:1]], axis=1)
        rhs = jnp.concatenate(
            [right.reshape(segs * 2 * wins, blk), swapped.reshape(segs * 2 * wins, blk)], axis=1
        )
        out = lax.dot_general(
            left, rhs, (((0,), (0,)), ((), ())), preferred_element_type=jnp.float32
        )
        o_ref[0, jl, 0] = out[:, :blk] * scale
        o_ref[0, jl, 1] = out[:, blk:] * scale
        return carry

    lax.fori_loop(0, bins, one_bin, 0)


def stack_pairs(gathered, pair_blocks, kept_windows):
    halves, segs, bins, two, wins, chans = gathered.shape
    blocks_per_half = chans // CH_BLK
    npairs = pair_blocks.shape[0]

    def left_map(p, pb, kw):
        a = pb[p, 0]
        return (a // blocks_per_half, 0, 0, 0, 0, a % blocks_per_half)

    def right_map(p, pb, kw):
        b = pb[p, 1]
        return (b // blocks_per_half, 0, 0, 0, 0, b % blocks_per_half)

    block = (None, segs, bins, two, wins, CH_BLK)
    grid_spec = pltpu.PrefetchScalarGridSpec(
        num_scalar_prefetch=2,
        grid=(npairs,),
        in_specs=[pl.BlockSpec(block, left_map), pl.BlockSpec(block, right_map)],
        out_specs=pl.BlockSpec((1, bins, 2, CH_BLK, CH_BLK), lambda p, pb, kw: (p, 0, 0, 0, 0)),
    )
    flops = 2 * npairs * bins * CH_BLK * (2 * CH_BLK) * (segs * two * wins)
    out_bytes = npairs * bins * 2 * CH_BLK * CH_BLK * 4
    in_bytes = 2 * npairs * segs * bins * two * wins * CH_BLK * 2
    return pl.pallas_call(
        functools.partial(stack_kernel, blocks_per_half),
        grid_spec=grid_spec,
        out_shape=jax.ShapeDtypeStruct((npairs, bins, 2, CH_BLK, CH_BLK), jnp.float32),
        compiler_params=pltpu.CompilerParams(
            dimension_semantics=("arbitrary",), vmem_limit_bytes=48 * 1024 * 1024
        ),
        cost_estimate=pl.CostEstimate(
            flops=flops, bytes_accessed=out_bytes + in_bytes, transcendentals=0
        ),
    )(pair_blocks, kept_windows, gathered, gathered)


def per_device(recording, fir_taps, kept_windows, pair_blocks):
    channels, length = recording.shape
    width = fir_taps.shape[0]
    sections = lax.axis_size("tm")
    tail_rows = from_behind(recording[:, length - width :], "tm", 1)
    filtered = bandpass(recording, fir_taps, tail_rows)
    windows_dev = length // WIN
    spectrum = jnp.einsum(
        "cwt,tk->kwc",
        filtered.reshape(channels, windows_dev, WIN),
        dft_table(WIN, NF, FLO),
        preferred_element_type=jnp.float32,
    )
    inverse_rms = lax.rsqrt(jnp.mean(spectrum * spectrum, axis=0, keepdims=True) + whiten_eps)
    segment = lax.axis_index("tm")
    kept_count = lax.dynamic_index_in_dim(kept_windows, segment, 0, keepdims=False)
    window_mask = (jnp.arange(windows_dev, dtype=jnp.int32) < kept_count).astype(jnp.float32)
    whitened = (spectrum * inverse_rms * window_mask[None, :, None]).astype(jnp.bfloat16)
    bins_dev = NF // sections
    outgoing = whitened.reshape(sections, bins_dev, 2, windows_dev, channels)
    by_freq = lax.all_to_all(outgoing, "tm", split_axis=0, concat_axis=0, tiled=True)
    gathered = lax.all_gather(by_freq, "pair", axis=0, tiled=False)
    return stack_pairs(gathered, pair_blocks, kept_windows)


def solution(mesh):
    placed = (P(("groups", "pair"), "tm"), P(), P("groups"), P(("groups", "pair"), None))
    return jax.shard_map(
        per_device,
        mesh=mesh,
        in_specs=placed,
        out_specs=P(("groups", "pair"), "tm", None, None, None),
        check_vma=False,
    )
```

profile of v0, /device:TPU:0, one launch (start us, length us, event | category | flops | bytes accessed | tf_op | source)
XLA Modules:
  0.0 241.9 jit_solution(11716149095161323212)
XLA Ops:
  6.5 0.0 all-gather.3.cloned.1.call-start
  6.5 1.0 slice.9
  7.5 4.9 %collective-permute-start = (bf16[512,256]{1,0:T(8,128)(2,1)S(1)}, bf16[512,256]{1,0:T(8,128)(2,1)S(1)}, u32[]{:S(2)}, u32[]{:S(2)}) collective-permute-start(bf16[512,256]{1,0:T(8,128)(2,1)S(1)} %slice.9), channel_id=1, source_target_pairs={{0,2},{2,4},{4,6},{6,8},{8,10},{10,12},{12,14},{1,3},{3,5},{5,7},{... | collective-permute-start | bytes 786440 | tf_op jit(solution)/shard_map/ppermute | solution.py:23
  12.4 1.1 cosine_convert_fusion
  13.6 13.4 %concatenate.16 = bf16[16384,256]{1,0:T(8,128)(2,1)} reshape(bf16[512,8192]{1,0:T(8,128)(2,1)} %param.4) | data formatting | bytes 16777216 | tf_op jit(solution)/shard_map/concatenate | solution.py:41
  27.0 0.2 copy.21
  27.2 0.1 reshape.147
  27.3 0.0 copy-start.2
  27.3 0.0 copy-start
  27.3 9.5 %copy.27 = bf16[64,8,32,256]{3,2,1,0:T(8,128)(2,1)} copy(bf16[64,8,32,256]{3,1,2,0:T(8,128)(2,1)} %bitcast.21) | data formatting | bytes 16777216
  36.9 0.0 copy-done.2
  36.9 0.1 rev.3
  37.0 0.1 pad_maximum_fusion.2
  37.1 0.6 tile.10
  37.7 0.2 reshape.144
  37.9 0.0 copy-done
  37.9 0.6 dynamic_slice.4
  38.5 0.6 compare_convert_fusion
  39.2 0.0 collective-permute-done
  39.2 0.4 copy.22
  39.6 11.9 %pad_maximum_fusion = bf16[512,32,256]{2,1,0:T(8,128)(2,1)} fusion(bf16[512,31,256]{2,1,0:T(8,128)(2,1)} %bitcast.24, bf16[512,1,256]{2,1,0:T(2,128)(2,1)S(1)} %copy.22), kind=kLoop, calls=%fused_computation.4 | loop fusion | flops 16777216 | bytes 16777216 | tf_op jit(solution)/shard_map/concatenate | solution.py:40
  51.5 10.2 %convolution_convert_fusion = bf16[16384,256]{1,0:T(8,128)(2,1)} fusion(bf16[256,512]{1,0:T(8,128)(2,1)S(1)} %reshape.144, bf16[16384,256]{1,0:T(8,128)(2,1)} %concatenate.16, bf16[16384,256]{1,0:T(8,128)(2,1)} %bitcast.26), kind=kOutput, calls=%fused_computation | convolution fusion | flops 4332716032 | bytes 25427968 | tf_op jit(solution)/shard_map/dot_general | solution.py:44
  61.8 12.9 %convert_element_type.46 = bf16[512,16,512]{2,1,0:T(8,128)(2,1)} reshape(bf16[16384,256]{1,0:T(8,128)(2,1)} %convolution_convert_fusion) | data formatting | bytes 16777216 | tf_op jit(solution)/shard_map/convert_element_type | solution.py:45
  74.6 10.0 %fusion.3 = (f32[16,512]{1,0:T(8,128)S(1)}, f32[256,512,16]{1,0,2:T(8,128)S(1)}) fusion(bf16[512,256,1]{0,1,2:T(8,128)(2,1)S(1)} %reshape.147, bf16[512,16,512]{2,1,0:T(8,128)(2,1)} %convert_element_type.46), kind=kOutput, calls=%fused_computation.7 | convolution fusion | flops 2151669760 | bytes 17072128 | tf_op jit(solution)/shard_map/cwt,tk->kwc/dot_general | solution.py:126
  84.6 1.6 fusion.5
  86.3 2.3 copy.26
  88.6 0.0 copy-start.1
  88.7 97.9 %all_to_all.5 = bf16[8,16,2,16,512]{4,3,2,1,0:T(8,128)(2,1)} all-to-all(bf16[8,16,2,16,512]{4,3,2,1,0:T(8,128)(2,1)S(1)} %bitcast.25), channel_id=1, replica_groups=mesh['groups'=2,'tm'=8,'pair'=2] {'tm'}, dimensions={0} | all-to-all | bytes 8388608 | tf_op jit(solution)/shard_map/all_to_all | solution.py:139
  186.5 0.0 all-gather.3.cloned.1.call-update
  186.6 0.0 copy-done.1
  186.6 0.1 copy.25.pb_ref
  186.7 18.7 %all-gather.3.cloned.1.call-done = bf16[16,16,2,16,512]{4,3,2,1,0:T(8,128)(2,1)} async-done(((bf16[8,16,2,16,512]{4,3,2,1,0:T(8,128)(2,1)}), bf16[16,16,2,16,512]{4,3,2,1,0:T(8,128)(2,1)}) %all-gather.3.cloned.1.call-update) | async-done | bytes 8388624 | tf_op jit(solution)/shard_map/all_gather | solution.py:140
  205.4 29.7 %shard_map.46 = f32[8,16,2,128,128]{4,3,2,1,0:T(8,128)} custom-call(s32[8,2]{1,0:T(8,128)S(1)} %copy.25.pb_ref, s32[8]{0:T(128)S(1)} %copy-done, bf16[2,8,16,2,16,512]{5,4,3,2,1,0:T(8,128)(2,1)} %bitcast.22, bf16[2,8,16,2,16,512]{5,4,3,2,1,0:T(8,128)(2,1)} %bitcast.23), custom_call_target="tpu_custom_call" | custom-call | flops 2147483648 | bytes 33554432 | tf_op jit(solution)/shard_map/pallas_call | solution.py:106
  (6 shorter events, 0.1 us)
Async XLA Ops:
  6.5 198.8 %all-gather.3.cloned.1.call-start = ((), (), s32[]{:S(2)}) async-start(), calls=%async_computation.1 | async-start | bytes 12582912 | tf_op jit(solution)/shard_map/all_gather | solution.py:140
  7.5 31.7 %collective-permute-start = (bf16[512,256]{1,0:T(8,128)(2,1)S(1)}, bf16[512,256]{1,0:T(8,128)(2,1)S(1)}, u32[]{:S(2)}, u32[]{:S(2)}) collective-permute-start(bf16[512,256]{1,0:T(8,128)(2,1)S(1)} %slice.9), channel_id=1, source_target_pairs={{0,2},{2,4},{4,6},{6,8},{8,10},{10,12},{12,14},{1,3},{3,5},{5,7},{... | collective-permute-start | bytes 786440 | tf_op jit(solution)/shard_map/ppermute | solution.py:23
  27.3 9.6 %copy-start.2 = (bf16[256]{0:T(256)(128)(2,1)S(1)}, bf16[256]{0:T(256)(128)(2,1)}, u32[]{:S(2)}) copy-start(bf16[256]{0:T(256)(128)(2,1)} %param.5) | copy-start | bytes 1540
  27.3 10.6 %copy-start = (s32[8]{0:T(128)S(1)}, s32[8]{0:T(128)}, u32[]{:S(2)}) copy-start(s32[8]{0:T(128)} %kw_ref.1) | copy-start | bytes 100
  88.6 97.9 %copy-start.1 = (s32[8,2]{0,1:T(2,128)S(1)}, s32[8,2]{0,1:T(2,128)}, u32[]{:S(2)}) copy-start(s32[8,2]{0,1:T(2,128)} %param.7) | copy-start | bytes 196
Sparse Core Ops, SparseCore 0:
  186.7 18.6 all-gather.2
where the time goes:
time: 243 us; the launch traced here: 242 us
  blocking collectives  97.9 us (40%)
  local copies, waits for them, and re-layouts  41.5 us (17%)
  Pallas kernels  29.7 us (12%)
  matrix products  20.2 us (8%)
  waiting for transfers between devices  18.7 us (8%)
  other arithmetic  15.5 us (6%)
  between operations  13.6 us (6%)
  starting transfers between devices  4.89 us (2%)
    all_to_all x1, blocking collectives, per_device(): lax.all_to_all(outgoing, 'tm', split_axis=0, concat_axis=0, tiled=True)  97.9 us
    pallas_call x1, Pallas kernels, stack_pairs(): pl.pallas_call(functools.partial(stack_kernel, blocks_per_half), grid_spe...  29.7 us
    all_gather x1, waiting for transfers between devices, per_device(): gathered = lax.all_gather(by_freq, 'pair', axis=0, tiled=False)  18.7 us
    concatenate x1, local copies, waits for them, and re-layouts, bandpass(): jnp.concatenate([previous, current], axis=2)  13.4 us
    convert_element_type x1, local copies, waits for them, and re-layouts, bandpass(): return product.reshape(channels, length).astype(jnp.bfloat16)  12.9 us
    concatenate x1, other arithmetic, bandpass(): jnp.concatenate([tail_rows[:, None, :], current[:, :-1, :]], axis=1)  11.9 us
    dot_general x1, matrix products, bandpass(): jnp.dot(extended, toeplitz(fir_taps), preferred_element_type=jnp.float32)  10.2 us
    dot_general x1, matrix products, per_device(): jnp.einsum('cwt,tk->kwc', filtered.reshape(channels, windows_dev, WIN), d...  10 us
  transfers between devices with their start and end apart: 2, of which 1 were waited for; matrix products, arithmetic and copies ran while one was open for 11% of the time, Pallas kernels for 0%

commit v1 on v0

--- a/solution.py
+++ b/solution.py
@@ -55,23 +55,96 @@
     return basis_table.reshape(length, 2 * bins).astype(jnp.bfloat16)
 
 
-def stack_kernel(blocks_per_half, pb_ref, kw_ref, a_ref, b_ref, o_ref):
+def front_kernel(cnt_ref, rec_ref, tail_ref, toep_ref, basis_ref, o_ref, scr_ref, inv_ref):
+    tile, length = rec_ref.shape
+    width = tail_ref.shape[1]
+    bins2 = basis_ref.shape[1]
+    windows = length // WIN
+    toep = toep_ref[...]
+    basis = basis_ref[...]
+    count = cnt_ref[0]
+    for w in range(windows):
+        if w == 0:
+            ext0 = jnp.concatenate([tail_ref[...], rec_ref[:, 0:width]], axis=1)
+        else:
+            ext0 = rec_ref[:, WIN * w - width : WIN * w + width]
+        ext1 = rec_ref[:, WIN * w : WIN * w + 2 * width]
+        f0 = jnp.dot(ext0, toep, preferred_element_type=jnp.float32).astype(jnp.bfloat16)
+        f1 = jnp.dot(ext1, toep, preferred_element_type=jnp.float32).astype(jnp.bfloat16)
+        spec = jnp.dot(
+            jnp.concatenate([f0, f1], axis=1), basis, preferred_element_type=jnp.float32
+        ).T
+        for h in range(tile // CH_BLK):
+            scr_ref[h, pl.ds(bins2 * w, bins2), :] = spec[:, CH_BLK * h : CH_BLK * (h + 1)]
+        power = jnp.sum(spec * spec, axis=0, keepdims=True) * (1.0 / bins2)
+        keep = jnp.where(count > w, 1.0, 0.0).astype(jnp.float32)
+        inv_ref[pl.ds(w, 1), :] = lax.rsqrt(power + whiten_eps) * keep
+    scales = inv_ref[...]
+
+    def one_row(k, carry):
+        for h in range(tile // CH_BLK):
+            rows = scr_ref[h, pl.ds(k, windows, stride=bins2), :]
+            part = rows * scales[:, CH_BLK * h : CH_BLK * (h + 1)]
+            o_ref[k, :, CH_BLK * h : CH_BLK * (h + 1)] = part.astype(o_ref.dtype)
+        return carry
+
+    lax.fori_loop(0, bins2, one_row, 0)
+
+
+def whiten_front(recording, tail_rows, fir_taps, kept_count, tile=256):
+    channels, length = recording.shape
+    width = tail_rows.shape[1]
+    windows = length // WIN
+    toep = toeplitz(fir_taps)
+    basis = dft_table(WIN, NF, FLO)
+    bins2 = basis.shape[1]
+    grid_spec = pltpu.PrefetchScalarGridSpec(
+        num_scalar_prefetch=1,
+        grid=(channels // tile,),
+        in_specs=[
+            pl.BlockSpec((tile, length), lambda i, c: (i, 0)),
+            pl.BlockSpec((tile, width), lambda i, c: (i, 0)),
+            pl.BlockSpec(toep.shape, lambda i, c: (0, 0)),
+            pl.BlockSpec(basis.shape, lambda i, c: (0, 0)),
+        ],
+        out_specs=pl.BlockSpec((bins2, windows, tile), lambda i, c: (0, 0, i)),
+        scratch_shapes=[
+            pltpu.VMEM((tile // CH_BLK, windows * bins2, CH_BLK), jnp.float32),
+            pltpu.VMEM((windows, tile), jnp.float32),
+        ],
+    )
+    flops = 2 * channels * windows * 3 * (2 * width) * bins2 * 2
+    return pl.pallas_call(
+        front_kernel,
+        grid_spec=grid_spec,
+        out_shape=jax.ShapeDtypeStruct((bins2, windows, channels), jnp.bfloat16),
+        compiler_params=pltpu.CompilerParams(
+            dimension_semantics=("arbitrary",), vmem_limit_bytes=48 * 1024 * 1024
+        ),
+        cost_estimate=pl.CostEstimate(
+            flops=flops,
+            bytes_accessed=channels * length * 2 + bins2 * windows * channels * 2,
+            transcendentals=channels * windows,
+        ),
+    )(kept_count, recording, tail_rows, toep, basis)
+
+
+def stack_kernel(pb_ref, kw_ref, a_ref, b_ref, o_ref):
     sections = kw_ref.shape[0]
     total = kw_ref[0]
     for s in range(1, sections):
         total = total + kw_ref[s]
     scale = 1.0 / jnp.sqrt(jnp.full((1, 1), total, jnp.int32).astype(jnp.float32))
-    segs, bins, _, wins, blk = a_ref.shape
+    bins, blk, depth = a_ref.shape
+    half = depth // 2
 
     def one_bin(jl, carry):
-        left = a_ref[:, jl].reshape(segs * 2 * wins, blk)
-        right = b_ref[:, jl]
-        swapped = jnp.concatenate([right[:, 1:2], -right[:, 0:1]], axis=1)
-        rhs = jnp.concatenate(
-            [right.reshape(segs * 2 * wins, blk), swapped.reshape(segs * 2 * wins, blk)], axis=1
-        )
+        left = a_ref[jl]
+        right = b_ref[jl]
+        swapped = jnp.concatenate([right[:, half:], -right[:, :half]], axis=1)
+        rhs = jnp.concatenate([right, swapped], axis=0)
         out = lax.dot_general(
-            left, rhs, (((0,), (0,)), ((), ())), preferred_element_type=jnp.float32
+            left, rhs, (((1,), (1,)), ((), ())), preferred_element_type=jnp.float32
         )
         o_ref[0, jl, 0] = out[:, :blk] * scale
         o_ref[0, jl, 1] = out[:, blk:] * scale
@@ -81,30 +154,30 @@
 
 
 def stack_pairs(gathered, pair_blocks, kept_windows):
-    halves, segs, bins, two, wins, chans = gathered.shape
+    halves, bins, chans, depth = gathered.shape
     blocks_per_half = chans // CH_BLK
     npairs = pair_blocks.shape[0]
 
     def left_map(p, pb, kw):
         a = pb[p, 0]
-        return (a // blocks_per_half, 0, 0, 0, 0, a % blocks_per_half)
+        return (a // blocks_per_half, 0, a % blocks_per_half, 0)
 
     def right_map(p, pb, kw):
         b = pb[p, 1]
-        return (b // blocks_per_half, 0, 0, 0, 0, b % blocks_per_half)
-
-    block = (None, segs, bins, two, wins, CH_BLK)
+        return (b // blocks_per_half, 0, b % blocks_per_half, 0)
+
+    block = (None, bins, CH_BLK, depth)
     grid_spec = pltpu.PrefetchScalarGridSpec(
         num_scalar_prefetch=2,
         grid=(npairs,),
         in_specs=[pl.BlockSpec(block, left_map), pl.BlockSpec(block, right_map)],
         out_specs=pl.BlockSpec((1, bins, 2, CH_BLK, CH_BLK), lambda p, pb, kw: (p, 0, 0, 0, 0)),
     )
-    flops = 2 * npairs * bins * CH_BLK * (2 * CH_BLK) * (segs * two * wins)
+    flops = 2 * npairs * bins * CH_BLK * (2 * CH_BLK) * depth
     out_bytes = npairs * bins * 2 * CH_BLK * CH_BLK * 4
-    in_bytes = 2 * npairs * segs * bins * two * wins * CH_BLK * 2
+    in_bytes = 2 * npairs * bins * CH_BLK * depth * 2
     return pl.pallas_call(
-        functools.partial(stack_kernel, blocks_per_half),
+        stack_kernel,
         grid_spec=grid_spec,
         out_shape=jax.ShapeDtypeStruct((npairs, bins, 2, CH_BLK, CH_BLK), jnp.float32),
         compiler_params=pltpu.CompilerParams(
@@ -121,23 +194,17 @@
     width = fir_taps.shape[0]
     sections = lax.axis_size("tm")
     tail_rows = from_behind(recording[:, length - width :], "tm", 1)
-    filtered = bandpass(recording, fir_taps, tail_rows)
     windows_dev = length // WIN
-    spectrum = jnp.einsum(
-        "cwt,tk->kwc",
-        filtered.reshape(channels, windows_dev, WIN),
-        dft_table(WIN, NF, FLO),
-        preferred_element_type=jnp.float32,
-    )
-    inverse_rms = lax.rsqrt(jnp.mean(spectrum * spectrum, axis=0, keepdims=True) + whiten_eps)
     segment = lax.axis_index("tm")
-    kept_count = lax.dynamic_index_in_dim(kept_windows, segment, 0, keepdims=False)
-    window_mask = (jnp.arange(windows_dev, dtype=jnp.int32) < kept_count).astype(jnp.float32)
-    whitened = (spectrum * inverse_rms * window_mask[None, :, None]).astype(jnp.bfloat16)
+    kept_count = lax.dynamic_slice_in_dim(kept_windows, segment, 1, 0)
+    whitened = whiten_front(recording, tail_rows, fir_taps, kept_count)
     bins_dev = NF // sections
     outgoing = whitened.reshape(sections, bins_dev, 2, windows_dev, channels)
     by_freq = lax.all_to_all(outgoing, "tm", split_axis=0, concat_axis=0, tiled=True)
-    gathered = lax.all_gather(by_freq, "pair", axis=0, tiled=False)
+    by_chan = jnp.transpose(by_freq, (1, 4, 2, 0, 3)).reshape(
+        bins_dev, channels, 2 * sections * windows_dev
+    )
+    gathered = lax.all_gather(by_chan, "pair", axis=0, tiled=False)
     return stack_pairs(gathered, pair_blocks, kept_windows)
 
 

time: 243 us -> 206 us (0.85)
  local copies, waits for them, and re-layouts: 41.5 us -> 13.3 us
  Pallas kernels: 29.7 us -> 53.8 us
  matrix products: 20.2 us -> 0 us
  other arithmetic: 15.5 us -> 1.23 us
    pallas_call x1 -> x2, Pallas kernels: 29.7 us -> 53.8 us  [the longest x1 30.1 us: stack_pairs(): pl.pallas_call(stack_kernel, grid_spec=grid_spec, out_shape=jax.ShapeDtyp...]
    dot_general x2 -> x0, matrix products: 20.2 us -> none  [the longest x1 10.2 us: bandpass(): jnp.dot(extended, toeplitz(fir_taps), preferred_element_type=jnp.float32)]
    concatenate x1 -> x0, local copies, waits for them, and re-layouts: 13.4 us -> none  [bandpass(): jnp.concatenate([previous, current], axis=2)]
    convert_element_type x1 -> x0, local copies, waits for them, and re-layouts: 12.9 us -> none  [bandpass(): return product.reshape(channels, length).astype(jnp.bfloat16)]
    concatenate x1 -> x0, other arithmetic: 11.9 us -> none  [bandpass(): jnp.concatenate([tail_rows[:, None, :], current[:, :-1, :]], axis=1)]
    unnamed x8 -> x5, local copies, waits for them, and re-layouts: 9.64 us -> 0.74 us
    another operation x0 -> x1, local copies, waits for them, and re-layouts: none -> 6.36 us  [per_device(): gathered = lax.all_gather(by_chan, 'pair', axis=0, tiled=False)]
    all_to_all x0 -> x1, local copies, waits for them, and re-layouts: none -> 2.49 us  [per_device(): lax.all_to_all(outgoing, 'tm', split_axis=0, concat_axis=0, tiled=True)]
  transfers between devices with their start and end apart: 2 -> 2, of which waited for: 1 -> 2; matrix products, arithmetic and copies ran while one was open for 11% -> 2% of each run, Pallas kernels for 0% -> 0%
where the time goes in v1:
time: 206 us; the launch traced here: 205 us
  blocking collectives  99.1 us (48%)
  Pallas kernels  53.8 us (26%)
  waiting for transfers between devices  19.6 us (10%)
  between operations  13.5 us (7%)
  local copies, waits for them, and re-layouts  13.3 us (6%)
  starting transfers between devices  4.89 us (2%)
    all_to_all x1, blocking collectives, per_device(): lax.all_to_all(outgoing, 'tm', split_axis=0, concat_axis=0, tiled=True)  99.1 us
    pallas_call x1, Pallas kernels, stack_pairs(): pl.pallas_call(stack_kernel, grid_spec=grid_spec, out_shape=jax.ShapeDtyp...  30.1 us
    pallas_call x1, Pallas kernels, whiten_front(): pl.pallas_call(front_kernel, grid_spec=grid_spec, out_shape=jax.ShapeDtyp...  23.7 us
    all_gather x1, waiting for transfers between devices, per_device(): gathered = lax.all_gather(by_chan, 'pair', axis=0, tiled=False)  18.1 us
    another operation x1, local copies, waits for them, and re-layouts, per_device(): gathered = lax.all_gather(by_chan, 'pair', axis=0, tiled=False)  6.36 us
    ppermute x1, starting transfers between devices, from_behind(): return lax.ppermute(array, axis, pairs)  4.89 us
  transfers between devices with their start and end apart: 2, of which 2 were waited for; matrix products, arithmetic and copies ran while one was open for 2% of the time, Pallas kernels for 0%

profile of v1, /device:TPU:0, one launch (start us, length us, event | category | flops | bytes accessed | tf_op | source)
XLA Modules:
  0.0 205.4 jit_solution(6601930633525515631)
XLA Ops:
  6.5 0.0 copy-start
  6.5 0.0 all-gather.2.cloned.1.call-start
  6.5 1.0 slice.6
  7.5 4.9 %collective-permute-start = (bf16[512,256]{1,0:T(8,128)(2,1)S(1)}, bf16[512,256]{1,0:T(8,128)(2,1)S(1)}, u32[]{:S(2)}, u32[]{:S(2)}) collective-permute-start(bf16[512,256]{1,0:T(8,128)(2,1)S(1)} %slice.6), channel_id=1, source_target_pairs={{0,2},{2,4},{4,6},{6,8},{8,10},{10,12},{12,14},{1,3},{3,5},{5,7},{... | collective-permute-start | bytes 786440 | tf_op jit(solution)/shard_map/ppermute | solution.py:23
  12.4 1.1 cosine_convert_fusion
  13.6 0.7 rev.3
  14.3 0.2 copy.18
  14.5 0.1 convert_element_type.20
  14.7 0.1 copy.19.basis_ref
  14.8 0.1 pad_maximum_fusion.1
  14.9 0.6 tile.10
  15.6 0.2 reshape.113
  15.7 0.1 copy.17
  15.9 0.0 copy-done
  15.9 0.6 dynamic_slice.3.cnt_ref
  16.5 1.5 collective-permute-done.tail_ref
  17.9 23.7 %shard_map.46 = bf16[256,16,512]{2,1,0:T(8,128)(2,1)S(1)} custom-call(s32[1]{0:T(128)} %dynamic_slice.3.cnt_ref, bf16[512,8192]{1,0:T(8,128)(2,1)} %rec_ref.1, bf16[512,256]{1,0:T(8,128)(2,1)S(1)} %collective-permute-done.tail_ref, bf16[512,256]{1,0:T(8,128)(2,1)S(1)} %bitcast.8, bf16[512,256]{1,0:T(8,128)(2,1)S(1)} %copy.19.basis_ref), custom_call_target="tpu_custom_call" | custom-call | flops 12884901888 | bytes 12582912 | tf_op jit(solution)/shard_map/pallas_call | solution.py:117
  41.7 99.1 %all_to_all.5 = bf16[8,16,2,16,512]{4,3,2,1,0:T(8,128)(2,1)S(1)} all-to-all(bf16[8,16,2,16,512]{4,3,2,1,0:T(8,128)(2,1)S(1)} %bitcast.7), channel_id=1, replica_groups=mesh['groups'=2,'tm'=8,'pair'=2] {'tm'}, dimensions={0} | all-to-all | bytes 8388608 | tf_op jit(solution)/shard_map/all_to_all | solution.py:203
  140.8 2.5 %copy.20 = bf16[8,16,2,16,512]{4,3,0,2,1:T(8,128)(2,1)} copy(bf16[8,16,2,16,512]{4,3,2,1,0:T(8,128)(2,1)S(1)} %all_to_all.5) | data formatting | bytes 8388608 | tf_op jit(solution)/shard_map/all_to_all | solution.py:203
  143.3 6.4 %copy.21 = bf16[1,16,512,256]{3,2,1,0:T(8,128)(2,1)} copy(bf16[1,16,512,256]{2,3,1,0:T(8,128)(2,1)} %bitcast.9) | data formatting | bytes 8388608 | tf_op jit(solution)/shard_map/all_gather;reshape | solution.py:207
  149.6 0.0 copy-start.1
  149.6 0.0 all-gather.2.cloned.1.call-update
  149.7 0.7 copy-done.1
  150.3 0.1 copy.22.pb_ref
  150.4 18.1 %all-gather.2.cloned.1.call-done.a_ref.b_ref = bf16[2,16,512,256]{3,2,1,0:T(8,128)(2,1)} async-done(((bf16[1,16,512,256]{3,2,1,0:T(8,128)(2,1)}), bf16[2,16,512,256]{3,2,1,0:T(8,128)(2,1)}) %all-gather.2.cloned.1.call-update) | async-done | bytes 8388624 | tf_op jit(solution)/shard_map/all_gather | solution.py:207
  168.5 30.1 %shard_map.47 = f32[8,16,2,128,128]{4,3,2,1,0:T(8,128)} custom-call(s32[8,2]{1,0:T(8,128)S(1)} %copy.22.pb_ref, s32[8]{0:T(128)S(1)} %copy-done, bf16[2,16,512,256]{3,2,1,0:T(8,128)(2,1)} %all-gather.2.cloned.1.call-done.a_ref.b_ref, bf16[2,16,512,256]{3,2,1,0:T(8,128)(2,1)} %all-gather.2.cloned.1.call-done.a_ref.b_ref), custom_call_target="tpu_custom_call" | custom-call | flops 2147483648 | bytes 33554432 | tf_op jit(solution)/shard_map/pallas_call | solution.py:179
  (5 shorter events, 0.1 us)
Async XLA Ops:
  6.5 9.3 %copy-start = (s32[8]{0:T(128)S(1)}, s32[8]{0:T(128)}, u32[]{:S(2)}) copy-start(s32[8]{0:T(128)} %kw_ref.1) | copy-start | bytes 100
  6.5 161.9 %all-gather.2.cloned.1.call-start = ((), (), s32[]{:S(2)}) async-start(), calls=%async_computation.1 | async-start | bytes 12582912 | tf_op jit(solution)/shard_map/all_gather | solution.py:207
  7.5 10.4 %collective-permute-start = (bf16[512,256]{1,0:T(8,128)(2,1)S(1)}, bf16[512,256]{1,0:T(8,128)(2,1)S(1)}, u32[]{:S(2)}, u32[]{:S(2)}) collective-permute-start(bf16[512,256]{1,0:T(8,128)(2,1)S(1)} %slice.6), channel_id=1, source_target_pairs={{0,2},{2,4},{4,6},{6,8},{8,10},{10,12},{12,14},{1,3},{3,5},{5,7},{... | collective-permute-start | bytes 786440 | tf_op jit(solution)/shard_map/ppermute | solution.py:23
  149.6 0.7 copy-start.1
Sparse Core Ops, SparseCore 0:
  149.8 18.6 all-gather.1

commit v2 on v1

--- a/solution.py
+++ b/solution.py
@@ -21,6 +21,17 @@
     count = lax.axis_size(axis)
     pairs = [(i, i + by) for i in range(count) if 0 <= i + by < count]
     return lax.ppermute(array, axis, pairs)
+
+
+def exchange(outgoing, axis):
+    count = lax.axis_size(axis)
+    me = lax.axis_index(axis)
+    pieces = [lax.dynamic_index_in_dim(outgoing, me, 0, keepdims=False)]
+    for shift in range(1, count):
+        piece = lax.dynamic_index_in_dim(outgoing, (me + shift) % count, 0, keepdims=False)
+        pairs = [(i, (i + shift) % count) for i in range(count)]
+        pieces.append(lax.ppermute(piece, axis, pairs))
+    return jnp.stack(pieces)
 
 
 def toeplitz(fir_taps):
@@ -91,12 +102,14 @@
     lax.fori_loop(0, bins2, one_row, 0)
 
 
-def whiten_front(recording, tail_rows, fir_taps, kept_count, tile=256):
+def whiten_front(recording, tail_rows, fir_taps, kept_count, chunks, tile=256):
     channels, length = recording.shape
     width = tail_rows.shape[1]
     windows = length // WIN
     toep = toeplitz(fir_taps)
-    basis = dft_table(WIN, NF, FLO)
+    sections = lax.axis_size("tm")
+    basis = dft_table(WIN, NF, FLO).reshape(WIN, sections, chunks, NF // sections // chunks, 2)
+    basis = jnp.transpose(basis, (0, 2, 1, 3, 4)).reshape(WIN, 2 * NF)
     bins2 = basis.shape[1]
     grid_spec = pltpu.PrefetchScalarGridSpec(
         num_scalar_prefetch=1,
@@ -129,22 +142,24 @@
     )(kept_count, recording, tail_rows, toep, basis)
 
 
-def stack_kernel(pb_ref, kw_ref, a_ref, b_ref, o_ref):
+def stack_kernel(pb_ref, kw_ref, a_ref, b_ref, *rest):
+    o_ref = rest[-1]
     sections = kw_ref.shape[0]
     total = kw_ref[0]
     for s in range(1, sections):
         total = total + kw_ref[s]
     scale = 1.0 / jnp.sqrt(jnp.full((1, 1), total, jnp.int32).astype(jnp.float32))
-    bins, blk, depth = a_ref.shape
-    half = depth // 2
+    segs, bins, _, wins, blk = a_ref.shape
 
     def one_bin(jl, carry):
-        left = a_ref[jl]
-        right = b_ref[jl]
-        swapped = jnp.concatenate([right[:, half:], -right[:, :half]], axis=1)
-        rhs = jnp.concatenate([right, swapped], axis=0)
+        left = a_ref[:, jl].reshape(segs * 2 * wins, blk)
+        right = b_ref[:, jl]
+        swapped = jnp.concatenate([right[:, 1:2], -right[:, 0:1]], axis=1)
+        rhs = jnp.concatenate(
+            [right.reshape(segs * 2 * wins, blk), swapped.reshape(segs * 2 * wins, blk)], axis=1
+        )
         out = lax.dot_general(
-            left, rhs, (((1,), (1,)), ((), ())), preferred_element_type=jnp.float32
+            left, rhs, (((0,), (0,)), ((), ())), preferred_element_type=jnp.float32
         )
         o_ref[0, jl, 0] = out[:, :blk] * scale
         o_ref[0, jl, 1] = out[:, blk:] * scale
@@ -153,43 +168,53 @@
     lax.fori_loop(0, bins, one_bin, 0)
 
 
-def stack_pairs(gathered, pair_blocks, kept_windows):
-    halves, bins, chans, depth = gathered.shape
+def stack_pairs(gathered, pair_blocks, kept_windows, chunk, chunks, previous=None):
+    halves, segs, bins, two, wins, chans = gathered.shape
     blocks_per_half = chans // CH_BLK
     npairs = pair_blocks.shape[0]
 
     def left_map(p, pb, kw):
         a = pb[p, 0]
-        return (a // blocks_per_half, 0, a % blocks_per_half, 0)
+        return (a // blocks_per_half, 0, 0, 0, 0, a % blocks_per_half)
 
     def right_map(p, pb, kw):
         b = pb[p, 1]
-        return (b // blocks_per_half, 0, b % blocks_per_half, 0)
-
-    block = (None, bins, CH_BLK, depth)
+        return (b // blocks_per_half, 0, 0, 0, 0, b % blocks_per_half)
+
+    block = (None, segs, bins, two, wins, CH_BLK)
+    in_specs = [pl.BlockSpec(block, left_map), pl.BlockSpec(block, right_map)]
+    operands = [pair_blocks, kept_windows, gathered, gathered]
+    aliases = {}
+    if previous is not None:
+        in_specs.append(pl.BlockSpec(memory_space=pl.ANY))
+        operands.append(previous)
+        aliases = {4: 0}
     grid_spec = pltpu.PrefetchScalarGridSpec(
         num_scalar_prefetch=2,
         grid=(npairs,),
-        in_specs=[pl.BlockSpec(block, left_map), pl.BlockSpec(block, right_map)],
-        out_specs=pl.BlockSpec((1, bins, 2, CH_BLK, CH_BLK), lambda p, pb, kw: (p, 0, 0, 0, 0)),
-    )
-    flops = 2 * npairs * bins * CH_BLK * (2 * CH_BLK) * depth
+        in_specs=in_specs,
+        out_specs=pl.BlockSpec(
+            (1, bins, 2, CH_BLK, CH_BLK), lambda p, pb, kw: (p, chunk, 0, 0, 0)
+        ),
+    )
+    flops = 2 * npairs * bins * CH_BLK * (2 * CH_BLK) * (segs * two * wins)
     out_bytes = npairs * bins * 2 * CH_BLK * CH_BLK * 4
-    in_bytes = 2 * npairs * bins * CH_BLK * depth * 2
+    in_bytes = 2 * npairs * segs * bins * two * wins * CH_BLK * 2
     return pl.pallas_call(
         stack_kernel,
         grid_spec=grid_spec,
-        out_shape=jax.ShapeDtypeStruct((npairs, bins, 2, CH_BLK, CH_BLK), jnp.float32),
+        out_shape=jax.ShapeDtypeStruct((npairs, bins * chunks, 2, CH_BLK, CH_BLK), jnp.float32),
+        input_output_aliases=aliases,
         compiler_params=pltpu.CompilerParams(
             dimension_semantics=("arbitrary",), vmem_limit_bytes=48 * 1024 * 1024
         ),
         cost_estimate=pl.CostEstimate(
             flops=flops, bytes_accessed=out_bytes + in_bytes, transcendentals=0
         ),
-    )(pair_blocks, kept_windows, gathered, gathered)
-
-
-def per_device(recording, fir_taps, kept_windows, pair_blocks):
+    )(*operands)
+
+
+def per_device(recording, fir_taps, kept_windows, pair_blocks, chunks=2):
     channels, length = recording.shape
     width = fir_taps.shape[0]
     sections = lax.axis_size("tm")
@@ -197,15 +222,16 @@
     windows_dev = length // WIN
     segment = lax.axis_index("tm")
     kept_count = lax.dynamic_slice_in_dim(kept_windows, segment, 1, 0)
-    whitened = whiten_front(recording, tail_rows, fir_taps, kept_count)
     bins_dev = NF // sections
-    outgoing = whitened.reshape(sections, bins_dev, 2, windows_dev, channels)
-    by_freq = lax.all_to_all(outgoing, "tm", split_axis=0, concat_axis=0, tiled=True)
-    by_chan = jnp.transpose(by_freq, (1, 4, 2, 0, 3)).reshape(
-        bins_dev, channels, 2 * sections * windows_dev
-    )
-    gathered = lax.all_gather(by_chan, "pair", axis=0, tiled=False)
-    return stack_pairs(gathered, pair_blocks, kept_windows)
+    chunks = math.gcd(chunks, bins_dev)
+    whitened = whiten_front(recording, tail_rows, fir_taps, kept_count, chunks)
+    outgoing = whitened.reshape(chunks, sections, bins_dev // chunks, 2, windows_dev, channels)
+    result = None
+    for h in range(chunks):
+        by_freq = exchange(outgoing[h], "tm")
+        gathered = lax.all_gather(by_freq, "pair", axis=0, tiled=False)
+        result = stack_pairs(gathered, pair_blocks, kept_windows, h, chunks, result)
+    return result
 
 
 def solution(mesh):

time: 206 us -> 193 us (0.937)
  blocking collectives: 99.1 us -> 0 us
  starting transfers between devices: 4.89 us -> 44.4 us
  waiting for transfers between devices: 19.6 us -> 56.5 us
  local copies, waits for them, and re-layouts: 13.3 us -> 20.7 us
  Pallas kernels: 53.8 us -> 56.3 us
    all_to_all x1 -> x0, blocking collectives: 99.1 us -> none  [per_device(): lax.all_to_all(outgoing, 'tm', split_axis=0, concat_axis=0, tiled=True)]
    ppermute x0 -> x14, waiting for transfers between devices: none -> 55.3 us  [exchange(): pieces.append(lax.ppermute(piece, axis, pairs))]
    ppermute x0 -> x14, starting transfers between devices: none -> 39.4 us  [exchange(): pieces.append(lax.ppermute(piece, axis, pairs))]
    all_gather x1 -> x2, waiting for transfers between devices: 18.1 us -> 0.01 us  [per_device(): gathered = lax.all_gather(by_freq, 'pair', axis=0, tiled=False)]
    unnamed x5 -> x21, local copies, waits for them, and re-layouts: 0.74 us -> 13.2 us
    another operation x2, local copies, waits for them, and re-layouts: 6.56 us -> 1.46 us  [exchange(): return jnp.stack(pieces)]
    pallas_call x1 -> x2, Pallas kernels: 30.1 us -> 32.7 us  [stack_pairs(): pl.pallas_call(stack_kernel, grid_spec=grid_spec, out_shape=jax.ShapeDtyp...]
    all_to_all x1 -> x0, local copies, waits for them, and re-layouts: 2.49 us -> none  [per_device(): lax.all_to_all(outgoing, 'tm', split_axis=0, concat_axis=0, tiled=True)]
  transfers between devices with their start and end apart: 2 -> 17, of which waited for: 2 -> 7; matrix products, arithmetic and copies ran while one was open for 2% -> 8% of each run, Pallas kernels for 0% -> 8%
where the time goes in v2:
time: 193 us
  waiting for transfers between devices  56.5 us (29%)
  Pallas kernels  56.3 us (29%)
  starting transfers between devices  44.4 us (23%)
  local copies, waits for them, and re-layouts  20.7 us (11%)
  between operations  13.7 us (7%)
    ppermute x14, waiting for transfers between devices, exchange(): pieces.append(lax.ppermute(piece, axis, pairs))  55.3 us
    ppermute x14, starting transfers between devices, exchange(): pieces.append(lax.ppermute(piece, axis, pairs))  39.4 us
    pallas_call x2, Pallas kernels, stack_pairs(): pl.pallas_call(stack_kernel, grid_spec=grid_spec, out_shape=jax.ShapeDtyp...  32.7 us
    pallas_call x1, Pallas kernels, whiten_front(): pl.pallas_call(front_kernel, grid_spec=grid_spec, out_shape=jax.ShapeDtyp...  23.6 us
    unnamed x21, local copies, waits for them, and re-layouts  13.2 us
    ppermute x1, starting transfers between devices, from_behind(): return lax.ppermute(array, axis, pairs)  4.89 us
  transfers between devices with their start and end apart: 17, of which 7 were waited for; matrix products, arithmetic and copies ran while one was open for 8% of the time, Pallas kernels for 8%

profile of v2, /device:TPU:0, one launch (start us, length us, event | category | flops | bytes accessed | tf_op | source)
XLA Modules:
  0.0 193.0 jit_solution(14562209786293130364)
XLA Ops:
  6.5 1.0 slice.14
  7.5 4.9 %collective-permute-start = (bf16[512,256]{1,0:T(8,128)(2,1)S(1)}, bf16[512,256]{1,0:T(8,128)(2,1)S(1)}, u32[]{:S(2)}, u32[]{:S(2)}) collective-permute-start(bf16[512,256]{1,0:T(8,128)(2,1)S(1)} %slice.14), channel_id=1, source_target_pairs={{0,2},{2,4},{4,6},{6,8},{8,10},{10,12},{12,14},{1,3},{3,5},{5,7},{... | collective-permute-start | bytes 786440 | tf_op jit(solution)/shard_map/ppermute | solution.py:23
  12.4 1.2 cosine_convert_fusion
  13.8 0.7 rev.3
  14.5 0.0 copy-start.2
  14.6 0.2 copy.17
  14.8 0.1 reshape.115
  14.9 0.1 copy.18.basis_ref
  15.1 0.1 pad_maximum_fusion
  15.2 0.6 tile.10
  15.8 0.2 reshape.114
  16.0 0.1 copy.16
  16.2 0.6 dynamic_slice.52.cnt_ref
  16.8 1.2 collective-permute-done.tail_ref
  17.9 23.6 %shard_map.46 = bf16[256,16,512]{2,1,0:T(8,128)(2,1)S(1)} custom-call(s32[1]{0:T(128)} %dynamic_slice.52.cnt_ref, bf16[512,8192]{1,0:T(8,128)(2,1)} %rec_ref.1, bf16[512,256]{1,0:T(8,128)(2,1)S(1)} %collective-permute-done.tail_ref, bf16[512,256]{1,0:T(8,128)(2,1)S(1)} %bitcast.69, bf16[512,256]{1,0:T(8,128)(2,1)S(1)} %copy.18.basis_ref), custom_call_target="tpu_custom_call" | custom-call | flops 12884901888 | bytes 12582912 | tf_op jit(solution)/shard_map/pallas_call | solution.py:130
  41.6 0.4 fusion.6
  42.0 0.9 dynamic-slice_bitcast_fusion
  42.9 2.5 %collective-permute-start.8 = (bf16[8,2,16,512]{3,2,1,0:T(8,128)(2,1)S(1)}, bf16[8,2,16,512]{3,2,1,0:T(8,128)(2,1)S(1)}, u32[]{:S(2)}, u32[]{:S(2)}) collective-permute-start(bf16[8,2,16,512]{3,2,1,0:T(8,128)(2,1)S(1)} %get-tuple-element.13), channel_id=1, source_target_pairs={{0,2},{2,4},{4,6},{6,8},{8,10},{10,12},{12,14},{14,0},{1,3},{3,5},... | collective-permute-start | bytes 786440 | tf_op jit(solution)/shard_map/ppermute | solution.py:33
  45.4 1.6 collective-permute-start.9
  47.0 4.1 %collective-permute-start.14 = (bf16[8,2,16,512]{3,2,1,0:T(8,128)(2,1)S(1)}, bf16[8,2,16,512]{3,2,1,0:T(8,128)(2,1)S(1)}, u32[]{:S(2)}, u32[]{:S(2)}) collective-permute-start(bf16[8,2,16,512]{3,2,1,0:T(8,128)(2,1)S(1)} %get-tuple-element.7), channel_id=1, source_target_pairs={{0,14},{2,0},{4,2},{6,4},{8,6},{10,8},{12,10},{14,12},{1,15},{3,1}... | collective-permute-start | bytes 786440 | tf_op jit(solution)/shard_map/ppermute | solution.py:33
  51.1 0.2 collective-permute-start.13
  51.3 0.6 collective-permute-start.12
  51.9 3.9 %collective-permute-done.8 = bf16[8,2,16,512]{3,2,1,0:T(8,128)(2,1)S(1)} collective-permute-done((bf16[8,2,16,512]{3,2,1,0:T(8,128)(2,1)S(1)}, bf16[8,2,16,512]{3,2,1,0:T(8,128)(2,1)S(1)}, u32[]{:S(2)}, u32[]{:S(2)}) %collective-permute-start.8) | collective-permute-done | bytes 262176 | tf_op jit(solution)/shard_map/ppermute | solution.py:33
  55.8 0.0 collective-permute-start.10
  55.8 0.7 bitcast_dynamic-update-slice_fusion.6
  56.5 0.0 collective-permute-done.9
  56.6 16.8 %collective-permute-start.11 = (bf16[8,2,16,512]{3,2,1,0:T(8,128)(2,1)S(1)}, bf16[8,2,16,512]{3,2,1,0:T(8,128)(2,1)S(1)}, u32[]{:S(2)}, u32[]{:S(2)}) collective-permute-start(bf16[8,2,16,512]{3,2,1,0:T(8,128)(2,1)S(1)} %get-tuple-element.10), channel_id=1, source_target_pairs={{0,8},{2,10},{4,12},{6,14},{8,0},{10,2},{12,4},{14,6},{1,9},{3,11}... | collective-permute-start | bytes 786440 | tf_op jit(solution)/shard_map/ppermute | solution.py:33
  73.4 0.7 bitcast_dynamic-update-slice_fusion.5
  74.1 10.8 %collective-permute-done.10 = bf16[8,2,16,512]{3,2,1,0:T(8,128)(2,1)S(1)} collective-permute-done((bf16[8,2,16,512]{3,2,1,0:T(8,128)(2,1)S(1)}, bf16[8,2,16,512]{3,2,1,0:T(8,128)(2,1)S(1)}, u32[]{:S(2)}, u32[]{:S(2)}) %collective-permute-start.10) | collective-permute-done | bytes 262176 | tf_op jit(solution)/shard_map/ppermute | solution.py:33
  84.9 0.7 bitcast_dynamic-update-slice_fusion.4
  85.6 7.9 %collective-permute-done.11 = bf16[8,2,16,512]{3,2,1,0:T(8,128)(2,1)S(1)} collective-permute-done((bf16[8,2,16,512]{3,2,1,0:T(8,128)(2,1)S(1)}, bf16[8,2,16,512]{3,2,1,0:T(8,128)(2,1)S(1)}, u32[]{:S(2)}, u32[]{:S(2)}) %collective-permute-start.11) | collective-permute-done | bytes 262176 | tf_op jit(solution)/shard_map/ppermute | solution.py:33
  93.5 0.7 bitcast_dynamic-update-slice_fusion.3
  94.2 0.0 collective-permute-done.12
  94.2 0.7 bitcast_dynamic-update-slice_fusion.2
  94.9 0.0 collective-permute-done.13
  94.9 0.7 bitcast_dynamic-update-slice_fusion.1
  95.7 0.0 collective-permute-done.14
  95.7 0.7 bitcast_dynamic-update-slice_fusion
  96.4 0.0 all-gather.7.cloned.1.call-update
  96.4 0.0 all-gather.5.cloned.1.call-start
  96.5 1.0 dynamic-slice_bitcast_fusion.7
  97.4 0.3 collective-permute-start.1
  97.7 0.0 collective-permute-start.2
  97.7 4.4 %collective-permute-start.7 = (bf16[8,2,16,512]{3,2,1,0:T(8,128)(2,1)S(1)}, bf16[8,2,16,512]{3,2,1,0:T(8,128)(2,1)S(1)}, u32[]{:S(2)}, u32[]{:S(2)}) collective-permute-start(bf16[8,2,16,512]{3,2,1,0:T(8,128)(2,1)S(1)} %get-tuple-element.15), channel_id=1, source_target_pairs={{0,14},{2,0},{4,2},{6,4},{8,6},{10,8},{12,10},{14,12},{1,15},{3,1}... | collective-permute-start | bytes 786440 | tf_op jit(solution)/shard_map/ppermute | solution.py:33
  102.2 2.0 %collective-permute-start.6 = (bf16[8,2,16,512]{3,2,1,0:T(8,128)(2,1)S(1)}, bf16[8,2,16,512]{3,2,1,0:T(8,128)(2,1)S(1)}, u32[]{:S(2)}, u32[]{:S(2)}) collective-permute-start(bf16[8,2,16,512]{3,2,1,0:T(8,128)(2,1)S(1)} %get-tuple-element.16), channel_id=1, source_target_pairs={{0,12},{2,14},{4,0},{6,2},{8,4},{10,6},{12,8},{14,10},{1,13},{3,15... | collective-permute-start | bytes 786440 | tf_op jit(solution)/shard_map/ppermute | solution.py:33
  104.2 0.0 collective-permute-start.5
  104.2 5.3 %collective-permute-done.1 = bf16[8,2,16,512]{3,2,1,0:T(8,128)(2,1)S(1)} collective-permute-done((bf16[8,2,16,512]{3,2,1,0:T(8,128)(2,1)S(1)}, bf16[8,2,16,512]{3,2,1,0:T(8,128)(2,1)S(1)}, u32[]{:S(2)}, u32[]{:S(2)}) %collective-permute-start.1) | collective-permute-done | bytes 262176 | tf_op jit(solution)/shard_map/ppermute | solution.py:33
  109.5 0.7 bitcast_dynamic-update-slice_fusion.13
  110.3 0.0 collective-permute-done.2
  110.3 6.9 %collective-permute-start.4 = (bf16[8,2,16,512]{3,2,1,0:T(8,128)(2,1)S(1)}, bf16[8,2,16,512]{3,2,1,0:T(8,128)(2,1)S(1)}, u32[]{:S(2)}, u32[]{:S(2)}) collective-permute-start(bf16[8,2,16,512]{3,2,1,0:T(8,128)(2,1)S(1)} %get-tuple-element.18), channel_id=1, source_target_pairs={{0,8},{2,10},{4,12},{6,14},{8,0},{10,2},{12,4},{14,6},{1,9},{3,11}... | collective-permute-start | bytes 786440 | tf_op jit(solution)/shard_map/ppermute | solution.py:33
  117.2 0.7 bitcast_dynamic-update-slice_fusion.12
  117.9 23.5 %collective-permute-done.3 = bf16[8,2,16,512]{3,2,1,0:T(8,128)(2,1)S(1)} collective-permute-done((bf16[8,2,16,512]{3,2,1,0:T(8,128)(2,1)S(1)}, bf16[8,2,16,512]{3,2,1,0:T(8,128)(2,1)S(1)}, u32[]{:S(2)}, u32[]{:S(2)}) %collective-permute-start.3) | collective-permute-done | bytes 262176 | tf_op jit(solution)/shard_map/ppermute | solution.py:33
  141.4 0.7 bitcast_dynamic-update-slice_fusion.11
  142.1 3.9 %collective-permute-done.4 = bf16[8,2,16,512]{3,2,1,0:T(8,128)(2,1)S(1)} collective-permute-done((bf16[8,2,16,512]{3,2,1,0:T(8,128)(2,1)S(1)}, bf16[8,2,16,512]{3,2,1,0:T(8,128)(2,1)S(1)}, u32[]{:S(2)}, u32[]{:S(2)}) %collective-permute-start.4) | collective-permute-done | bytes 262176 | tf_op jit(solution)/shard_map/ppermute | solution.py:33
  146.0 0.7 bitcast_dynamic-update-slice_fusion.10
  146.7 0.7 bitcast_dynamic-update-slice_fusion.9
  147.5 0.7 bitcast_dynamic-update-slice_fusion.8
  148.2 0.7 bitcast_dynamic-update-slice_fusion.7
  148.9 0.0 all-gather.5.cloned.1.call-update
  149.0 0.1 copy.20.pb_ref
  149.1 2.2 %copy-done.1 = bf16[16,8,2,16,512]{4,3,2,1,0:T(8,128)(2,1)S(1)} copy-done((bf16[16,8,2,16,512]{4,3,2,1,0:T(8,128)(2,1)S(1)}, bf16[16,8,2,16,512]{4,3,2,1,0:T(8,128)(2,1)}, u32[]{:S(2)}) %copy-start.1) | copy-done | bytes 4194328
  151.2 16.4 %shard_map.47.rest_0_ = f32[8,16,2,128,128]{4,3,2,1,0:T(8,128)} custom-call(s32[8,2]{1,0:T(8,128)S(1)} %copy.20.pb_ref, s32[8]{0:T(128)S(1)} %copy-done.2, bf16[2,8,8,2,16,512]{5,4,3,2,1,0:T(8,128)(2,1)S(1)} %bitcast.67, bf16[2,8,8,2,16,512]{5,4,3,2,1,0:T(8,128)(2,1)S(1)} %bitcast.68), custom_call_target="tpu_custom_call" | custom-call | flops 1073741824 | bytes 16777216 | tf_op jit(solution)/shard_map/pallas_call | solution.py:203
  167.6 2.2 %copy-done = bf16[16,8,2,16,512]{4,3,2,1,0:T(8,128)(2,1)S(1)} copy-done((bf16[16,8,2,16,512]{4,3,2,1,0:T(8,128)(2,1)S(1)}, bf16[16,8,2,16,512]{4,3,2,1,0:T(8,128)(2,1)}, u32[]{:S(2)}) %copy-start) | copy-done | bytes 4194328
  169.8 16.4 %shard_map.48 = f32[8,16,2,128,128]{4,3,2,1,0:T(8,128)} custom-call(s32[8,2]{1,0:T(8,128)S(1)} %copy.20.pb_ref, s32[8]{0:T(128)S(1)} %copy-done.2, bf16[2,8,8,2,16,512]{5,4,3,2,1,0:T(8,128)(2,1)S(1)} %bitcast.65, bf16[2,8,8,2,16,512]{5,4,3,2,1,0:T(8,128)(2,1)S(1)} %bitcast.66, f32[8,16,2,128,128]{4,3,2,1,0:T(8,128)} %shard_map.47.rest_0_), custom_call_target="tpu_custom_call", output_to_operand_aliasing={{}: (4, {})} | custom-call | flops 1073741824 | bytes 16777216 | tf_op jit(solution)/shard_map/pallas_call | solution.py:203
  (17 shorter events, 0.1 us)
Async XLA Ops:
  6.5 142.5 %all-gather.7.cloned.1.call-start = ((), (), s32[]{:S(2)}) async-start(), calls=%async_computation.1 | async-start | bytes 6291456 | tf_op jit(solution)/shard_map/all_gather | solution.py:232
  7.5 10.4 %collective-permute-start = (bf16[512,256]{1,0:T(8,128)(2,1)S(1)}, bf16[512,256]{1,0:T(8,128)(2,1)S(1)}, u32[]{:S(2)}, u32[]{:S(2)}) collective-permute-start(bf16[512,256]{1,0:T(8,128)(2,1)S(1)} %slice.14), channel_id=1, source_target_pairs={{0,2},{2,4},{4,6},{6,8},{8,10},{10,12},{12,14},{1,3},{3,5},{5,7},{... | collective-permute-start | bytes 786440 | tf_op jit(solution)/shard_map/ppermute | solution.py:23
  14.5 1.6 copy-start.2
  42.9 12.9 %collective-permute-start.8 = (bf16[8,2,16,512]{3,2,1,0:T(8,128)(2,1)S(1)}, bf16[8,2,16,512]{3,2,1,0:T(8,128)(2,1)S(1)}, u32[]{:S(2)}, u32[]{:S(2)}) collective-permute-start(bf16[8,2,16,512]{3,2,1,0:T(8,128)(2,1)S(1)} %get-tuple-element.13), channel_id=1, source_target_pairs={{0,2},{2,4},{4,6},{6,8},{8,10},{10,12},{12,14},{14,0},{1,3},{3,5},... | collective-permute-start | bytes 786440 | tf_op jit(solution)/shard_map/ppermute | solution.py:33
  45.4 11.1 %collective-permute-start.9 = (bf16[8,2,16,512]{3,2,1,0:T(8,128)(2,1)S(1)}, bf16[8,2,16,512]{3,2,1,0:T(8,128)(2,1)S(1)}, u32[]{:S(2)}, u32[]{:S(2)}) collective-permute-start(bf16[8,2,16,512]{3,2,1,0:T(8,128)(2,1)S(1)} %get-tuple-element.12), channel_id=1, source_target_pairs={{0,4},{2,6},{4,8},{6,10},{8,12},{10,14},{12,0},{14,2},{1,5},{3,7},... | collective-permute-start | bytes 786440 | tf_op jit(solution)/shard_map/ppermute | solution.py:33
  47.0 48.7 %collective-permute-start.14 = (bf16[8,2,16,512]{3,2,1,0:T(8,128)(2,1)S(1)}, bf16[8,2,16,512]{3,2,1,0:T(8,128)(2,1)S(1)}, u32[]{:S(2)}, u32[]{:S(2)}) collective-permute-start(bf16[8,2,16,512]{3,2,1,0:T(8,128)(2,1)S(1)} %get-tuple-element.7), channel_id=1, source_target_pairs={{0,14},{2,0},{4,2},{6,4},{8,6},{10,8},{12,10},{14,12},{1,15},{3,1}... | collective-permute-start | bytes 786440 | tf_op jit(solution)/shard_map/ppermute | solution.py:33
  51.1 43.8 %collective-permute-start.13 = (bf16[8,2,16,512]{3,2,1,0:T(8,128)(2,1)S(1)}, bf16[8,2,16,512]{3,2,1,0:T(8,128)(2,1)S(1)}, u32[]{:S(2)}, u32[]{:S(2)}) collective-permute-start(bf16[8,2,16,512]{3,2,1,0:T(8,128)(2,1)S(1)} %get-tuple-element.8), channel_id=1, source_target_pairs={{0,12},{2,14},{4,0},{6,2},{8,4},{10,6},{12,8},{14,10},{1,13},{3,15... | collective-permute-start | bytes 786440 | tf_op jit(solution)/shard_map/ppermute | solution.py:33
  51.3 42.9 %collective-permute-start.12 = (bf16[8,2,16,512]{3,2,1,0:T(8,128)(2,1)S(1)}, bf16[8,2,16,512]{3,2,1,0:T(8,128)(2,1)S(1)}, u32[]{:S(2)}, u32[]{:S(2)}) collective-permute-start(bf16[8,2,16,512]{3,2,1,0:T(8,128)(2,1)S(1)} %get-tuple-element.9), channel_id=1, source_target_pairs={{0,10},{2,12},{4,14},{6,0},{8,2},{10,4},{12,6},{14,8},{1,11},{3,13... | collective-permute-start | bytes 786440 | tf_op jit(solution)/shard_map/ppermute | solution.py:33
  55.8 29.1 %collective-permute-start.10 = (bf16[8,2,16,512]{3,2,1,0:T(8,128)(2,1)S(1)}, bf16[8,2,16,512]{3,2,1,0:T(8,128)(2,1)S(1)}, u32[]{:S(2)}, u32[]{:S(2)}) collective-permute-start(bf16[8,2,16,512]{3,2,1,0:T(8,128)(2,1)S(1)} %get-tuple-element.11), channel_id=1, source_target_pairs={{0,6},{2,8},{4,10},{6,12},{8,14},{10,0},{12,2},{14,4},{1,7},{3,9},... | collective-permute-start | bytes 786440 | tf_op jit(solution)/shard_map/ppermute | solution.py:33
  56.6 36.9 %collective-permute-start.11 = (bf16[8,2,16,512]{3,2,1,0:T(8,128)(2,1)S(1)}, bf16[8,2,16,512]{3,2,1,0:T(8,128)(2,1)S(1)}, u32[]{:S(2)}, u32[]{:S(2)}) collective-permute-start(bf16[8,2,16,512]{3,2,1,0:T(8,128)(2,1)S(1)} %get-tuple-element.10), channel_id=1, source_target_pairs={{0,8},{2,10},{4,12},{6,14},{8,0},{10,2},{12,4},{14,6},{1,9},{3,11}... | collective-permute-start | bytes 786440 | tf_op jit(solution)/shard_map/ppermute | solution.py:33
  96.4 71.2 %all-gather.5.cloned.1.call-start = ((), (), s32[]{:S(2)}) async-start(), calls=%async_computation | async-start | bytes 6291456 | tf_op jit(solution)/shard_map/all_gather | solution.py:232
  97.4 12.1 %collective-permute-start.1 = (bf16[8,2,16,512]{3,2,1,0:T(8,128)(2,1)S(1)}, bf16[8,2,16,512]{3,2,1,0:T(8,128)(2,1)S(1)}, u32[]{:S(2)}, u32[]{:S(2)}) collective-permute-start(bf16[8,2,16,512]{3,2,1,0:T(8,128)(2,1)S(1)} %get-tuple-element.21), channel_id=1, source_target_pairs={{0,2},{2,4},{4,6},{6,8},{8,10},{10,12},{12,14},{14,0},{1,3},{3,5},... | collective-permute-start | bytes 786440 | tf_op jit(solution)/shard_map/ppermute | solution.py:33
  97.7 12.5 %collective-permute-start.2 = (bf16[8,2,16,512]{3,2,1,0:T(8,128)(2,1)S(1)}, bf16[8,2,16,512]{3,2,1,0:T(8,128)(2,1)S(1)}, u32[]{:S(2)}, u32[]{:S(2)}) collective-permute-start(bf16[8,2,16,512]{3,2,1,0:T(8,128)(2,1)S(1)} %get-tuple-element.20), channel_id=1, source_target_pairs={{0,4},{2,6},{4,8},{6,10},{8,12},{10,14},{12,0},{14,2},{1,5},{3,7},... | collective-permute-start | bytes 786440 | tf_op jit(solution)/shard_map/ppermute | solution.py:33
  97.7 50.5 %collective-permute-start.7 = (bf16[8,2,16,512]{3,2,1,0:T(8,128)(2,1)S(1)}, bf16[8,2,16,512]{3,2,1,0:T(8,128)(2,1)S(1)}, u32[]{:S(2)}, u32[]{:S(2)}) collective-permute-start(bf16[8,2,16,512]{3,2,1,0:T(8,128)(2,1)S(1)} %get-tuple-element.15), channel_id=1, source_target_pairs={{0,14},{2,0},{4,2},{6,4},{8,6},{10,8},{12,10},{14,12},{1,15},{3,1}... | collective-permute-start | bytes 786440 | tf_op jit(solution)/shard_map/ppermute | solution.py:33
  102.2 45.3 %collective-permute-start.6 = (bf16[8,2,16,512]{3,2,1,0:T(8,128)(2,1)S(1)}, bf16[8,2,16,512]{3,2,1,0:T(8,128)(2,1)S(1)}, u32[]{:S(2)}, u32[]{:S(2)}) collective-permute-start(bf16[8,2,16,512]{3,2,1,0:T(8,128)(2,1)S(1)} %get-tuple-element.16), channel_id=1, source_target_pairs={{0,12},{2,14},{4,0},{6,2},{8,4},{10,6},{12,8},{14,10},{1,13},{3,15... | collective-permute-start | bytes 786440 | tf_op jit(solution)/shard_map/ppermute | solution.py:33
  104.2 42.6 %collective-permute-start.5 = (bf16[8,2,16,512]{3,2,1,0:T(8,128)(2,1)S(1)}, bf16[8,2,16,512]{3,2,1,0:T(8,128)(2,1)S(1)}, u32[]{:S(2)}, u32[]{:S(2)}) collective-permute-start(bf16[8,2,16,512]{3,2,1,0:T(8,128)(2,1)S(1)} %get-tuple-element.17), channel_id=1, source_target_pairs={{0,10},{2,12},{4,14},{6,0},{8,2},{10,4},{12,6},{14,8},{1,11},{3,13... | collective-permute-start | bytes 786440 | tf_op jit(solution)/shard_map/ppermute | solution.py:33
  109.5 31.9 %collective-permute-start.3 = (bf16[8,2,16,512]{3,2,1,0:T(8,128)(2,1)S(1)}, bf16[8,2,16,512]{3,2,1,0:T(8,128)(2,1)S(1)}, u32[]{:S(2)}, u32[]{:S(2)}) collective-permute-start(bf16[8,2,16,512]{3,2,1,0:T(8,128)(2,1)S(1)} %get-tuple-element.19), channel_id=1, source_target_pairs={{0,6},{2,8},{4,10},{6,12},{8,14},{10,0},{12,2},{14,4},{1,7},{3,9},... | collective-permute-start | bytes 786440 | tf_op jit(solution)/shard_map/ppermute | solution.py:33
  110.3 35.7 %collective-permute-start.4 = (bf16[8,2,16,512]{3,2,1,0:T(8,128)(2,1)S(1)}, bf16[8,2,16,512]{3,2,1,0:T(8,128)(2,1)S(1)}, u32[]{:S(2)}, u32[]{:S(2)}) collective-permute-start(bf16[8,2,16,512]{3,2,1,0:T(8,128)(2,1)S(1)} %get-tuple-element.18), channel_id=1, source_target_pairs={{0,8},{2,10},{4,12},{6,14},{8,0},{10,2},{12,4},{14,6},{1,9},{3,11}... | collective-permute-start | bytes 786440 | tf_op jit(solution)/shard_map/ppermute | solution.py:33
  142.1 6.8 %copy-start.3 = (s32[8,2]{0,1:T(2,128)S(1)}, s32[8,2]{0,1:T(2,128)}, u32[]{:S(2)}) copy-start(s32[8,2]{0,1:T(2,128)} %param.7) | copy-start | bytes 196
  149.1 2.2 %copy-start.1 = (bf16[16,8,2,16,512]{4,3,2,1,0:T(8,128)(2,1)S(1)}, bf16[16,8,2,16,512]{4,3,2,1,0:T(8,128)(2,1)}, u32[]{:S(2)}) copy-start(bf16[16,8,2,16,512]{4,3,2,1,0:T(8,128)(2,1)} %all-gather.7.cloned.1.call-done) | copy-start | bytes 12582916
  167.6 2.2 %copy-start = (bf16[16,8,2,16,512]{4,3,2,1,0:T(8,128)(2,1)S(1)}, bf16[16,8,2,16,512]{4,3,2,1,0:T(8,128)(2,1)}, u32[]{:S(2)}) copy-start(bf16[16,8,2,16,512]{4,3,2,1,0:T(8,128)(2,1)} %all-gather.5.cloned.1.call-done) | copy-start | bytes 12582916
Sparse Core Ops, SparseCore 0:
  96.5 12.5 all-gather.6
  149.1 12.0 all-gather.4

commit v3 on v2

--- a/solution.py
+++ b/solution.py
@@ -142,7 +142,7 @@
     )(kept_count, recording, tail_rows, toep, basis)
 
 
-def stack_kernel(pb_ref, kw_ref, a_ref, b_ref, *rest):
+def stack_kernel(pb_ref, kw_ref, q_ref, a_ref, b_ref, *rest):
     o_ref = rest[-1]
     sections = kw_ref.shape[0]
     total = kw_ref[0]
@@ -165,36 +165,36 @@
         o_ref[0, jl, 1] = out[:, blk:] * scale
         return carry
 
-    lax.fori_loop(0, bins, one_bin, 0)
-
-
-def stack_pairs(gathered, pair_blocks, kept_windows, chunk, chunks, previous=None):
+    lax.fori_loop(0, bins, one_bin, 0, unroll=2)
+
+
+def stack_pairs(gathered, pair_blocks, kept_windows, half, chunk, chunks, previous=None):
     halves, segs, bins, two, wins, chans = gathered.shape
     blocks_per_half = chans // CH_BLK
     npairs = pair_blocks.shape[0]
 
-    def left_map(p, pb, kw):
+    def left_map(p, pb, kw, q):
         a = pb[p, 0]
-        return (a // blocks_per_half, 0, 0, 0, 0, a % blocks_per_half)
-
-    def right_map(p, pb, kw):
+        return ((a // blocks_per_half + q[0]) % halves, 0, 0, 0, 0, a % blocks_per_half)
+
+    def right_map(p, pb, kw, q):
         b = pb[p, 1]
-        return (b // blocks_per_half, 0, 0, 0, 0, b % blocks_per_half)
+        return ((b // blocks_per_half + q[0]) % halves, 0, 0, 0, 0, b % blocks_per_half)
 
     block = (None, segs, bins, two, wins, CH_BLK)
     in_specs = [pl.BlockSpec(block, left_map), pl.BlockSpec(block, right_map)]
-    operands = [pair_blocks, kept_windows, gathered, gathered]
+    operands = [pair_blocks, kept_windows, half, gathered, gathered]
     aliases = {}
     if previous is not None:
         in_specs.append(pl.BlockSpec(memory_space=pl.ANY))
         operands.append(previous)
-        aliases = {4: 0}
+        aliases = {5: 0}
     grid_spec = pltpu.PrefetchScalarGridSpec(
-        num_scalar_prefetch=2,
+        num_scalar_prefetch=3,
         grid=(npairs,),
         in_specs=in_specs,
         out_specs=pl.BlockSpec(
-            (1, bins, 2, CH_BLK, CH_BLK), lambda p, pb, kw: (p, chunk, 0, 0, 0)
+            (1, bins, 2, CH_BLK, CH_BLK), lambda p, pb, kw, q: (p, chunk, 0, 0, 0)
         ),
     )
     flops = 2 * npairs * bins * CH_BLK * (2 * CH_BLK) * (segs * two * wins)
@@ -226,11 +226,12 @@
     chunks = math.gcd(chunks, bins_dev)
     whitened = whiten_front(recording, tail_rows, fir_taps, kept_count, chunks)
     outgoing = whitened.reshape(chunks, sections, bins_dev // chunks, 2, windows_dev, channels)
+    half = jnp.zeros((1,), jnp.int32)
     result = None
     for h in range(chunks):
-        by_freq = exchange(outgoing[h], "tm")
+        by_freq = lax.all_to_all(outgoing[h], "tm", split_axis=0, concat_axis=0, tiled=True)
         gathered = lax.all_gather(by_freq, "pair", axis=0, tiled=False)
-        result = stack_pairs(gathered, pair_blocks, kept_windows, h, chunks, result)
+        result = stack_pairs(gathered, pair_blocks, kept_windows, half, h, chunks, result)
     return result
 
 

time: 193 us -> 181 us (0.938)
  blocking collectives: 0 us -> 105 us
  waiting for transfers between devices: 56.5 us -> 1.35 us
  starting transfers between devices: 44.4 us -> 4.93 us
  local copies, waits for them, and re-layouts: 20.7 us -> 8.66 us
  Pallas kernels: 56.3 us -> 45.7 us
    all_to_all x0 -> x2, blocking collectives: none -> 105 us  [per_device(): lax.all_to_all(outgoing[h], 'tm', split_axis=0, concat_axis=0, tiled=True)]
    ppermute x14 -> x0, waiting for transfers between devices: 55.3 us -> none  [exchange(): pieces.append(lax.ppermute(piece, axis, pairs))]
    ppermute x14 -> x0, starting transfers between devices: 39.4 us -> none  [exchange(): pieces.append(lax.ppermute(piece, axis, pairs))]
    pallas_call x2, Pallas kernels: 32.7 us -> 22 us  [stack_pairs(): pl.pallas_call(stack_kernel, grid_spec=grid_spec, out_shape=jax.ShapeDtyp...]
    unnamed x21 -> x9, local copies, waits for them, and re-layouts: 13.2 us -> 4.47 us
  transfers between devices with their start and end apart: 17 -> 3, of which waited for: 7 -> 1; matrix products, arithmetic and copies ran while one was open for 8% -> 2% of each run, Pallas kernels for 8% -> 6%
where the time goes in v3:
time: 181 us
  blocking collectives  105 us (58%)
  Pallas kernels  45.7 us (25%)
  between operations  13.5 us (7%)
  local copies, waits for them, and re-layouts  8.66 us (5%)
  starting transfers between devices  4.93 us (3%)
    all_to_all x2, blocking collectives, per_device(): lax.all_to_all(outgoing[h], 'tm', split_axis=0, concat_axis=0, tiled=True)  105 us
    pallas_call x1, Pallas kernels, whiten_front(): pl.pallas_call(front_kernel, grid_spec=grid_spec, out_shape=jax.ShapeDtyp...  23.7 us
    pallas_call x2, Pallas kernels, stack_pairs(): pl.pallas_call(stack_kernel, grid_spec=grid_spec, out_shape=jax.ShapeDtyp...  22 us
    ppermute x1, starting transfers between devices, from_behind(): return lax.ppermute(array, axis, pairs)  4.89 us
    unnamed x9, local copies, waits for them, and re-layouts  4.47 us
  transfers between devices with their start and end apart: 3, of which 1 were waited for; matrix products, arithmetic and copies ran while one was open for 2% of the time, Pallas kernels for 6%

profile of v3, /device:TPU:0, one launch (start us, length us, event | category | flops | bytes accessed | tf_op | source)
XLA Modules:
  0.0 180.9 jit_solution(11028946280863057211)
XLA Ops:
  6.5 0.0 copy-start.2
  6.5 0.0 all-gather.7.cloned.1.call-start
  6.5 1.0 slice.14
  7.5 4.9 %collective-permute-start = (bf16[512,256]{1,0:T(8,128)(2,1)S(1)}, bf16[512,256]{1,0:T(8,128)(2,1)S(1)}, u32[]{:S(2)}, u32[]{:S(2)}) collective-permute-start(bf16[512,256]{1,0:T(8,128)(2,1)S(1)} %slice.14), channel_id=1, source_target_pairs={{0,2},{2,4},{4,6},{6,8},{8,10},{10,12},{12,14},{1,3},{3,5},{5,7},{... | collective-permute-start | bytes 786440 | tf_op jit(solution)/shard_map/ppermute | solution.py:23
  12.4 1.2 cosine_convert_fusion
  13.7 0.7 rev.3
  14.5 0.2 copy.17
  14.7 0.1 reshape.115
  14.8 0.1 copy.18.basis_ref
  15.0 0.1 pad_maximum_fusion
  15.1 0.6 tile.10
  15.7 0.2 reshape.114
  15.9 0.1 copy.16
  16.0 0.0 copy-done.2
  16.0 0.6 dynamic_slice.3.cnt_ref
  16.6 1.3 collective-permute-done.tail_ref
  17.9 23.7 %shard_map.46 = bf16[256,16,512]{2,1,0:T(8,128)(2,1)S(1)} custom-call(s32[1]{0:T(128)} %dynamic_slice.3.cnt_ref, bf16[512,8192]{1,0:T(8,128)(2,1)} %rec_ref.1, bf16[512,256]{1,0:T(8,128)(2,1)S(1)} %collective-permute-done.tail_ref, bf16[512,256]{1,0:T(8,128)(2,1)S(1)} %bitcast.13, bf16[512,256]{1,0:T(8,128)(2,1)S(1)} %copy.18.basis_ref), custom_call_target="tpu_custom_call" | custom-call | flops 12884901888 | bytes 12582912 | tf_op jit(solution)/shard_map/pallas_call | solution.py:130
  41.7 0.4 fusion.6
  42.1 54.2 %all_to_all.10 = bf16[8,8,2,16,512]{4,3,2,1,0:T(8,128)(2,1)} all-to-all(bf16[8,8,2,16,512]{4,3,2,1,0:T(8,128)(2,1)S(1)} %bitcast.15), channel_id=1, replica_groups=mesh['groups'=2,'tm'=8,'pair'=2] {'tm'}, dimensions={0} | all-to-all | bytes 4194304 | tf_op jit(solution)/shard_map/all_to_all | solution.py:232
  96.3 0.0 copy-start.3
  96.3 0.0 all-gather.7.cloned.1.call-update
  96.3 0.0 all-gather.5.cloned.1.call-start
  96.3 51.2 %all_to_all.11 = bf16[8,8,2,16,512]{4,3,2,1,0:T(8,128)(2,1)} all-to-all(bf16[8,8,2,16,512]{4,3,2,1,0:T(8,128)(2,1)S(1)} %bitcast.14), channel_id=1, replica_groups=mesh['groups'=2,'tm'=8,'pair'=2] {'tm'}, dimensions={0} | all-to-all | bytes 4194304 | tf_op jit(solution)/shard_map/all_to_all | solution.py:232
  147.6 0.0 all-gather.5.cloned.1.call-update
  147.6 0.0 copy-done.3
  147.6 0.1 copy.20.pb_ref
  147.7 0.0 all-gather.7.cloned.1.call-done
  147.7 0.0 copy-start.1
  147.7 2.2 %copy-done.1 = bf16[16,8,2,16,512]{4,3,2,1,0:T(8,128)(2,1)S(1)} copy-done((bf16[16,8,2,16,512]{4,3,2,1,0:T(8,128)(2,1)S(1)}, bf16[16,8,2,16,512]{4,3,2,1,0:T(8,128)(2,1)}, u32[]{:S(2)}) %copy-start.1) | copy-done | bytes 4194328
  149.9 11.0 %shard_map.47.rest_0_ = f32[8,16,2,128,128]{4,3,2,1,0:T(8,128)} custom-call(s32[8,2]{1,0:T(8,128)S(1)} %copy.20.pb_ref, s32[8]{0:T(128)S(1)} %copy-done.2, s32[1]{0:T(128)} %constant.12.clone.1.q_ref, bf16[2,8,8,2,16,512]{5,4,3,2,1,0:T(8,128)(2,1)S(1)} %bitcast.11, bf16[2,8,8,2,16,512]{5,4,3,2,1,0:T(8,128)(2,1)S(1)} %bitcast.12), custom_call_target="tpu_custom_call" | custom-call | flops 1073741824 | bytes 16777216 | tf_op jit(solution)/shard_map/pallas_call | solution.py:203
  160.9 0.0 all-gather.5.cloned.1.call-done
  160.9 0.0 copy-start
  160.9 2.2 %copy-done = bf16[16,8,2,16,512]{4,3,2,1,0:T(8,128)(2,1)S(1)} copy-done((bf16[16,8,2,16,512]{4,3,2,1,0:T(8,128)(2,1)S(1)}, bf16[16,8,2,16,512]{4,3,2,1,0:T(8,128)(2,1)}, u32[]{:S(2)}) %copy-start) | copy-done | bytes 4194328
  163.1 11.0 %shard_map.48 = f32[8,16,2,128,128]{4,3,2,1,0:T(8,128)} custom-call(s32[8,2]{1,0:T(8,128)S(1)} %copy.20.pb_ref, s32[8]{0:T(128)S(1)} %copy-done.2, s32[1]{0:T(128)} %constant.12.clone.1.q_ref, bf16[2,8,8,2,16,512]{5,4,3,2,1,0:T(8,128)(2,1)S(1)} %bitcast.9, bf16[2,8,8,2,16,512]{5,4,3,2,1,0:T(8,128)(2,1)S(1)} %bitcast.10, ...), custom_call_target="tpu_custom_call", output_to_operand_aliasing={{}: (5, {})} | custom-call | flops 1073741824 | bytes 16777216 | tf_op jit(solution)/shard_map/pallas_call | solution.py:203
  (5 shorter events, 0.1 us)
Async XLA Ops:
  6.5 9.5 %copy-start.2 = (s32[8]{0:T(128)S(1)}, s32[8]{0:T(128)}, u32[]{:S(2)}) copy-start(s32[8]{0:T(128)} %kw_ref.3) | copy-start | bytes 100
  6.5 141.2 %all-gather.7.cloned.1.call-start = ((), (), s32[]{:S(2)}) async-start(), calls=%async_computation.3 | async-start | bytes 6291456 | tf_op jit(solution)/shard_map/all_gather | solution.py:233
  7.5 10.4 %collective-permute-start = (bf16[512,256]{1,0:T(8,128)(2,1)S(1)}, bf16[512,256]{1,0:T(8,128)(2,1)S(1)}, u32[]{:S(2)}, u32[]{:S(2)}) collective-permute-start(bf16[512,256]{1,0:T(8,128)(2,1)S(1)} %slice.14), channel_id=1, source_target_pairs={{0,2},{2,4},{4,6},{6,8},{8,10},{10,12},{12,14},{1,3},{3,5},{5,7},{... | collective-permute-start | bytes 786440 | tf_op jit(solution)/shard_map/ppermute | solution.py:23
  96.3 51.3 %copy-start.3 = (s32[8,2]{0,1:T(2,128)S(1)}, s32[8,2]{0,1:T(2,128)}, u32[]{:S(2)}) copy-start(s32[8,2]{0,1:T(2,128)} %param.7) | copy-start | bytes 196
  96.3 64.6 %all-gather.5.cloned.1.call-start = ((), (), s32[]{:S(2)}) async-start(), calls=%async_computation.2 | async-start | bytes 6291456 | tf_op jit(solution)/shard_map/all_gather | solution.py:233
  147.7 2.2 %copy-start.1 = (bf16[16,8,2,16,512]{4,3,2,1,0:T(8,128)(2,1)S(1)}, bf16[16,8,2,16,512]{4,3,2,1,0:T(8,128)(2,1)}, u32[]{:S(2)}) copy-start(bf16[16,8,2,16,512]{4,3,2,1,0:T(8,128)(2,1)} %all-gather.7.cloned.1.call-done) | copy-start | bytes 12582916
  160.9 2.2 %copy-start = (bf16[16,8,2,16,512]{4,3,2,1,0:T(8,128)(2,1)S(1)}, bf16[16,8,2,16,512]{4,3,2,1,0:T(8,128)(2,1)}, u32[]{:S(2)}) copy-start(bf16[16,8,2,16,512]{4,3,2,1,0:T(8,128)(2,1)} %all-gather.5.cloned.1.call-done) | copy-start | bytes 12582916
Sparse Core Ops, SparseCore 0:
  96.4 12.5 all-gather.6
  147.7 12.6 all-gather.4

commit v4 on v3

--- a/solution.py
+++ b/solution.py
@@ -74,22 +74,34 @@
     toep = toep_ref[...]
     basis = basis_ref[...]
     count = cnt_ref[0]
-    for w in range(windows):
-        if w == 0:
-            ext0 = jnp.concatenate([tail_ref[...], rec_ref[:, 0:width]], axis=1)
-        else:
-            ext0 = rec_ref[:, WIN * w - width : WIN * w + width]
-        ext1 = rec_ref[:, WIN * w : WIN * w + 2 * width]
-        f0 = jnp.dot(ext0, toep, preferred_element_type=jnp.float32).astype(jnp.bfloat16)
-        f1 = jnp.dot(ext1, toep, preferred_element_type=jnp.float32).astype(jnp.bfloat16)
-        spec = jnp.dot(
-            jnp.concatenate([f0, f1], axis=1), basis, preferred_element_type=jnp.float32
-        ).T
-        for h in range(tile // CH_BLK):
-            scr_ref[h, pl.ds(bins2 * w, bins2), :] = spec[:, CH_BLK * h : CH_BLK * (h + 1)]
-        power = jnp.sum(spec * spec, axis=0, keepdims=True) * (1.0 / bins2)
-        keep = jnp.where(count > w, 1.0, 0.0).astype(jnp.float32)
-        inv_ref[pl.ds(w, 1), :] = lax.rsqrt(power + whiten_eps) * keep
+    pair = 2
+    for w0 in range(0, windows, pair):
+        exts = []
+        for w in range(w0, w0 + pair):
+            if w == 0:
+                exts.append(jnp.concatenate([tail_ref[...], rec_ref[:, 0:width]], axis=1))
+            else:
+                exts.append(rec_ref[:, WIN * w - width : WIN * w + width])
+            exts.append(rec_ref[:, WIN * w : WIN * w + 2 * width])
+        filt = jnp.dot(
+            jnp.concatenate(exts, axis=0), toep, preferred_element_type=jnp.float32
+        ).astype(jnp.bfloat16)
+        frames = [
+            jnp.concatenate(
+                [filt[2 * i * tile : (2 * i + 1) * tile], filt[(2 * i + 1) * tile : (2 * i + 2) * tile]],
+                axis=1,
+            )
+            for i in range(pair)
+        ]
+        specs = jnp.dot(jnp.concatenate(frames, axis=0), basis, preferred_element_type=jnp.float32)
+        for i in range(pair):
+            w = w0 + i
+            spec = specs[i * tile : (i + 1) * tile].T
+            for h in range(tile // CH_BLK):
+                scr_ref[h, pl.ds(bins2 * w, bins2), :] = spec[:, CH_BLK * h : CH_BLK * (h + 1)]
+            power = jnp.sum(spec * spec, axis=0, keepdims=True) * (1.0 / bins2)
+            keep = jnp.where(count > w, 1.0, 0.0).astype(jnp.float32)
+            inv_ref[pl.ds(w, 1), :] = lax.rsqrt(power + whiten_eps) * keep
     scales = inv_ref[...]
 
     def one_row(k, carry):
@@ -165,7 +177,7 @@
         o_ref[0, jl, 1] = out[:, blk:] * scale
         return carry
 
-    lax.fori_loop(0, bins, one_bin, 0, unroll=2)
+    lax.fori_loop(0, bins, one_bin, 0, unroll=True)
 
 
 def stack_pairs(gathered, pair_blocks, kept_windows, half, chunk, chunks, previous=None):

time: 181 us -> 180 us (level)
  Pallas kernels: 45.7 us -> 41.6 us
  waiting for transfers between devices: 1.35 us -> 4.46 us
    pallas_call x2, Pallas kernels: 22 us -> 14.7 us  [stack_pairs(): pl.pallas_call(stack_kernel, grid_spec=grid_spec, out_shape=jax.ShapeDtyp...]
    pallas_call x1, Pallas kernels: 23.7 us -> 26.9 us  [whiten_front(): pl.pallas_call(front_kernel, grid_spec=grid_spec, out_shape=jax.ShapeDtyp...]
    all_gather x2, waiting for transfers between devices: 0.01 us -> 3.11 us  [per_device(): gathered = lax.all_gather(by_freq, 'pair', axis=0, tiled=False)]
  transfers between devices with their start and end apart: 3 -> 3, of which waited for: 1 -> 2; matrix products, arithmetic and copies ran while one was open for 2% -> 2% of each run, Pallas kernels for 6% -> 4%
where the time goes in v4:
time: 180 us
  blocking collectives  105 us (58%)
  Pallas kernels  41.6 us (23%)
  between operations  13.5 us (8%)
  local copies, waits for them, and re-layouts  8.66 us (5%)
  starting transfers between devices  4.93 us (3%)
  waiting for transfers between devices  4.46 us (2%)
    all_to_all x2, blocking collectives, per_device(): lax.all_to_all(outgoing[h], 'tm', split_axis=0, concat_axis=0, tiled=True)  105 us
    pallas_call x1, Pallas kernels, whiten_front(): pl.pallas_call(front_kernel, grid_spec=grid_spec, out_shape=jax.ShapeDtyp...  26.9 us
    pallas_call x2, Pallas kernels, stack_pairs(): pl.pallas_call(stack_kernel, grid_spec=grid_spec, out_shape=jax.ShapeDtyp...  14.7 us
    ppermute x1, starting transfers between devices, from_behind(): return lax.ppermute(array, axis, pairs)  4.89 us
    unnamed x9, local copies, waits for them, and re-layouts  4.46 us
  transfers between devices with their start and end apart: 3, of which 2 were waited for; matrix products, arithmetic and copies ran while one was open for 2% of the time, Pallas kernels for 4%

profile of v4, /device:TPU:0, one launch (start us, length us, event | category | flops | bytes accessed | tf_op | source)
XLA Modules:
  0.0 179.9 jit_solution(2080458037518953946)
XLA Ops:
  6.5 0.0 copy-start.2
  6.5 0.0 all-gather.7.cloned.1.call-start
  6.5 1.0 slice.14
  7.5 4.9 %collective-permute-start = (bf16[512,256]{1,0:T(8,128)(2,1)S(1)}, bf16[512,256]{1,0:T(8,128)(2,1)S(1)}, u32[]{:S(2)}, u32[]{:S(2)}) collective-permute-start(bf16[512,256]{1,0:T(8,128)(2,1)S(1)} %slice.14), channel_id=1, source_target_pairs={{0,2},{2,4},{4,6},{6,8},{8,10},{10,12},{12,14},{1,3},{3,5},{5,7},{... | collective-permute-start | bytes 786440 | tf_op jit(solution)/shard_map/ppermute | solution.py:23
  12.4 1.2 cosine_convert_fusion
  13.7 0.7 rev.3
  14.5 0.2 copy.17
  14.7 0.1 reshape.115
  14.8 0.1 copy.18.basis_ref
  15.0 0.1 pad_maximum_fusion
  15.1 0.6 tile.10
  15.7 0.2 reshape.114
  15.9 0.1 copy.16
  16.0 0.0 copy-done.2
  16.0 0.6 dynamic_slice.3.cnt_ref
  16.6 1.3 collective-permute-done.tail_ref
  17.9 26.9 %shard_map.46 = bf16[256,16,512]{2,1,0:T(8,128)(2,1)S(1)} custom-call(s32[1]{0:T(128)} %dynamic_slice.3.cnt_ref, bf16[512,8192]{1,0:T(8,128)(2,1)} %rec_ref.1, bf16[512,256]{1,0:T(8,128)(2,1)S(1)} %collective-permute-done.tail_ref, bf16[512,256]{1,0:T(8,128)(2,1)S(1)} %bitcast.13, bf16[512,256]{1,0:T(8,128)(2,1)S(1)} %copy.18.basis_ref), custom_call_target="tpu_custom_call" | custom-call | flops 12884901888 | bytes 12582912 | tf_op jit(solution)/shard_map/pallas_call | solution.py:142
  44.9 0.4 fusion.6
  45.3 54.2 %all_to_all.10 = bf16[8,8,2,16,512]{4,3,2,1,0:T(8,128)(2,1)} all-to-all(bf16[8,8,2,16,512]{4,3,2,1,0:T(8,128)(2,1)S(1)} %bitcast.15), channel_id=1, replica_groups=mesh['groups'=2,'tm'=8,'pair'=2] {'tm'}, dimensions={0} | all-to-all | bytes 4194304 | tf_op jit(solution)/shard_map/all_to_all | solution.py:244
  99.5 0.0 copy-start.3
  99.5 0.0 all-gather.7.cloned.1.call-update
  99.5 0.0 all-gather.5.cloned.1.call-start
  99.6 51.2 %all_to_all.11 = bf16[8,8,2,16,512]{4,3,2,1,0:T(8,128)(2,1)} all-to-all(bf16[8,8,2,16,512]{4,3,2,1,0:T(8,128)(2,1)S(1)} %bitcast.14), channel_id=1, replica_groups=mesh['groups'=2,'tm'=8,'pair'=2] {'tm'}, dimensions={0} | all-to-all | bytes 4194304 | tf_op jit(solution)/shard_map/all_to_all | solution.py:244
  150.8 0.0 all-gather.5.cloned.1.call-update
  150.8 0.0 copy-done.3
  150.8 0.1 copy.20.pb_ref
  150.9 0.0 all-gather.7.cloned.1.call-done
  150.9 0.0 copy-start.1
  150.9 2.2 %copy-done.1 = bf16[16,8,2,16,512]{4,3,2,1,0:T(8,128)(2,1)S(1)} copy-done((bf16[16,8,2,16,512]{4,3,2,1,0:T(8,128)(2,1)S(1)}, bf16[16,8,2,16,512]{4,3,2,1,0:T(8,128)(2,1)}, u32[]{:S(2)}) %copy-start.1) | copy-done | bytes 4194328
  153.1 7.3 %shard_map.47.rest_0_ = f32[8,16,2,128,128]{4,3,2,1,0:T(8,128)} custom-call(s32[8,2]{1,0:T(8,128)S(1)} %copy.20.pb_ref, s32[8]{0:T(128)S(1)} %copy-done.2, s32[1]{0:T(128)} %constant.12.clone.1.q_ref, bf16[2,8,8,2,16,512]{5,4,3,2,1,0:T(8,128)(2,1)S(1)} %bitcast.11, bf16[2,8,8,2,16,512]{5,4,3,2,1,0:T(8,128)(2,1)S(1)} %bitcast.12), custom_call_target="tpu_custom_call" | custom-call | flops 1073741824 | bytes 16777216 | tf_op jit(solution)/shard_map/pallas_call | solution.py:215
  160.5 3.1 %all-gather.5.cloned.1.call-done = bf16[16,8,2,16,512]{4,3,2,1,0:T(8,128)(2,1)} async-done(((bf16[8,8,2,16,512]{4,3,2,1,0:T(8,128)(2,1)}), bf16[16,8,2,16,512]{4,3,2,1,0:T(8,128)(2,1)}) %all-gather.5.cloned.1.call-update) | async-done | bytes 4194320 | tf_op jit(solution)/shard_map/all_gather | solution.py:245
  163.6 0.0 copy-start
  163.6 2.2 %copy-done = bf16[16,8,2,16,512]{4,3,2,1,0:T(8,128)(2,1)S(1)} copy-done((bf16[16,8,2,16,512]{4,3,2,1,0:T(8,128)(2,1)S(1)}, bf16[16,8,2,16,512]{4,3,2,1,0:T(8,128)(2,1)}, u32[]{:S(2)}) %copy-start) | copy-done | bytes 4194328
  165.8 7.3 %shard_map.48 = f32[8,16,2,128,128]{4,3,2,1,0:T(8,128)} custom-call(s32[8,2]{1,0:T(8,128)S(1)} %copy.20.pb_ref, s32[8]{0:T(128)S(1)} %copy-done.2, s32[1]{0:T(128)} %constant.12.clone.1.q_ref, bf16[2,8,8,2,16,512]{5,4,3,2,1,0:T(8,128)(2,1)S(1)} %bitcast.9, bf16[2,8,8,2,16,512]{5,4,3,2,1,0:T(8,128)(2,1)S(1)} %bitcast.10, ...), custom_call_target="tpu_custom_call", output_to_operand_aliasing={{}: (5, {})} | custom-call | flops 1073741824 | bytes 16777216 | tf_op jit(solution)/shard_map/pallas_call | solution.py:215
  (5 shorter events, 0.1 us)
Async XLA Ops:
  6.5 9.5 %copy-start.2 = (s32[8]{0:T(128)S(1)}, s32[8]{0:T(128)}, u32[]{:S(2)}) copy-start(s32[8]{0:T(128)} %kw_ref.3) | copy-start | bytes 100
  6.5 144.4 %all-gather.7.cloned.1.call-start = ((), (), s32[]{:S(2)}) async-start(), calls=%async_computation.3 | async-start | bytes 6291456 | tf_op jit(solution)/shard_map/all_gather | solution.py:245
  7.5 10.4 %collective-permute-start = (bf16[512,256]{1,0:T(8,128)(2,1)S(1)}, bf16[512,256]{1,0:T(8,128)(2,1)S(1)}, u32[]{:S(2)}, u32[]{:S(2)}) collective-permute-start(bf16[512,256]{1,0:T(8,128)(2,1)S(1)} %slice.14), channel_id=1, source_target_pairs={{0,2},{2,4},{4,6},{6,8},{8,10},{10,12},{12,14},{1,3},{3,5},{5,7},{... | collective-permute-start | bytes 786440 | tf_op jit(solution)/shard_map/ppermute | solution.py:23
  99.5 51.3 %copy-start.3 = (s32[8,2]{0,1:T(2,128)S(1)}, s32[8,2]{0,1:T(2,128)}, u32[]{:S(2)}) copy-start(s32[8,2]{0,1:T(2,128)} %param.7) | copy-start | bytes 196
  99.5 64.1 %all-gather.5.cloned.1.call-start = ((), (), s32[]{:S(2)}) async-start(), calls=%async_computation.2 | async-start | bytes 6291456 | tf_op jit(solution)/shard_map/all_gather | solution.py:245
  150.9 2.2 %copy-start.1 = (bf16[16,8,2,16,512]{4,3,2,1,0:T(8,128)(2,1)S(1)}, bf16[16,8,2,16,512]{4,3,2,1,0:T(8,128)(2,1)}, u32[]{:S(2)}) copy-start(bf16[16,8,2,16,512]{4,3,2,1,0:T(8,128)(2,1)} %all-gather.7.cloned.1.call-done) | copy-start | bytes 12582916
  163.6 2.2 %copy-start = (bf16[16,8,2,16,512]{4,3,2,1,0:T(8,128)(2,1)S(1)}, bf16[16,8,2,16,512]{4,3,2,1,0:T(8,128)(2,1)}, u32[]{:S(2)}) copy-start(bf16[16,8,2,16,512]{4,3,2,1,0:T(8,128)(2,1)} %all-gather.5.cloned.1.call-done) | copy-start | bytes 12582916
Sparse Core Ops, SparseCore 0:
  99.6 12.5 all-gather.6
  150.9 12.5 all-gather.4

commit v5 on v3

--- a/solution.py
+++ b/solution.py
@@ -102,7 +102,7 @@
     lax.fori_loop(0, bins2, one_row, 0)
 
 
-def whiten_front(recording, tail_rows, fir_taps, kept_count, chunks, tile=256):
+def whiten_front(recording, tail_rows, fir_taps, kept_count, chunks, tile=512):
     channels, length = recording.shape
     width = tail_rows.shape[1]
     windows = length // WIN
@@ -165,7 +165,7 @@
         o_ref[0, jl, 1] = out[:, blk:] * scale
         return carry
 
-    lax.fori_loop(0, bins, one_bin, 0, unroll=2)
+    lax.fori_loop(0, bins, one_bin, 0, unroll=True)
 
 
 def stack_pairs(gathered, pair_blocks, kept_windows, half, chunk, chunks, previous=None):

time: 181 us -> 175 us (0.967)
  Pallas kernels: 45.7 us -> 35.8 us
  waiting for transfers between devices: 1.35 us -> 4.47 us
    pallas_call x2, Pallas kernels: 22 us -> 14.7 us  [stack_pairs(): pl.pallas_call(stack_kernel, grid_spec=grid_spec, out_shape=jax.ShapeDtyp...]
    all_gather x2, waiting for transfers between devices: 0.01 us -> 3.12 us  [per_device(): gathered = lax.all_gather(by_freq, 'pair', axis=0, tiled=False)]
    pallas_call x1, Pallas kernels: 23.7 us -> 21.1 us  [whiten_front(): pl.pallas_call(front_kernel, grid_spec=grid_spec, out_shape=jax.ShapeDtyp...]
  transfers between devices with their start and end apart: 3 -> 3, of which waited for: 1 -> 2; matrix products, arithmetic and copies ran while one was open for 2% -> 2% of each run, Pallas kernels for 6% -> 4%
where the time goes in v5:
time: 175 us; the launch traced here: 174 us
  blocking collectives  105 us (60%)
  Pallas kernels  35.8 us (20%)
  between operations  13.5 us (8%)
  local copies, waits for them, and re-layouts  8.66 us (5%)
  starting transfers between devices  4.93 us (3%)
  waiting for transfers between devices  4.47 us (3%)
    all_to_all x2, blocking collectives, per_device(): lax.all_to_all(outgoing[h], 'tm', split_axis=0, concat_axis=0, tiled=True)  105 us
    pallas_call x1, Pallas kernels, whiten_front(): pl.pallas_call(front_kernel, grid_spec=grid_spec, out_shape=jax.ShapeDtyp...  21.1 us
    pallas_call x2, Pallas kernels, stack_pairs(): pl.pallas_call(stack_kernel, grid_spec=grid_spec, out_shape=jax.ShapeDtyp...  14.7 us
    ppermute x1, starting transfers between devices, from_behind(): return lax.ppermute(array, axis, pairs)  4.89 us
    unnamed x9, local copies, waits for them, and re-layouts  4.46 us
  transfers between devices with their start and end apart: 3, of which 2 were waited for; matrix products, arithmetic and copies ran while one was open for 2% of the time, Pallas kernels for 4%

profile of v5, /device:TPU:0, one launch (start us, length us, event | category | flops | bytes accessed | tf_op | source)
XLA Modules:
  0.0 174.1 jit_solution(16720722904188730265)
XLA Ops:
  6.5 0.0 copy-start.2
  6.5 0.0 all-gather.7.cloned.1.call-start
  6.5 1.0 slice.14
  7.5 4.9 %collective-permute-start = (bf16[512,256]{1,0:T(8,128)(2,1)S(1)}, bf16[512,256]{1,0:T(8,128)(2,1)S(1)}, u32[]{:S(2)}, u32[]{:S(2)}) collective-permute-start(bf16[512,256]{1,0:T(8,128)(2,1)S(1)} %slice.14), channel_id=1, source_target_pairs={{0,2},{2,4},{4,6},{6,8},{8,10},{10,12},{12,14},{1,3},{3,5},{5,7},{... | collective-permute-start | bytes 786440 | tf_op jit(solution)/shard_map/ppermute | solution.py:23
  12.4 1.2 cosine_convert_fusion
  13.7 0.7 rev.3
  14.5 0.2 copy.17
  14.7 0.1 reshape.115
  14.8 0.1 copy.18.basis_ref
  15.0 0.1 pad_maximum_fusion
  15.1 0.6 tile.10
  15.7 0.2 reshape.114
  15.9 0.1 copy.16
  16.0 0.0 copy-done.2
  16.0 0.6 dynamic_slice.3.cnt_ref
  16.6 1.3 collective-permute-done.tail_ref
  17.9 21.1 %shard_map.46 = bf16[256,16,512]{2,1,0:T(8,128)(2,1)S(1)} custom-call(s32[1]{0:T(128)} %dynamic_slice.3.cnt_ref, bf16[512,8192]{1,0:T(8,128)(2,1)} %rec_ref.1, bf16[512,256]{1,0:T(8,128)(2,1)S(1)} %collective-permute-done.tail_ref, bf16[512,256]{1,0:T(8,128)(2,1)S(1)} %bitcast.13, bf16[512,256]{1,0:T(8,128)(2,1)S(1)} %copy.18.basis_ref), custom_call_target="tpu_custom_call" | custom-call | flops 12884901888 | bytes 12582912 | tf_op jit(solution)/shard_map/pallas_call | solution.py:130
  39.1 0.4 fusion.6
  39.5 54.2 %all_to_all.10 = bf16[8,8,2,16,512]{4,3,2,1,0:T(8,128)(2,1)} all-to-all(bf16[8,8,2,16,512]{4,3,2,1,0:T(8,128)(2,1)S(1)} %bitcast.15), channel_id=1, replica_groups=mesh['groups'=2,'tm'=8,'pair'=2] {'tm'}, dimensions={0} | all-to-all | bytes 4194304 | tf_op jit(solution)/shard_map/all_to_all | solution.py:232
  93.7 0.0 copy-start.3
  93.7 0.0 all-gather.7.cloned.1.call-update
  93.7 0.0 all-gather.5.cloned.1.call-start
  93.7 51.2 %all_to_all.11 = bf16[8,8,2,16,512]{4,3,2,1,0:T(8,128)(2,1)} all-to-all(bf16[8,8,2,16,512]{4,3,2,1,0:T(8,128)(2,1)S(1)} %bitcast.14), channel_id=1, replica_groups=mesh['groups'=2,'tm'=8,'pair'=2] {'tm'}, dimensions={0} | all-to-all | bytes 4194304 | tf_op jit(solution)/shard_map/all_to_all | solution.py:232
  145.0 0.0 all-gather.5.cloned.1.call-update
  145.0 0.0 copy-done.3
  145.0 0.1 copy.20.pb_ref
  145.1 0.0 all-gather.7.cloned.1.call-done
  145.1 0.0 copy-start.1
  145.1 2.2 %copy-done.1 = bf16[16,8,2,16,512]{4,3,2,1,0:T(8,128)(2,1)S(1)} copy-done((bf16[16,8,2,16,512]{4,3,2,1,0:T(8,128)(2,1)S(1)}, bf16[16,8,2,16,512]{4,3,2,1,0:T(8,128)(2,1)}, u32[]{:S(2)}) %copy-start.1) | copy-done | bytes 4194328
  147.3 7.3 %shard_map.47.rest_0_ = f32[8,16,2,128,128]{4,3,2,1,0:T(8,128)} custom-call(s32[8,2]{1,0:T(8,128)S(1)} %copy.20.pb_ref, s32[8]{0:T(128)S(1)} %copy-done.2, s32[1]{0:T(128)} %constant.12.clone.1.q_ref, bf16[2,8,8,2,16,512]{5,4,3,2,1,0:T(8,128)(2,1)S(1)} %bitcast.11, bf16[2,8,8,2,16,512]{5,4,3,2,1,0:T(8,128)(2,1)S(1)} %bitcast.12), custom_call_target="tpu_custom_call" | custom-call | flops 1073741824 | bytes 16777216 | tf_op jit(solution)/shard_map/pallas_call | solution.py:203
  154.6 3.1 %all-gather.5.cloned.1.call-done = bf16[16,8,2,16,512]{4,3,2,1,0:T(8,128)(2,1)} async-done(((bf16[8,8,2,16,512]{4,3,2,1,0:T(8,128)(2,1)}), bf16[16,8,2,16,512]{4,3,2,1,0:T(8,128)(2,1)}) %all-gather.5.cloned.1.call-update) | async-done | bytes 4194320 | tf_op jit(solution)/shard_map/all_gather | solution.py:233
  157.8 0.0 copy-start
  157.8 2.2 %copy-done = bf16[16,8,2,16,512]{4,3,2,1,0:T(8,128)(2,1)S(1)} copy-done((bf16[16,8,2,16,512]{4,3,2,1,0:T(8,128)(2,1)S(1)}, bf16[16,8,2,16,512]{4,3,2,1,0:T(8,128)(2,1)}, u32[]{:S(2)}) %copy-start) | copy-done | bytes 4194328
  159.9 7.3 %shard_map.48 = f32[8,16,2,128,128]{4,3,2,1,0:T(8,128)} custom-call(s32[8,2]{1,0:T(8,128)S(1)} %copy.20.pb_ref, s32[8]{0:T(128)S(1)} %copy-done.2, s32[1]{0:T(128)} %constant.12.clone.1.q_ref, bf16[2,8,8,2,16,512]{5,4,3,2,1,0:T(8,128)(2,1)S(1)} %bitcast.9, bf16[2,8,8,2,16,512]{5,4,3,2,1,0:T(8,128)(2,1)S(1)} %bitcast.10, ...), custom_call_target="tpu_custom_call", output_to_operand_aliasing={{}: (5, {})} | custom-call | flops 1073741824 | bytes 16777216 | tf_op jit(solution)/shard_map/pallas_call | solution.py:203
  (5 shorter events, 0.1 us)
Async XLA Ops:
  6.5 9.5 %copy-start.2 = (s32[8]{0:T(128)S(1)}, s32[8]{0:T(128)}, u32[]{:S(2)}) copy-start(s32[8]{0:T(128)} %kw_ref.3) | copy-start | bytes 100
  6.5 138.6 %all-gather.7.cloned.1.call-start = ((), (), s32[]{:S(2)}) async-start(), calls=%async_computation.3 | async-start | bytes 6291456 | tf_op jit(solution)/shard_map/all_gather | solution.py:233
  7.5 10.4 %collective-permute-start = (bf16[512,256]{1,0:T(8,128)(2,1)S(1)}, bf16[512,256]{1,0:T(8,128)(2,1)S(1)}, u32[]{:S(2)}, u32[]{:S(2)}) collective-permute-start(bf16[512,256]{1,0:T(8,128)(2,1)S(1)} %slice.14), channel_id=1, source_target_pairs={{0,2},{2,4},{4,6},{6,8},{8,10},{10,12},{12,14},{1,3},{3,5},{5,7},{... | collective-permute-start | bytes 786440 | tf_op jit(solution)/shard_map/ppermute | solution.py:23
  93.7 51.3 %copy-start.3 = (s32[8,2]{0,1:T(2,128)S(1)}, s32[8,2]{0,1:T(2,128)}, u32[]{:S(2)}) copy-start(s32[8,2]{0,1:T(2,128)} %param.7) | copy-start | bytes 196
  93.7 64.1 %all-gather.5.cloned.1.call-start = ((), (), s32[]{:S(2)}) async-start(), calls=%async_computation.2 | async-start | bytes 6291456 | tf_op jit(solution)/shard_map/all_gather | solution.py:233
  145.1 2.2 %copy-start.1 = (bf16[16,8,2,16,512]{4,3,2,1,0:T(8,128)(2,1)S(1)}, bf16[16,8,2,16,512]{4,3,2,1,0:T(8,128)(2,1)}, u32[]{:S(2)}) copy-start(bf16[16,8,2,16,512]{4,3,2,1,0:T(8,128)(2,1)} %all-gather.7.cloned.1.call-done) | copy-start | bytes 12582916
  157.8 2.2 %copy-start = (bf16[16,8,2,16,512]{4,3,2,1,0:T(8,128)(2,1)S(1)}, bf16[16,8,2,16,512]{4,3,2,1,0:T(8,128)(2,1)}, u32[]{:S(2)}) copy-start(bf16[16,8,2,16,512]{4,3,2,1,0:T(8,128)(2,1)} %all-gather.5.cloned.1.call-done) | copy-start | bytes 12582916
Sparse Core Ops, SparseCore 0:
  93.8 12.5 all-gather.6
  145.1 12.5 all-gather.4

commit v6 on v5

--- a/solution.py
+++ b/solution.py
@@ -3,6 +3,8 @@
 
 import jax
 import jax.numpy as jnp
+import ml_dtypes
+import numpy as np
 from jax import lax
 from jax.experimental import pallas as pl
 from jax.experimental.pallas import tpu as pltpu
@@ -57,16 +59,17 @@
 
 
 def dft_table(length, bins, lowest):
-    samples = jnp.arange(length, dtype=jnp.int32)
-    indices = lowest + jnp.arange(bins, dtype=jnp.int32)
-    phase = (samples[:, None] * indices[None, :] % length).astype(jnp.float32) * (
+    samples = np.arange(length, dtype=np.int64)
+    indices = lowest + np.arange(bins, dtype=np.int64)
+    phase = (samples[:, None] * indices[None, :] % length).astype(np.float64) * (
         2.0 * math.pi / length
     )
-    basis_table = jnp.stack([jnp.cos(phase), -jnp.sin(phase)], axis=2)
-    return basis_table.reshape(length, 2 * bins).astype(jnp.bfloat16)
-
-
-def front_kernel(cnt_ref, rec_ref, tail_ref, toep_ref, basis_ref, o_ref, scr_ref, inv_ref):
+    basis_table = np.stack([np.cos(phase), -np.sin(phase)], axis=2)
+    return basis_table.reshape(length, 2 * bins).astype(ml_dtypes.bfloat16)
+
+
+def front_kernel(cnt_ref, rec_ref, tail_ref, toep_ref, basis_ref, *rest):
+    outs, (scr_ref, inv_ref) = rest[:-2], rest[-2:]
     tile, length = rec_ref.shape
     width = tail_ref.shape[1]
     bins2 = basis_ref.shape[1]
@@ -92,14 +95,18 @@
         inv_ref[pl.ds(w, 1), :] = lax.rsqrt(power + whiten_eps) * keep
     scales = inv_ref[...]
 
-    def one_row(k, carry):
-        for h in range(tile // CH_BLK):
-            rows = scr_ref[h, pl.ds(k, windows, stride=bins2), :]
-            part = rows * scales[:, CH_BLK * h : CH_BLK * (h + 1)]
-            o_ref[k, :, CH_BLK * h : CH_BLK * (h + 1)] = part.astype(o_ref.dtype)
-        return carry
-
-    lax.fori_loop(0, bins2, one_row, 0)
+    start = 0
+    for o_ref in outs:
+
+        def one_row(k, carry, o_ref=o_ref, start=start):
+            for h in range(tile // CH_BLK):
+                rows = scr_ref[h, pl.ds(start + k, windows, stride=bins2), :]
+                part = rows * scales[:, CH_BLK * h : CH_BLK * (h + 1)]
+                o_ref[k, :, CH_BLK * h : CH_BLK * (h + 1)] = part.astype(o_ref.dtype)
+            return carry
+
+        lax.fori_loop(0, o_ref.shape[0], one_row, 0)
+        start += o_ref.shape[0]
 
 
 def whiten_front(recording, tail_rows, fir_taps, kept_count, chunks, tile=512):
@@ -108,9 +115,14 @@
     windows = length // WIN
     toep = toeplitz(fir_taps)
     sections = lax.axis_size("tm")
-    basis = dft_table(WIN, NF, FLO).reshape(WIN, sections, chunks, NF // sections // chunks, 2)
-    basis = jnp.transpose(basis, (0, 2, 1, 3, 4)).reshape(WIN, 2 * NF)
+    bins_dev = NF // sections
+    basis = dft_table(WIN, NF, FLO).reshape(WIN, sections, bins_dev, 2)
+    basis = np.concatenate(
+        [basis[:, :, lo:hi].reshape(WIN, -1) for lo, hi in zip(chunks[:-1], chunks[1:])], axis=1
+    )
+    basis = jnp.asarray(basis)
     bins2 = basis.shape[1]
+    rows = [sections * (hi - lo) * 2 for lo, hi in zip(chunks[:-1], chunks[1:])]
     grid_spec = pltpu.PrefetchScalarGridSpec(
         num_scalar_prefetch=1,
         grid=(channels // tile,),
@@ -120,7 +132,7 @@
             pl.BlockSpec(toep.shape, lambda i, c: (0, 0)),
             pl.BlockSpec(basis.shape, lambda i, c: (0, 0)),
         ],
-        out_specs=pl.BlockSpec((bins2, windows, tile), lambda i, c: (0, 0, i)),
+        out_specs=[pl.BlockSpec((r, windows, tile), lambda i, c: (0, 0, i)) for r in rows],
         scratch_shapes=[
             pltpu.VMEM((tile // CH_BLK, windows * bins2, CH_BLK), jnp.float32),
             pltpu.VMEM((windows, tile), jnp.float32),
@@ -130,7 +142,7 @@
     return pl.pallas_call(
         front_kernel,
         grid_spec=grid_spec,
-        out_shape=jax.ShapeDtypeStruct((bins2, windows, channels), jnp.bfloat16),
+        out_shape=[jax.ShapeDtypeStruct((r, windows, channels), jnp.bfloat16) for r in rows],
         compiler_params=pltpu.CompilerParams(
             dimension_semantics=("arbitrary",), vmem_limit_bytes=48 * 1024 * 1024
         ),
@@ -168,7 +180,7 @@
     lax.fori_loop(0, bins, one_bin, 0, unroll=True)
 
 
-def stack_pairs(gathered, pair_blocks, kept_windows, half, chunk, chunks, previous=None):
+def stack_pairs(gathered, pair_blocks, kept_windows, half, chunk, all_bins, previous=None):
     halves, segs, bins, two, wins, chans = gathered.shape
     blocks_per_half = chans // CH_BLK
     npairs = pair_blocks.shape[0]
@@ -203,7 +215,7 @@
     return pl.pallas_call(
         stack_kernel,
         grid_spec=grid_spec,
-        out_shape=jax.ShapeDtypeStruct((npairs, bins * chunks, 2, CH_BLK, CH_BLK), jnp.float32),
+        out_shape=jax.ShapeDtypeStruct((npairs, all_bins, 2, CH_BLK, CH_BLK), jnp.float32),
         input_output_aliases=aliases,
         compiler_params=pltpu.CompilerParams(
             dimension_semantics=("arbitrary",), vmem_limit_bytes=48 * 1024 * 1024
@@ -214,7 +226,7 @@
     )(*operands)
 
 
-def per_device(recording, fir_taps, kept_windows, pair_blocks, chunks=2):
+def per_device(recording, fir_taps, kept_windows, pair_blocks):
     channels, length = recording.shape
     width = fir_taps.shape[0]
     sections = lax.axis_size("tm")
@@ -223,15 +235,18 @@
     segment = lax.axis_index("tm")
     kept_count = lax.dynamic_slice_in_dim(kept_windows, segment, 1, 0)
     bins_dev = NF // sections
-    chunks = math.gcd(chunks, bins_dev)
+    small = max(bins_dev // 4, 1)
+    chunks = [0, bins_dev - small, bins_dev] if bins_dev > 1 else [0, bins_dev]
     whitened = whiten_front(recording, tail_rows, fir_taps, kept_count, chunks)
-    outgoing = whitened.reshape(chunks, sections, bins_dev // chunks, 2, windows_dev, channels)
     half = jnp.zeros((1,), jnp.int32)
     result = None
-    for h in range(chunks):
-        by_freq = lax.all_to_all(outgoing[h], "tm", split_axis=0, concat_axis=0, tiled=True)
+    for lo, hi, part in zip(chunks[:-1], chunks[1:], whitened):
+        outgoing = part.reshape(sections, hi - lo, 2, windows_dev, channels)
+        by_freq = lax.all_to_all(outgoing, "tm", split_axis=0, concat_axis=0, tiled=True)
         gathered = lax.all_gather(by_freq, "pair", axis=0, tiled=False)
-        result = stack_pairs(gathered, pair_blocks, kept_windows, half, h, chunks, result)
+        result = stack_pairs(
+            gathered, pair_blocks, kept_windows, half, lo // (hi - lo), bins_dev, result
+        )
     return result
 
 

time: 175 us -> 174 us (level)
  Pallas kernels: 35.8 us -> 40.3 us
  local copies, waits for them, and re-layouts: 8.66 us -> 6.55 us
  waiting for transfers between devices: 4.47 us -> 2.51 us
    pallas_call x2, Pallas kernels: 14.7 us -> 19.1 us  [stack_pairs(): pl.pallas_call(stack_kernel, grid_spec=grid_spec, out_shape=jax.ShapeDtyp...]
    all_gather x2, waiting for transfers between devices: 3.12 us -> 0.01 us  [per_device(): gathered = lax.all_gather(by_freq, 'pair', axis=0, tiled=False)]
    unnamed x9, local copies, waits for them, and re-layouts: 4.46 us -> 2.63 us
  transfers between devices with their start and end apart: 3 -> 3, of which waited for: 2 -> 1; matrix products, arithmetic and copies ran while one was open for 2% -> 2% of each run, Pallas kernels for 4% -> 8%
where the time goes in v6:
time: 174 us; the launch traced here: 173 us
  blocking collectives  105 us (60%)
  Pallas kernels  40.3 us (23%)
  between operations  13.5 us (8%)
  local copies, waits for them, and re-layouts  6.55 us (4%)
  starting transfers between devices  4.93 us (3%)
  waiting for transfers between devices  2.51 us (1%)
    all_to_all x2, blocking collectives, per_device(): lax.all_to_all(outgoing, 'tm', split_axis=0, concat_axis=0, tiled=True)  105 us
    pallas_call x1, Pallas kernels, whiten_front(): pl.pallas_call(front_kernel, grid_spec=grid_spec, out_shape=[jax.ShapeDty...  21.2 us
    pallas_call x2, Pallas kernels, stack_pairs(): pl.pallas_call(stack_kernel, grid_spec=grid_spec, out_shape=jax.ShapeDtyp...  19.1 us
    ppermute x1, starting transfers between devices, from_behind(): return lax.ppermute(array, axis, pairs)  4.89 us
  transfers between devices with their start and end apart: 3, of which 1 were waited for; matrix products, arithmetic and copies ran while one was open for 2% of the time, Pallas kernels for 8%

profile of v6, /device:TPU:0, one launch (start us, length us, event | category | flops | bytes accessed | tf_op | source)
XLA Modules:
  0.0 173.2 jit_solution(16051458092160032254)
XLA Ops:
  6.5 0.0 all-gather.7.cloned.1.call-start
  6.5 1.0 slice.6
  7.5 4.9 %collective-permute-start = (bf16[512,256]{1,0:T(8,128)(2,1)S(1)}, bf16[512,256]{1,0:T(8,128)(2,1)S(1)}, u32[]{:S(2)}, u32[]{:S(2)}) collective-permute-start(bf16[512,256]{1,0:T(8,128)(2,1)S(1)} %slice.6), channel_id=1, source_target_pairs={{0,2},{2,4},{4,6},{6,8},{8,10},{10,12},{12,14},{1,3},{3,5},{5,7},{... | collective-permute-start | bytes 786440 | tf_op jit(solution)/shard_map/ppermute | solution.py:25
  12.4 0.7 rev.3
  13.2 0.1 pad_maximum_fusion
  13.3 0.6 tile.10
  13.9 0.2 reshape.10
  14.1 0.1 copy.12
  14.2 1.2 dynamic_slice.3.cnt_ref
  15.5 2.5 %collective-permute-done.tail_ref = bf16[512,256]{1,0:T(8,128)(2,1)S(1)} collective-permute-done((bf16[512,256]{1,0:T(8,128)(2,1)S(1)}, bf16[512,256]{1,0:T(8,128)(2,1)S(1)}, u32[]{:S(2)}, u32[]{:S(2)}) %collective-permute-start) | collective-permute-done | bytes 262176 | tf_op jit(solution)/shard_map/ppermute | solution.py:25
  17.9 0.0 copy-start.2
  17.9 0.9 copy-done.2
  18.9 21.2 %shard_map.55 = (bf16[192,16,512]{2,1,0:T(8,128)(2,1)S(1)}, bf16[64,16,512]{2,1,0:T(8,128)(2,1)S(1)}) custom-call(s32[1]{0:T(128)} %dynamic_slice.3.cnt_ref, bf16[512,8192]{1,0:T(8,128)(2,1)} %rec_ref.1, bf16[512,256]{1,0:T(8,128)(2,1)S(1)} %collective-permute-done.tail_ref, bf16[512,256]{1,0:T(8,128)(2,1)S(1)} %bitcast.9, bf16[512,256]{1,0:T(8,128)(2,1)S(1)} %copy-done.2), custom_call_target="tpu_custom_call" | custom-call | flops 12884901888 | bytes 12582912 | tf_op jit(solution)/shard_map/pallas_call | solution.py:142
  40.1 0.0 copy-start.3
  40.1 0.0 copy-start.1
  40.1 76.7 %all_to_all.10 = bf16[8,12,2,16,512]{4,3,2,1,0:T(8,128)(2,1)} all-to-all(bf16[8,12,2,16,512]{4,3,2,1,0:T(8,128)(2,1)S(1)} %bitcast.7), channel_id=1, replica_groups=mesh['groups'=2,'tm'=8,'pair'=2] {'tm'}, dimensions={0} | all-to-all | bytes 6291456 | tf_op jit(solution)/shard_map/all_to_all | solution.py:245
  116.8 0.0 all-gather.7.cloned.1.call-update
  116.8 0.0 all-gather.5.cloned.1.call-start
  116.9 28.7 %all_to_all.11 = bf16[8,4,2,16,512]{4,3,2,1,0:T(8,128)(2,1)} all-to-all(bf16[8,4,2,16,512]{4,3,2,1,0:T(8,128)(2,1)S(1)} %bitcast.8), channel_id=1, replica_groups=mesh['groups'=2,'tm'=8,'pair'=2] {'tm'}, dimensions={0} | all-to-all | bytes 2097152 | tf_op jit(solution)/shard_map/all_to_all | solution.py:245
  145.6 0.0 all-gather.5.cloned.1.call-update
  145.6 0.0 copy-done.3
  145.6 0.1 copy.14.pb_ref
  145.7 0.0 all-gather.7.cloned.1.call-done
  145.7 0.0 copy-done.1
  145.7 13.2 %shard_map.56.rest_0_ = f32[8,16,2,128,128]{4,3,2,1,0:T(8,128)} custom-call(s32[8,2]{1,0:T(8,128)S(1)} %copy.14.pb_ref, s32[8]{0:T(128)S(1)} %copy-done.1, s32[1]{0:T(128)} %constant.3.clone.1.q_ref, bf16[2,8,12,2,16,512]{5,4,3,2,1,0:T(8,128)(2,1)} %bitcast.10, bf16[2,8,12,2,16,512]{5,4,3,2,1,0:T(8,128)(2,1)} %bitcast.11), custom_call_target="tpu_custom_call" | custom-call | flops 1610612736 | bytes 25165824 | tf_op jit(solution)/shard_map/pallas_call | solution.py:215
  158.8 0.0 all-gather.5.cloned.1.call-done
  158.8 0.0 copy-start
  158.9 1.6 copy-done
  160.4 5.9 %shard_map.57 = f32[8,16,2,128,128]{4,3,2,1,0:T(8,128)} custom-call(s32[8,2]{1,0:T(8,128)S(1)} %copy.14.pb_ref, s32[8]{0:T(128)S(1)} %copy-done.1, s32[1]{0:T(128)} %constant.3.clone.1.q_ref, bf16[2,8,4,2,16,512]{5,4,3,2,1,0:T(8,128)(2,1)S(1)} %bitcast.5, bf16[2,8,4,2,16,512]{5,4,3,2,1,0:T(8,128)(2,1)S(1)} %bitcast.6, ...), custom_call_target="tpu_custom_call", output_to_operand_aliasing={{}: (5, {})} | custom-call | flops 536870912 | bytes 8388608 | tf_op jit(solution)/shard_map/pallas_call | solution.py:215
  (3 shorter events, 0.1 us)
Async XLA Ops:
  6.5 139.1 %all-gather.7.cloned.1.call-start = ((), (), s32[]{:S(2)}) async-start(), calls=%async_computation.3 | async-start | bytes 9437184 | tf_op jit(solution)/shard_map/all_gather | solution.py:246
  7.5 10.4 %collective-permute-start = (bf16[512,256]{1,0:T(8,128)(2,1)S(1)}, bf16[512,256]{1,0:T(8,128)(2,1)S(1)}, u32[]{:S(2)}, u32[]{:S(2)}) collective-permute-start(bf16[512,256]{1,0:T(8,128)(2,1)S(1)} %slice.6), channel_id=1, source_target_pairs={{0,2},{2,4},{4,6},{6,8},{8,10},{10,12},{12,14},{1,3},{3,5},{5,7},{... | collective-permute-start | bytes 786440 | tf_op jit(solution)/shard_map/ppermute | solution.py:25
  17.9 0.9 copy-start.2
  40.1 105.5 %copy-start.3 = (s32[8,2]{0,1:T(2,128)S(1)}, s32[8,2]{0,1:T(2,128)}, u32[]{:S(2)}) copy-start(s32[8,2]{0,1:T(2,128)} %param.8) | copy-start | bytes 196
  40.1 105.6 %copy-start.1 = (s32[8]{0:T(128)S(1)}, s32[8]{0:T(128)}, u32[]{:S(2)}) copy-start(s32[8]{0:T(128)} %kw_ref.3) | copy-start | bytes 100
  116.8 42.0 %all-gather.5.cloned.1.call-start = ((), (), s32[]{:S(2)}) async-start(), calls=%async_computation.2 | async-start | bytes 3145728 | tf_op jit(solution)/shard_map/all_gather | solution.py:246
  158.8 1.6 copy-start
Sparse Core Ops, SparseCore 0:
  116.9 15.6 all-gather.6
  145.7 9.5 all-gather.4

commit v7 on v6

--- a/solution.py
+++ b/solution.py
@@ -68,26 +68,20 @@
     return basis_table.reshape(length, 2 * bins).astype(ml_dtypes.bfloat16)
 
 
-def front_kernel(cnt_ref, rec_ref, tail_ref, toep_ref, basis_ref, *rest):
+def front_kernel(cnt_ref, rec_ref, tail_ref, g_ref, *rest):
     outs, (scr_ref, inv_ref) = rest[:-2], rest[-2:]
     tile, length = rec_ref.shape
     width = tail_ref.shape[1]
-    bins2 = basis_ref.shape[1]
+    bins2 = g_ref.shape[1]
     windows = length // WIN
-    toep = toep_ref[...]
-    basis = basis_ref[...]
+    response = g_ref[...]
     count = cnt_ref[0]
     for w in range(windows):
         if w == 0:
-            ext0 = jnp.concatenate([tail_ref[...], rec_ref[:, 0:width]], axis=1)
+            ext = jnp.concatenate([tail_ref[...], rec_ref[:, 0:WIN]], axis=1)
         else:
-            ext0 = rec_ref[:, WIN * w - width : WIN * w + width]
-        ext1 = rec_ref[:, WIN * w : WIN * w + 2 * width]
-        f0 = jnp.dot(ext0, toep, preferred_element_type=jnp.float32).astype(jnp.bfloat16)
-        f1 = jnp.dot(ext1, toep, preferred_element_type=jnp.float32).astype(jnp.bfloat16)
-        spec = jnp.dot(
-            jnp.concatenate([f0, f1], axis=1), basis, preferred_element_type=jnp.float32
-        ).T
+            ext = rec_ref[:, WIN * w - width : WIN * w + WIN]
+        spec = jnp.dot(ext, response, preferred_element_type=jnp.float32).T
         for h in range(tile // CH_BLK):
             scr_ref[h, pl.ds(bins2 * w, bins2), :] = spec[:, CH_BLK * h : CH_BLK * (h + 1)]
         power = jnp.sum(spec * spec, axis=0, keepdims=True) * (1.0 / bins2)
@@ -122,6 +116,14 @@
     )
     basis = jnp.asarray(basis)
     bins2 = basis.shape[1]
+    blocks = [
+        jnp.dot(toep, basis[i * width : (i + 1) * width], preferred_element_type=jnp.float32)
+        for i in range(WIN // width)
+    ]
+    response = jnp.zeros((WIN + width, bins2), jnp.float32)
+    for i, part in enumerate(blocks):
+        response = response.at[i * width : i * width + 2 * width].add(part)
+    response = response.astype(jnp.bfloat16)
     rows = [sections * (hi - lo) * 2 for lo, hi in zip(chunks[:-1], chunks[1:])]
     grid_spec = pltpu.PrefetchScalarGridSpec(
         num_scalar_prefetch=1,
@@ -129,8 +131,7 @@
         in_specs=[
             pl.BlockSpec((tile, length), lambda i, c: (i, 0)),
             pl.BlockSpec((tile, width), lambda i, c: (i, 0)),
-            pl.BlockSpec(toep.shape, lambda i, c: (0, 0)),
-            pl.BlockSpec(basis.shape, lambda i, c: (0, 0)),
+            pl.BlockSpec(response.shape, lambda i, c: (0, 0)),
         ],
         out_specs=[pl.BlockSpec((r, windows, tile), lambda i, c: (0, 0, i)) for r in rows],
         scratch_shapes=[
@@ -138,7 +139,7 @@
             pltpu.VMEM((windows, tile), jnp.float32),
         ],
     )
-    flops = 2 * channels * windows * 3 * (2 * width) * bins2 * 2
+    flops = 2 * channels * windows * (WIN + width) * bins2
     return pl.pallas_call(
         front_kernel,
         grid_spec=grid_spec,
@@ -151,7 +152,7 @@
             bytes_accessed=channels * length * 2 + bins2 * windows * channels * 2,
             transcendentals=channels * windows,
         ),
-    )(kept_count, recording, tail_rows, toep, basis)
+    )(kept_count, recording, tail_rows, response)
 
 
 def stack_kernel(pb_ref, kw_ref, q_ref, a_ref, b_ref, *rest):

time: 174 us -> 169 us (0.971)
  Pallas kernels: 40.3 us -> 36.7 us
  matrix products: 0 us -> 2.35 us
    pallas_call x1, Pallas kernels: 21.2 us -> 17.9 us  [whiten_front(): pl.pallas_call(front_kernel, grid_spec=grid_spec, out_shape=[jax.ShapeDty...]
    dot_general x0 -> x2, matrix products: none -> 2.35 us  [whiten_front(): jnp.dot(toep, basis[i * width:(i + 1) * width], preferred_element_type=jn...]
  transfers between devices with their start and end apart: 3 -> 3, of which waited for: 1 -> 1; matrix products, arithmetic and copies ran while one was open for 2% -> 3% of each run, Pallas kernels for 8% -> 8%
where the time goes in v7:
time: 169 us
  blocking collectives  105 us (62%)
  Pallas kernels  36.7 us (22%)
  between operations  13.5 us (8%)
  starting transfers between devices  4.93 us (3%)
  local copies, waits for them, and re-layouts  4.88 us (3%)
  matrix products  2.35 us (1%)
    all_to_all x2, blocking collectives, per_device(): lax.all_to_all(outgoing, 'tm', split_axis=0, concat_axis=0, tiled=True)  105 us
    pallas_call x2, Pallas kernels, stack_pairs(): pl.pallas_call(stack_kernel, grid_spec=grid_spec, out_shape=jax.ShapeDtyp...  18.8 us
    pallas_call x1, Pallas kernels, whiten_front(): pl.pallas_call(front_kernel, grid_spec=grid_spec, out_shape=[jax.ShapeDty...  17.9 us
    ppermute x1, starting transfers between devices, from_behind(): return lax.ppermute(array, axis, pairs)  4.89 us
  transfers between devices with their start and end apart: 3, of which 1 were waited for; matrix products, arithmetic and copies ran while one was open for 3% of the time, Pallas kernels for 8%

profile of v7, /device:TPU:0, one launch (start us, length us, event | category | flops | bytes accessed | tf_op | source)
XLA Modules:
  0.0 168.6 jit_solution(3884319564470563064)
XLA Ops:
  6.5 0.0 copy-start.1
  6.5 0.0 all-gather.7.cloned.1.call-start
  6.5 1.0 slice.47
  7.5 4.9 %collective-permute-start = (bf16[512,256]{1,0:T(8,128)(2,1)S(1)}, bf16[512,256]{1,0:T(8,128)(2,1)S(1)}, u32[]{:S(2)}, u32[]{:S(2)}) collective-permute-start(bf16[512,256]{1,0:T(8,128)(2,1)S(1)} %slice.47), channel_id=1, source_target_pairs={{0,2},{2,4},{4,6},{6,8},{8,10},{10,12},{12,14},{1,3},{3,5},{5,7},{... | collective-permute-start | bytes 786440 | tf_op jit(solution)/shard_map/ppermute | solution.py:25
  12.4 0.7 rev.3
  13.2 0.1 pad_maximum_fusion
  13.3 0.6 tile.10
  13.9 0.2 reshape.59
  14.1 1.2 fusion.1
  15.3 0.1 scatter-add.6
  15.3 1.2 fusion
  16.6 0.0 copy-done.1
  16.6 0.6 dynamic_slice.3.cnt_ref
  17.2 0.8 collective-permute-done.tail_ref
  17.9 17.9 %shard_map.55 = (bf16[192,16,512]{2,1,0:T(8,128)(2,1)S(1)}, bf16[64,16,512]{2,1,0:T(8,128)(2,1)S(1)}) custom-call(s32[1]{0:T(128)} %dynamic_slice.3.cnt_ref, bf16[512,8192]{1,0:T(8,128)(2,1)} %rec_ref.1, bf16[512,256]{1,0:T(8,128)(2,1)S(1)} %collective-permute-done.tail_ref, bf16[768,256]{1,0:T(8,128)(2,1)S(1)} %convert_element_type.3.g_ref), custom_call_target="tpu_custom_call" | custom-call | flops 3221225472 | bytes 12582912 | tf_op jit(solution)/shard_map/pallas_call | solution.py:143
  35.9 0.0 copy-start.2
  35.9 76.7 %all_to_all.10 = bf16[8,12,2,16,512]{4,3,2,1,0:T(8,128)(2,1)} all-to-all(bf16[8,12,2,16,512]{4,3,2,1,0:T(8,128)(2,1)S(1)} %bitcast.10), channel_id=1, replica_groups=mesh['groups'=2,'tm'=8,'pair'=2] {'tm'}, dimensions={0} | all-to-all | bytes 6291456 | tf_op jit(solution)/shard_map/all_to_all | solution.py:246
  112.6 0.0 all-gather.7.cloned.1.call-update
  112.6 0.0 all-gather.5.cloned.1.call-start
  112.6 28.7 %all_to_all.11 = bf16[8,4,2,16,512]{4,3,2,1,0:T(8,128)(2,1)} all-to-all(bf16[8,4,2,16,512]{4,3,2,1,0:T(8,128)(2,1)S(1)} %bitcast.11), channel_id=1, replica_groups=mesh['groups'=2,'tm'=8,'pair'=2] {'tm'}, dimensions={0} | all-to-all | bytes 2097152 | tf_op jit(solution)/shard_map/all_to_all | solution.py:246
  141.3 0.0 all-gather.5.cloned.1.call-update
  141.3 0.0 copy-done.2
  141.4 0.1 copy.12.pb_ref
  141.4 0.0 all-gather.7.cloned.1.call-done
  141.4 12.9 %shard_map.56.rest_0_ = f32[8,16,2,128,128]{4,3,2,1,0:T(8,128)} custom-call(s32[8,2]{1,0:T(8,128)S(1)} %copy.12.pb_ref, s32[8]{0:T(128)S(1)} %copy-done.1, s32[1]{0:T(128)} %constant.64.clone.1.q_ref, bf16[2,8,12,2,16,512]{5,4,3,2,1,0:T(8,128)(2,1)} %bitcast.12, bf16[2,8,12,2,16,512]{5,4,3,2,1,0:T(8,128)(2,1)} %bitcast.13), custom_call_target="tpu_custom_call" | custom-call | flops 1610612736 | bytes 25165824 | tf_op jit(solution)/shard_map/pallas_call | solution.py:216
  154.4 0.0 all-gather.5.cloned.1.call-done
  154.4 0.0 copy-start
  154.4 1.6 copy-done
  156.0 5.8 %shard_map.57 = f32[8,16,2,128,128]{4,3,2,1,0:T(8,128)} custom-call(s32[8,2]{1,0:T(8,128)S(1)} %copy.12.pb_ref, s32[8]{0:T(128)S(1)} %copy-done.1, s32[1]{0:T(128)} %constant.64.clone.1.q_ref, bf16[2,8,4,2,16,512]{5,4,3,2,1,0:T(8,128)(2,1)S(1)} %bitcast.8, bf16[2,8,4,2,16,512]{5,4,3,2,1,0:T(8,128)(2,1)S(1)} %bitcast.9, ...), custom_call_target="tpu_custom_call", output_to_operand_aliasing={{}: (5, {})} | custom-call | flops 536870912 | bytes 8388608 | tf_op jit(solution)/shard_map/pallas_call | solution.py:216
  (4 shorter events, 0.1 us)
Async XLA Ops:
  6.5 10.0 %copy-start.1 = (s32[8]{0:T(128)S(1)}, s32[8]{0:T(128)}, u32[]{:S(2)}) copy-start(s32[8]{0:T(128)} %kw_ref.3) | copy-start | bytes 100
  6.5 134.9 %all-gather.7.cloned.1.call-start = ((), (), s32[]{:S(2)}) async-start(), calls=%async_computation.3 | async-start | bytes 9437184 | tf_op jit(solution)/shard_map/all_gather | solution.py:247
  7.5 10.4 %collective-permute-start = (bf16[512,256]{1,0:T(8,128)(2,1)S(1)}, bf16[512,256]{1,0:T(8,128)(2,1)S(1)}, u32[]{:S(2)}, u32[]{:S(2)}) collective-permute-start(bf16[512,256]{1,0:T(8,128)(2,1)S(1)} %slice.47), channel_id=1, source_target_pairs={{0,2},{2,4},{4,6},{6,8},{8,10},{10,12},{12,14},{1,3},{3,5},{5,7},{... | collective-permute-start | bytes 786440 | tf_op jit(solution)/shard_map/ppermute | solution.py:25
  35.9 105.5 %copy-start.2 = (s32[8,2]{0,1:T(2,128)S(1)}, s32[8,2]{0,1:T(2,128)}, u32[]{:S(2)}) copy-start(s32[8,2]{0,1:T(2,128)} %param.12) | copy-start | bytes 196
  112.6 41.8 %all-gather.5.cloned.1.call-start = ((), (), s32[]{:S(2)}) async-start(), calls=%async_computation.2 | async-start | bytes 3145728 | tf_op jit(solution)/shard_map/all_gather | solution.py:247
  154.4 1.6 copy-start
Sparse Core Ops, SparseCore 0:
  112.7 15.6 all-gather.6
  141.5 9.5 all-gather.4

commit v8 on v6

--- a/solution.py
+++ b/solution.py
@@ -105,7 +105,7 @@
                 o_ref[k, :, CH_BLK * h : CH_BLK * (h + 1)] = part.astype(o_ref.dtype)
             return carry
 
-        lax.fori_loop(0, o_ref.shape[0], one_row, 0)
+        lax.fori_loop(0, o_ref.shape[0], one_row, 0, unroll=8)
         start += o_ref.shape[0]
 
 

time: 174 us -> 169 us (0.971)
  Pallas kernels: 40.3 us -> 35.9 us
    pallas_call x1, Pallas kernels: 21.2 us -> 16.9 us  [whiten_front(): pl.pallas_call(front_kernel, grid_spec=grid_spec, out_shape=[jax.ShapeDty...]
where the time goes in v8:
time: 169 us
  blocking collectives  105 us (62%)
  Pallas kernels  35.9 us (21%)
  between operations  13.5 us (8%)
  local copies, waits for them, and re-layouts  6.55 us (4%)
  starting transfers between devices  4.93 us (3%)
  waiting for transfers between devices  2.51 us (1%)
    all_to_all x2, blocking collectives, per_device(): lax.all_to_all(outgoing, 'tm', split_axis=0, concat_axis=0, tiled=True)  105 us
    pallas_call x2, Pallas kernels, stack_pairs(): pl.pallas_call(stack_kernel, grid_spec=grid_spec, out_shape=jax.ShapeDtyp...  19.1 us
    pallas_call x1, Pallas kernels, whiten_front(): pl.pallas_call(front_kernel, grid_spec=grid_spec, out_shape=[jax.ShapeDty...  16.9 us
    ppermute x1, starting transfers between devices, from_behind(): return lax.ppermute(array, axis, pairs)  4.89 us
  transfers between devices with their start and end apart: 3, of which 1 were waited for; matrix products, arithmetic and copies ran while one was open for 2% of the time, Pallas kernels for 8%

profile of v8, /device:TPU:0, one launch (start us, length us, event | category | flops | bytes accessed | tf_op | source)
XLA Modules:
  0.0 168.8 jit_solution(15164641582743346776)
XLA Ops:
  6.5 0.0 all-gather.7.cloned.1.call-start
  6.5 1.0 slice.6
  7.5 4.9 %collective-permute-start = (bf16[512,256]{1,0:T(8,128)(2,1)S(1)}, bf16[512,256]{1,0:T(8,128)(2,1)S(1)}, u32[]{:S(2)}, u32[]{:S(2)}) collective-permute-start(bf16[512,256]{1,0:T(8,128)(2,1)S(1)} %slice.6), channel_id=1, source_target_pairs={{0,2},{2,4},{4,6},{6,8},{8,10},{10,12},{12,14},{1,3},{3,5},{5,7},{... | collective-permute-start | bytes 786440 | tf_op jit(solution)/shard_map/ppermute | solution.py:25
  12.4 0.7 rev.3
  13.2 0.1 pad_maximum_fusion
  13.3 0.6 tile.10
  13.9 0.2 reshape.10
  14.1 0.1 copy.12
  14.2 1.2 dynamic_slice.3.cnt_ref
  15.5 2.5 %collective-permute-done.tail_ref = bf16[512,256]{1,0:T(8,128)(2,1)S(1)} collective-permute-done((bf16[512,256]{1,0:T(8,128)(2,1)S(1)}, bf16[512,256]{1,0:T(8,128)(2,1)S(1)}, u32[]{:S(2)}, u32[]{:S(2)}) %collective-permute-start) | collective-permute-done | bytes 262176 | tf_op jit(solution)/shard_map/ppermute | solution.py:25
  17.9 0.0 copy-start.2
  17.9 0.9 copy-done.2
  18.9 16.9 %shard_map.55 = (bf16[192,16,512]{2,1,0:T(8,128)(2,1)S(1)}, bf16[64,16,512]{2,1,0:T(8,128)(2,1)S(1)}) custom-call(s32[1]{0:T(128)} %dynamic_slice.3.cnt_ref, bf16[512,8192]{1,0:T(8,128)(2,1)} %rec_ref.1, bf16[512,256]{1,0:T(8,128)(2,1)S(1)} %collective-permute-done.tail_ref, bf16[512,256]{1,0:T(8,128)(2,1)S(1)} %bitcast.9, bf16[512,256]{1,0:T(8,128)(2,1)S(1)} %copy-done.2), custom_call_target="tpu_custom_call" | custom-call | flops 12884901888 | bytes 12582912 | tf_op jit(solution)/shard_map/pallas_call | solution.py:142
  35.8 0.0 copy-start.3
  35.8 0.0 copy-start.1
  35.8 76.7 %all_to_all.10 = bf16[8,12,2,16,512]{4,3,2,1,0:T(8,128)(2,1)} all-to-all(bf16[8,12,2,16,512]{4,3,2,1,0:T(8,128)(2,1)S(1)} %bitcast.7), channel_id=1, replica_groups=mesh['groups'=2,'tm'=8,'pair'=2] {'tm'}, dimensions={0} | all-to-all | bytes 6291456 | tf_op jit(solution)/shard_map/all_to_all | solution.py:245
  112.4 0.0 all-gather.7.cloned.1.call-update
  112.5 0.0 all-gather.5.cloned.1.call-start
  112.5 28.7 %all_to_all.11 = bf16[8,4,2,16,512]{4,3,2,1,0:T(8,128)(2,1)} all-to-all(bf16[8,4,2,16,512]{4,3,2,1,0:T(8,128)(2,1)S(1)} %bitcast.8), channel_id=1, replica_groups=mesh['groups'=2,'tm'=8,'pair'=2] {'tm'}, dimensions={0} | all-to-all | bytes 2097152 | tf_op jit(solution)/shard_map/all_to_all | solution.py:245
  141.2 0.0 all-gather.5.cloned.1.call-update
  141.2 0.0 copy-done.3
  141.2 0.1 copy.14.pb_ref
  141.3 0.0 all-gather.7.cloned.1.call-done
  141.3 0.0 copy-done.1
  141.3 13.2 %shard_map.56.rest_0_ = f32[8,16,2,128,128]{4,3,2,1,0:T(8,128)} custom-call(s32[8,2]{1,0:T(8,128)S(1)} %copy.14.pb_ref, s32[8]{0:T(128)S(1)} %copy-done.1, s32[1]{0:T(128)} %constant.3.clone.1.q_ref, bf16[2,8,12,2,16,512]{5,4,3,2,1,0:T(8,128)(2,1)} %bitcast.10, bf16[2,8,12,2,16,512]{5,4,3,2,1,0:T(8,128)(2,1)} %bitcast.11), custom_call_target="tpu_custom_call" | custom-call | flops 1610612736 | bytes 25165824 | tf_op jit(solution)/shard_map/pallas_call | solution.py:215
  154.6 0.0 all-gather.5.cloned.1.call-done
  154.6 0.0 copy-start
  154.6 1.6 copy-done
  156.2 5.8 %shard_map.57 = f32[8,16,2,128,128]{4,3,2,1,0:T(8,128)} custom-call(s32[8,2]{1,0:T(8,128)S(1)} %copy.14.pb_ref, s32[8]{0:T(128)S(1)} %copy-done.1, s32[1]{0:T(128)} %constant.3.clone.1.q_ref, bf16[2,8,4,2,16,512]{5,4,3,2,1,0:T(8,128)(2,1)S(1)} %bitcast.5, bf16[2,8,4,2,16,512]{5,4,3,2,1,0:T(8,128)(2,1)S(1)} %bitcast.6, ...), custom_call_target="tpu_custom_call", output_to_operand_aliasing={{}: (5, {})} | custom-call | flops 536870912 | bytes 8388608 | tf_op jit(solution)/shard_map/pallas_call | solution.py:215
  (3 shorter events, 0.1 us)
Async XLA Ops:
  6.5 134.8 %all-gather.7.cloned.1.call-start = ((), (), s32[]{:S(2)}) async-start(), calls=%async_computation.3 | async-start | bytes 9437184 | tf_op jit(solution)/shard_map/all_gather | solution.py:246
  7.5 10.4 %collective-permute-start = (bf16[512,256]{1,0:T(8,128)(2,1)S(1)}, bf16[512,256]{1,0:T(8,128)(2,1)S(1)}, u32[]{:S(2)}, u32[]{:S(2)}) collective-permute-start(bf16[512,256]{1,0:T(8,128)(2,1)S(1)} %slice.6), channel_id=1, source_target_pairs={{0,2},{2,4},{4,6},{6,8},{8,10},{10,12},{12,14},{1,3},{3,5},{5,7},{... | collective-permute-start | bytes 786440 | tf_op jit(solution)/shard_map/ppermute | solution.py:25
  17.9 0.9 copy-start.2
  35.8 105.5 %copy-start.3 = (s32[8,2]{0,1:T(2,128)S(1)}, s32[8,2]{0,1:T(2,128)}, u32[]{:S(2)}) copy-start(s32[8,2]{0,1:T(2,128)} %param.8) | copy-start | bytes 196
  35.8 105.6 %copy-start.1 = (s32[8]{0:T(128)S(1)}, s32[8]{0:T(128)}, u32[]{:S(2)}) copy-start(s32[8]{0:T(128)} %kw_ref.3) | copy-start | bytes 100
  112.5 42.1 %all-gather.5.cloned.1.call-start = ((), (), s32[]{:S(2)}) async-start(), calls=%async_computation.2 | async-start | bytes 3145728 | tf_op jit(solution)/shard_map/all_gather | solution.py:246
  154.6 1.6 copy-start
Sparse Core Ops, SparseCore 0:
  112.6 15.6 all-gather.6
  141.4 9.5 all-gather.4

commit v9 on v8

--- a/solution.py
+++ b/solution.py
@@ -76,7 +76,7 @@
     windows = length // WIN
     toep = toep_ref[...]
     basis = basis_ref[...]
-    count = cnt_ref[0]
+    count = cnt_ref[lax.axis_index("tm")]
     for w in range(windows):
         if w == 0:
             ext0 = jnp.concatenate([tail_ref[...], rec_ref[:, 0:width]], axis=1)
@@ -105,7 +105,7 @@
                 o_ref[k, :, CH_BLK * h : CH_BLK * (h + 1)] = part.astype(o_ref.dtype)
             return carry
 
-        lax.fori_loop(0, o_ref.shape[0], one_row, 0, unroll=8)
+        lax.fori_loop(0, o_ref.shape[0], one_row, 0, unroll=16)
         start += o_ref.shape[0]
 
 
@@ -232,12 +232,10 @@
     sections = lax.axis_size("tm")
     tail_rows = from_behind(recording[:, length - width :], "tm", 1)
     windows_dev = length // WIN
-    segment = lax.axis_index("tm")
-    kept_count = lax.dynamic_slice_in_dim(kept_windows, segment, 1, 0)
     bins_dev = NF // sections
     small = max(bins_dev // 4, 1)
     chunks = [0, bins_dev - small, bins_dev] if bins_dev > 1 else [0, bins_dev]
-    whitened = whiten_front(recording, tail_rows, fir_taps, kept_count, chunks)
+    whitened = whiten_front(recording, tail_rows, fir_taps, kept_windows, chunks)
     half = jnp.zeros((1,), jnp.int32)
     result = None
     for lo, hi, part in zip(chunks[:-1], chunks[1:], whitened):

time: 169 us -> 170 us (level)
  transfers between devices with their start and end apart: 3 -> 3, of which waited for: 1 -> 1; matrix products, arithmetic and copies ran while one was open for 2% -> 1% of each run, Pallas kernels for 8% -> 8%
where the time goes in v9:
time: 170 us; the launch traced here: 169 us
  blocking collectives  105 us (62%)
  Pallas kernels  35.6 us (21%)
  between operations  13.5 us (8%)
  local copies, waits for them, and re-layouts  5.97 us (4%)
  starting transfers between devices  4.93 us (3%)
  waiting for transfers between devices  3.75 us (2%)
    all_to_all x2, blocking collectives, per_device(): lax.all_to_all(outgoing, 'tm', split_axis=0, concat_axis=0, tiled=True)  105 us
    pallas_call x2, Pallas kernels, stack_pairs(): pl.pallas_call(stack_kernel, grid_spec=grid_spec, out_shape=jax.ShapeDtyp...  19.1 us
    pallas_call x1, Pallas kernels, whiten_front(): pl.pallas_call(front_kernel, grid_spec=grid_spec, out_shape=[jax.ShapeDty...  16.5 us
    ppermute x1, starting transfers between devices, from_behind(): return lax.ppermute(array, axis, pairs)  4.89 us
    ppermute x1, waiting for transfers between devices, from_behind(): return lax.ppermute(array, axis, pairs)  3.71 us
  transfers between devices with their start and end apart: 3, of which 1 were waited for; matrix products, arithmetic and copies ran while one was open for 1% of the time, Pallas kernels for 8%

profile of v9, /device:TPU:0, one launch (start us, length us, event | category | flops | bytes accessed | tf_op | source)
XLA Modules:
  0.0 169.2 jit_solution(15813218896393589879)
XLA Ops:
  6.5 0.0 all-gather.7.cloned.1.call-start
  6.5 1.0 slice.6
  7.5 4.9 %collective-permute-start = (bf16[512,256]{1,0:T(8,128)(2,1)S(1)}, bf16[512,256]{1,0:T(8,128)(2,1)S(1)}, u32[]{:S(2)}, u32[]{:S(2)}) collective-permute-start(bf16[512,256]{1,0:T(8,128)(2,1)S(1)} %slice.6), channel_id=1, source_target_pairs={{0,2},{2,4},{4,6},{6,8},{8,10},{10,12},{12,14},{1,3},{3,5},{5,7},{... | collective-permute-start | bytes 786440 | tf_op jit(solution)/shard_map/ppermute | solution.py:25
  12.4 0.7 rev.3
  13.2 0.1 pad_maximum_fusion
  13.3 0.6 tile.10
  13.9 0.2 reshape.10
  14.1 0.1 copy.12
  14.2 3.7 %collective-permute-done.tail_ref = bf16[512,256]{1,0:T(8,128)(2,1)S(1)} collective-permute-done((bf16[512,256]{1,0:T(8,128)(2,1)S(1)}, bf16[512,256]{1,0:T(8,128)(2,1)S(1)}, u32[]{:S(2)}, u32[]{:S(2)}) %collective-permute-start) | collective-permute-done | bytes 262176 | tf_op jit(solution)/shard_map/ppermute | solution.py:25
  17.9 0.0 copy-start.1
  17.9 0.7 copy-done.1
  18.6 0.0 copy-start.3
  18.6 0.9 copy-done.3
  19.5 16.5 %shard_map.55 = (bf16[192,16,512]{2,1,0:T(8,128)(2,1)S(1)}, bf16[64,16,512]{2,1,0:T(8,128)(2,1)S(1)}) custom-call(s32[8]{0:T(128)S(1)} %copy-done.1, bf16[512,8192]{1,0:T(8,128)(2,1)} %rec_ref.1, bf16[512,256]{1,0:T(8,128)(2,1)S(1)} %collective-permute-done.tail_ref, bf16[512,256]{1,0:T(8,128)(2,1)S(1)} %bitcast.9, bf16[512,256]{1,0:T(8,128)(2,1)S(1)} %copy-done.3), custom_call_target="tpu_custom_call" | custom-call | flops 12884901888 | bytes 12582912 | tf_op jit(solution)/shard_map/pallas_call | solution.py:142
  36.0 0.0 copy-start.4
  36.0 0.0 copy-start.2
  36.0 76.7 %all_to_all.10 = bf16[8,12,2,16,512]{4,3,2,1,0:T(8,128)(2,1)} all-to-all(bf16[8,12,2,16,512]{4,3,2,1,0:T(8,128)(2,1)S(1)} %bitcast.7), channel_id=1, replica_groups=mesh['groups'=2,'tm'=8,'pair'=2] {'tm'}, dimensions={0} | all-to-all | bytes 6291456 | tf_op jit(solution)/shard_map/all_to_all | solution.py:243
  112.7 0.0 all-gather.7.cloned.1.call-update
  112.7 0.0 all-gather.5.cloned.1.call-start
  112.8 28.7 %all_to_all.11 = bf16[8,4,2,16,512]{4,3,2,1,0:T(8,128)(2,1)} all-to-all(bf16[8,4,2,16,512]{4,3,2,1,0:T(8,128)(2,1)S(1)} %bitcast.8), channel_id=1, replica_groups=mesh['groups'=2,'tm'=8,'pair'=2] {'tm'}, dimensions={0} | all-to-all | bytes 2097152 | tf_op jit(solution)/shard_map/all_to_all | solution.py:243
  141.5 0.0 all-gather.5.cloned.1.call-update
  141.5 0.0 copy-done.4
  141.5 0.1 copy.14.pb_ref
  141.6 0.0 all-gather.7.cloned.1.call-done
  141.6 0.0 copy-done.2
  141.6 13.2 %shard_map.56.rest_0_ = f32[8,16,2,128,128]{4,3,2,1,0:T(8,128)} custom-call(s32[8,2]{1,0:T(8,128)S(1)} %copy.14.pb_ref, s32[8]{0:T(128)S(1)} %copy-done.2, s32[1]{0:T(128)} %constant.1.clone.1.q_ref, bf16[2,8,12,2,16,512]{5,4,3,2,1,0:T(8,128)(2,1)} %bitcast.10, bf16[2,8,12,2,16,512]{5,4,3,2,1,0:T(8,128)(2,1)} %bitcast.11), custom_call_target="tpu_custom_call" | custom-call | flops 1610612736 | bytes 25165824 | tf_op jit(solution)/shard_map/pallas_call | solution.py:215
  154.8 0.0 all-gather.5.cloned.1.call-done
  154.8 0.0 copy-start
  154.8 1.6 copy-done
  156.4 5.9 %shard_map.57 = f32[8,16,2,128,128]{4,3,2,1,0:T(8,128)} custom-call(s32[8,2]{1,0:T(8,128)S(1)} %copy.14.pb_ref, s32[8]{0:T(128)S(1)} %copy-done.2, s32[1]{0:T(128)} %constant.1.clone.1.q_ref, bf16[2,8,4,2,16,512]{5,4,3,2,1,0:T(8,128)(2,1)S(1)} %bitcast.5, bf16[2,8,4,2,16,512]{5,4,3,2,1,0:T(8,128)(2,1)S(1)} %bitcast.6, ...), custom_call_target="tpu_custom_call", output_to_operand_aliasing={{}: (5, {})} | custom-call | flops 536870912 | bytes 8388608 | tf_op jit(solution)/shard_map/pallas_call | solution.py:215
  (3 shorter events, 0.1 us)
Async XLA Ops:
  6.5 135.1 %all-gather.7.cloned.1.call-start = ((), (), s32[]{:S(2)}) async-start(), calls=%async_computation.3 | async-start | bytes 9437184 | tf_op jit(solution)/shard_map/all_gather | solution.py:244
  7.5 10.4 %collective-permute-start = (bf16[512,256]{1,0:T(8,128)(2,1)S(1)}, bf16[512,256]{1,0:T(8,128)(2,1)S(1)}, u32[]{:S(2)}, u32[]{:S(2)}) collective-permute-start(bf16[512,256]{1,0:T(8,128)(2,1)S(1)} %slice.6), channel_id=1, source_target_pairs={{0,2},{2,4},{4,6},{6,8},{8,10},{10,12},{12,14},{1,3},{3,5},{5,7},{... | collective-permute-start | bytes 786440 | tf_op jit(solution)/shard_map/ppermute | solution.py:25
  17.9 0.7 copy-start.1
  18.6 0.9 copy-start.3
  36.0 105.5 %copy-start.4 = (s32[8,2]{0,1:T(2,128)S(1)}, s32[8,2]{0,1:T(2,128)}, u32[]{:S(2)}) copy-start(s32[8,2]{0,1:T(2,128)} %param.8) | copy-start | bytes 196
  36.0 105.6 %copy-start.2 = (s32[8]{0:T(128)S(1)}, s32[8]{0:T(128)}, u32[]{:S(2)}) copy-start(s32[8]{0:T(128)} %kw_ref.3) | copy-start | bytes 100
  112.7 42.1 %all-gather.5.cloned.1.call-start = ((), (), s32[]{:S(2)}) async-start(), calls=%async_computation.2 | async-start | bytes 3145728 | tf_op jit(solution)/shard_map/all_gather | solution.py:244
  154.8 1.6 copy-start
Sparse Core Ops, SparseCore 0:
  112.9 15.6 all-gather.6
  141.6 9.5 all-gather.4

commit v10 on v9

--- a/solution.py
+++ b/solution.py
@@ -154,18 +154,22 @@
     )(kept_count, recording, tail_rows, toep, basis)
 
 
-def stack_kernel(pb_ref, kw_ref, q_ref, a_ref, b_ref, *rest):
+def stack_kernel_for(half_blocks, pb_ref, kw_ref, am_ref, ap_ref, bm_ref, bp_ref, *rest):
     o_ref = rest[-1]
     sections = kw_ref.shape[0]
     total = kw_ref[0]
     for s in range(1, sections):
         total = total + kw_ref[s]
     scale = 1.0 / jnp.sqrt(jnp.full((1, 1), total, jnp.int32).astype(jnp.float32))
-    segs, bins, _, wins, blk = a_ref.shape
+    segs, bins, _, wins, blk = am_ref.shape
+    p = pl.program_id(0)
+    mine = lax.axis_index("pair")
+    left_mine = pb_ref[p, 0] // half_blocks == mine
+    right_mine = pb_ref[p, 1] // half_blocks == mine
 
     def one_bin(jl, carry):
-        left = a_ref[:, jl].reshape(segs * 2 * wins, blk)
-        right = b_ref[:, jl]
+        left = jnp.where(left_mine, am_ref[:, jl], ap_ref[:, jl]).reshape(segs * 2 * wins, blk)
+        right = jnp.where(right_mine, bm_ref[:, jl], bp_ref[:, jl])
         swapped = jnp.concatenate([right[:, 1:2], -right[:, 0:1]], axis=1)
         rhs = jnp.concatenate(
             [right.reshape(segs * 2 * wins, blk), swapped.reshape(segs * 2 * wins, blk)], axis=1
@@ -180,40 +184,38 @@
     lax.fori_loop(0, bins, one_bin, 0, unroll=True)
 
 
-def stack_pairs(gathered, pair_blocks, kept_windows, half, chunk, all_bins, previous=None):
-    halves, segs, bins, two, wins, chans = gathered.shape
+def stack_pairs(local, partner, pair_blocks, kept_windows, chunk, all_bins, previous=None):
+    segs, bins, two, wins, chans = local.shape
     blocks_per_half = chans // CH_BLK
     npairs = pair_blocks.shape[0]
 
-    def left_map(p, pb, kw, q):
-        a = pb[p, 0]
-        return ((a // blocks_per_half + q[0]) % halves, 0, 0, 0, 0, a % blocks_per_half)
-
-    def right_map(p, pb, kw, q):
-        b = pb[p, 1]
-        return ((b // blocks_per_half + q[0]) % halves, 0, 0, 0, 0, b % blocks_per_half)
-
-    block = (None, segs, bins, two, wins, CH_BLK)
-    in_specs = [pl.BlockSpec(block, left_map), pl.BlockSpec(block, right_map)]
-    operands = [pair_blocks, kept_windows, half, gathered, gathered]
+    def left_map(p, pb, kw):
+        return (0, 0, 0, 0, pb[p, 0] % blocks_per_half)
+
+    def right_map(p, pb, kw):
+        return (0, 0, 0, 0, pb[p, 1] % blocks_per_half)
+
+    block = (segs, bins, two, wins, CH_BLK)
+    in_specs = [pl.BlockSpec(block, left_map)] * 2 + [pl.BlockSpec(block, right_map)] * 2
+    operands = [pair_blocks, kept_windows, local, partner, local, partner]
     aliases = {}
     if previous is not None:
         in_specs.append(pl.BlockSpec(memory_space=pl.ANY))
         operands.append(previous)
-        aliases = {5: 0}
+        aliases = {6: 0}
     grid_spec = pltpu.PrefetchScalarGridSpec(
-        num_scalar_prefetch=3,
+        num_scalar_prefetch=2,
         grid=(npairs,),
         in_specs=in_specs,
         out_specs=pl.BlockSpec(
-            (1, bins, 2, CH_BLK, CH_BLK), lambda p, pb, kw, q: (p, chunk, 0, 0, 0)
+            (1, bins, 2, CH_BLK, CH_BLK), lambda p, pb, kw: (p, chunk, 0, 0, 0)
         ),
     )
     flops = 2 * npairs * bins * CH_BLK * (2 * CH_BLK) * (segs * two * wins)
     out_bytes = npairs * bins * 2 * CH_BLK * CH_BLK * 4
-    in_bytes = 2 * npairs * segs * bins * two * wins * CH_BLK * 2
+    in_bytes = 4 * npairs * segs * bins * two * wins * CH_BLK * 2
     return pl.pallas_call(
-        stack_kernel,
+        functools.partial(stack_kernel_for, blocks_per_half),
         grid_spec=grid_spec,
         out_shape=jax.ShapeDtypeStruct((npairs, all_bins, 2, CH_BLK, CH_BLK), jnp.float32),
         input_output_aliases=aliases,
@@ -236,14 +238,13 @@
     small = max(bins_dev // 4, 1)
     chunks = [0, bins_dev - small, bins_dev] if bins_dev > 1 else [0, bins_dev]
     whitened = whiten_front(recording, tail_rows, fir_taps, kept_windows, chunks)
-    half = jnp.zeros((1,), jnp.int32)
     result = None
     for lo, hi, part in zip(chunks[:-1], chunks[1:], whitened):
         outgoing = part.reshape(sections, hi - lo, 2, windows_dev, channels)
         by_freq = lax.all_to_all(outgoing, "tm", split_axis=0, concat_axis=0, tiled=True)
-        gathered = lax.all_gather(by_freq, "pair", axis=0, tiled=False)
+        partner = lax.ppermute(by_freq, "pair", [(0, 1), (1, 0)])
         result = stack_pairs(
-            gathered, pair_blocks, kept_windows, half, lo // (hi - lo), bins_dev, result
+            by_freq, partner, pair_blocks, kept_windows, lo // (hi - lo), bins_dev, result
         )
     return result
 

time: 170 us -> 158 us (0.929)
  between operations: 13.5 us -> 0.07 us
where the time goes in v10:
time: 158 us; the launch traced here: 157 us
  blocking collectives  106 us (67%)
  Pallas kernels  37.2 us (24%)
  starting transfers between devices  4.89 us (3%)
  local copies, waits for them, and re-layouts  4.37 us (3%)
  waiting for transfers between devices  3.72 us (2%)
    all_to_all x2, blocking collectives, per_device(): lax.all_to_all(outgoing, 'tm', split_axis=0, concat_axis=0, tiled=True)  106 us
    pallas_call x2, Pallas kernels, stack_pairs(): pl.pallas_call(functools.partial(stack_kernel_for, blocks_per_half), grid...  20.7 us
    pallas_call x1, Pallas kernels, whiten_front(): pl.pallas_call(front_kernel, grid_spec=grid_spec, out_shape=[jax.ShapeDty...  16.5 us
    ppermute x1, starting transfers between devices, from_behind(): return lax.ppermute(array, axis, pairs)  4.89 us
    ppermute x1, waiting for transfers between devices, from_behind(): return lax.ppermute(array, axis, pairs)  3.72 us
  transfers between devices with their start and end apart: 3, of which 1 were waited for; matrix products, arithmetic and copies ran while one was open for 1% of the time, Pallas kernels for 8%

profile of v10, /device:TPU:0, one launch (start us, length us, event | category | flops | bytes accessed | tf_op | source)
XLA Modules:
  0.0 156.6 jit_solution(8462348058086087428)
XLA Ops:
  0.0 1.0 slice.6
  1.0 4.9 %collective-permute-start = (bf16[512,256]{1,0:T(8,128)(2,1)S(1)}, bf16[512,256]{1,0:T(8,128)(2,1)S(1)}, u32[]{:S(2)}, u32[]{:S(2)}) collective-permute-start(bf16[512,256]{1,0:T(8,128)(2,1)S(1)} %slice.6), channel_id=1, source_target_pairs={{0,2},{2,4},{4,6},{6,8},{8,10},{10,12},{12,14},{1,3},{3,5},{5,7},{... | collective-permute-start | bytes 786440 | tf_op jit(solution)/shard_map/ppermute | solution.py:25
  5.9 0.7 rev.3
  6.6 0.1 pad_maximum_fusion
  6.7 0.6 tile.10
  7.4 0.2 reshape.10
  7.5 0.1 copy.9
  7.7 3.7 %collective-permute-done.tail_ref = bf16[512,256]{1,0:T(8,128)(2,1)S(1)} collective-permute-done((bf16[512,256]{1,0:T(8,128)(2,1)S(1)}, bf16[512,256]{1,0:T(8,128)(2,1)S(1)}, u32[]{:S(2)}, u32[]{:S(2)}) %collective-permute-start) | collective-permute-done | bytes 262176 | tf_op jit(solution)/shard_map/ppermute | solution.py:25
  11.4 0.0 copy-start
  11.4 0.7 copy-done
  12.1 0.0 copy-start.2
  12.1 0.9 copy-done.2
  13.0 16.5 %shard_map.55 = (bf16[192,16,512]{2,1,0:T(8,128)(2,1)S(1)}, bf16[64,16,512]{2,1,0:T(8,128)(2,1)S(1)}) custom-call(s32[8]{0:T(128)S(1)} %copy-done, bf16[512,8192]{1,0:T(8,128)(2,1)} %rec_ref.1, bf16[512,256]{1,0:T(8,128)(2,1)S(1)} %collective-permute-done.tail_ref, bf16[512,256]{1,0:T(8,128)(2,1)S(1)} %bitcast.5, bf16[512,256]{1,0:T(8,128)(2,1)S(1)} %copy-done.2), custom_call_target="tpu_custom_call" | custom-call | flops 12884901888 | bytes 12582912 | tf_op jit(solution)/shard_map/pallas_call | solution.py:142
  29.5 0.0 copy-start.3
  29.5 0.0 copy-start.1
  29.5 76.6 %all_to_all.10.am_ref.bm_ref = bf16[8,12,2,16,512]{4,3,2,1,0:T(8,128)(2,1)S(1)} all-to-all(bf16[8,12,2,16,512]{4,3,2,1,0:T(8,128)(2,1)S(1)} %bitcast.3), channel_id=1, replica_groups=mesh['groups'=2,'tm'=8,'pair'=2] {'tm'}, dimensions={0} | all-to-all | bytes 6291456 | tf_op jit(solution)/shard_map/all_to_all | solution.py:244
  106.1 0.0 collective-permute-start.2
  106.1 29.8 %all_to_all.11.am_ref.bm_ref = bf16[8,4,2,16,512]{4,3,2,1,0:T(8,128)(2,1)} all-to-all(bf16[8,4,2,16,512]{4,3,2,1,0:T(8,128)(2,1)S(1)} %bitcast.4), channel_id=1, replica_groups=mesh['groups'=2,'tm'=8,'pair'=2] {'tm'}, dimensions={0} | all-to-all | bytes 2097152 | tf_op jit(solution)/shard_map/all_to_all | solution.py:244
  135.8 0.0 collective-permute-start.1
  135.8 0.0 copy-done.3
  135.8 0.1 copy.11.pb_ref
  135.9 0.0 collective-permute-done.2.ap_ref.bp_ref
  135.9 0.0 copy-done.1
  135.9 12.1 %shard_map.56.rest_0_ = f32[8,16,2,128,128]{4,3,2,1,0:T(8,128)} custom-call(s32[8,2]{1,0:T(8,128)S(1)} %copy.11.pb_ref, s32[8]{0:T(128)S(1)} %copy-done.1, bf16[8,12,2,16,512]{4,3,2,1,0:T(8,128)(2,1)S(1)} %all_to_all.10.am_ref.bm_ref, bf16[8,12,2,16,512]{4,3,2,1,0:T(8,128)(2,1)} %collective-permute-done.2.ap_ref.bp_ref, ...), custom_call_target="tpu_custom_call" | custom-call | flops 1610612736 | bytes 37748736 | tf_op jit(solution)/shard_map/pallas_call | solution.py:217
  148.1 0.0 collective-permute-done.1.ap_ref.bp_ref
  148.1 8.6 %shard_map.57 = f32[8,16,2,128,128]{4,3,2,1,0:T(8,128)} custom-call(s32[8,2]{1,0:T(8,128)S(1)} %copy.11.pb_ref, s32[8]{0:T(128)S(1)} %copy-done.1, bf16[8,4,2,16,512]{4,3,2,1,0:T(8,128)(2,1)} %all_to_all.11.am_ref.bm_ref, bf16[8,4,2,16,512]{4,3,2,1,0:T(8,128)(2,1)} %collective-permute-done.1.ap_ref.bp_ref, ...), custom_call_target="tpu_custom_call", output_to_operand_aliasing={{}: (6, {})} | custom-call | flops 536870912 | bytes 12582912 | tf_op jit(solution)/shard_map/pallas_call | solution.py:217
  (3 shorter events, 0.1 us)
Async XLA Ops:
  1.0 10.4 %collective-permute-start = (bf16[512,256]{1,0:T(8,128)(2,1)S(1)}, bf16[512,256]{1,0:T(8,128)(2,1)S(1)}, u32[]{:S(2)}, u32[]{:S(2)}) collective-permute-start(bf16[512,256]{1,0:T(8,128)(2,1)S(1)} %slice.6), channel_id=1, source_target_pairs={{0,2},{2,4},{4,6},{6,8},{8,10},{10,12},{12,14},{1,3},{3,5},{5,7},{... | collective-permute-start | bytes 786440 | tf_op jit(solution)/shard_map/ppermute | solution.py:25
  11.4 0.7 copy-start
  12.1 0.9 copy-start.2
  29.5 106.4 %copy-start.3 = (s32[8,2]{0,1:T(2,128)S(1)}, s32[8,2]{0,1:T(2,128)}, u32[]{:S(2)}) copy-start(s32[8,2]{0,1:T(2,128)} %param.8) | copy-start | bytes 196
  29.5 106.4 %copy-start.1 = (s32[8]{0:T(128)S(1)}, s32[8]{0:T(128)}, u32[]{:S(2)}) copy-start(s32[8]{0:T(128)} %kw_ref.3) | copy-start | bytes 100
  106.1 29.9 %collective-permute-start.2 = (bf16[8,12,2,16,512]{4,3,2,1,0:T(8,128)(2,1)S(1)}, bf16[8,12,2,16,512]{4,3,2,1,0:T(8,128)(2,1)}, u32[]{:S(2)}, u32[]{:S(2)}) collective-permute-start(bf16[8,12,2,16,512]{4,3,2,1,0:T(8,128)(2,1)S(1)} %all_to_all.10.am_ref.bm_ref), channel_id=1, source_target_pairs={{0,1},{1,0},{2,3},{3,2},{4,5},{5,4},{6,7},{7,6},{8,9},{9,8},{10,11... | collective-permute-start | bytes 9437192 | tf_op jit(solution)/shard_map/ppermute | solution.py:245
  135.8 12.2 %collective-permute-start.1 = (bf16[8,4,2,16,512]{4,3,2,1,0:T(8,128)(2,1)}, bf16[8,4,2,16,512]{4,3,2,1,0:T(8,128)(2,1)}, u32[]{:S(2)}, u32[]{:S(2)}) collective-permute-start(bf16[8,4,2,16,512]{4,3,2,1,0:T(8,128)(2,1)} %all_to_all.11.am_ref.bm_ref), channel_id=1, source_target_pairs={{0,1},{1,0},{2,3},{3,2},{4,5},{5,4},{6,7},{7,6},{8,9},{9,8},{10,11... | collective-permute-start | bytes 3145736 | tf_op jit(solution)/shard_map/ppermute | solution.py:245

commit v11 on v10

--- a/solution.py
+++ b/solution.py
@@ -154,7 +154,7 @@
     )(kept_count, recording, tail_rows, toep, basis)
 
 
-def stack_kernel_for(half_blocks, pb_ref, kw_ref, am_ref, ap_ref, bm_ref, bp_ref, *rest):
+def stack_kernel_for(half_blocks, pb_ref, kw_ref, q_ref, am_ref, ap_ref, bm_ref, bp_ref, *rest):
     o_ref = rest[-1]
     sections = kw_ref.shape[0]
     total = kw_ref[0]
@@ -163,7 +163,7 @@
     scale = 1.0 / jnp.sqrt(jnp.full((1, 1), total, jnp.int32).astype(jnp.float32))
     segs, bins, _, wins, blk = am_ref.shape
     p = pl.program_id(0)
-    mine = lax.axis_index("pair")
+    mine = q_ref[0]
     left_mine = pb_ref[p, 0] // half_blocks == mine
     right_mine = pb_ref[p, 1] // half_blocks == mine
 
@@ -184,36 +184,49 @@
     lax.fori_loop(0, bins, one_bin, 0, unroll=True)
 
 
-def stack_pairs(local, partner, pair_blocks, kept_windows, chunk, all_bins, previous=None):
+def stack_pairs(local, partner, pair_blocks, kept_windows, half, chunk, all_bins, previous=None):
     segs, bins, two, wins, chans = local.shape
     blocks_per_half = chans // CH_BLK
     npairs = pair_blocks.shape[0]
 
-    def left_map(p, pb, kw):
-        return (0, 0, 0, 0, pb[p, 0] % blocks_per_half)
-
-    def right_map(p, pb, kw):
-        return (0, 0, 0, 0, pb[p, 1] % blocks_per_half)
+    def held_map(side, wanted):
+        def index_map(p, pb, kw, q):
+            def block_of(i):
+                return pb[i, side] % blocks_per_half
+
+            def used_at(i):
+                return (pb[i, side] // blocks_per_half == q[0]) == wanted
+
+            held = block_of(npairs - 1)
+            for i in reversed(range(npairs)):
+                held = jnp.where(used_at(i), block_of(i), held)
+            for i in range(npairs):
+                held = jnp.where(jnp.logical_and(i <= p, used_at(i)), block_of(i), held)
+            return (0, 0, 0, 0, held)
+
+        return index_map
 
     block = (segs, bins, two, wins, CH_BLK)
-    in_specs = [pl.BlockSpec(block, left_map)] * 2 + [pl.BlockSpec(block, right_map)] * 2
-    operands = [pair_blocks, kept_windows, local, partner, local, partner]
+    in_specs = [
+        pl.BlockSpec(block, held_map(side, wanted)) for side in (0, 1) for wanted in (True, False)
+    ]
+    operands = [pair_blocks, kept_windows, half, local, partner, local, partner]
     aliases = {}
     if previous is not None:
         in_specs.append(pl.BlockSpec(memory_space=pl.ANY))
         operands.append(previous)
-        aliases = {6: 0}
+        aliases = {7: 0}
     grid_spec = pltpu.PrefetchScalarGridSpec(
-        num_scalar_prefetch=2,
+        num_scalar_prefetch=3,
         grid=(npairs,),
         in_specs=in_specs,
         out_specs=pl.BlockSpec(
-            (1, bins, 2, CH_BLK, CH_BLK), lambda p, pb, kw: (p, chunk, 0, 0, 0)
+            (1, bins, 2, CH_BLK, CH_BLK), lambda p, pb, kw, q: (p, chunk, 0, 0, 0)
         ),
     )
     flops = 2 * npairs * bins * CH_BLK * (2 * CH_BLK) * (segs * two * wins)
     out_bytes = npairs * bins * 2 * CH_BLK * CH_BLK * 4
-    in_bytes = 4 * npairs * segs * bins * two * wins * CH_BLK * 2
+    in_bytes = 2 * npairs * segs * bins * two * wins * CH_BLK * 2
     return pl.pallas_call(
         functools.partial(stack_kernel_for, blocks_per_half),
         grid_spec=grid_spec,
@@ -238,13 +251,14 @@
     small = max(bins_dev // 4, 1)
     chunks = [0, bins_dev - small, bins_dev] if bins_dev > 1 else [0, bins_dev]
     whitened = whiten_front(recording, tail_rows, fir_taps, kept_windows, chunks)
+    half = lax.axis_index("pair").reshape(1).astype(jnp.int32)
     result = None
     for lo, hi, part in zip(chunks[:-1], chunks[1:], whitened):
         outgoing = part.reshape(sections, hi - lo, 2, windows_dev, channels)
         by_freq = lax.all_to_all(outgoing, "tm", split_axis=0, concat_axis=0, tiled=True)
         partner = lax.ppermute(by_freq, "pair", [(0, 1), (1, 0)])
         result = stack_pairs(
-            by_freq, partner, pair_blocks, kept_windows, lo // (hi - lo), bins_dev, result
+            by_freq, partner, pair_blocks, kept_windows, half, lo // (hi - lo), bins_dev, result
         )
     return result
 

time: 158 us -> 158 us (level)
  no operation moved by 1% of the time
where the time goes in v11:
time: 158 us
  blocking collectives  106 us (67%)
  Pallas kernels  38.5 us (24%)
  starting transfers between devices  4.89 us (3%)
  local copies, waits for them, and re-layouts  4.37 us (3%)
  waiting for transfers between devices  3.72 us (2%)
    all_to_all x2, blocking collectives, per_device(): lax.all_to_all(outgoing, 'tm', split_axis=0, concat_axis=0, tiled=True)  106 us
    pallas_call x2, Pallas kernels, stack_pairs(): pl.pallas_call(functools.partial(stack_kernel_for, blocks_per_half), grid...  22.1 us
    pallas_call x1, Pallas kernels, whiten_front(): pl.pallas_call(front_kernel, grid_spec=grid_spec, out_shape=[jax.ShapeDty...  16.5 us
    ppermute x1, starting transfers between devices, from_behind(): return lax.ppermute(array, axis, pairs)  4.89 us
    ppermute x1, waiting for transfers between devices, from_behind(): return lax.ppermute(array, axis, pairs)  3.72 us
  transfers between devices with their start and end apart: 3, of which 1 were waited for; matrix products, arithmetic and copies ran while one was open for 1% of the time, Pallas kernels for 8%

profile of v11, /device:TPU:0, one launch (start us, length us, event | category | flops | bytes accessed | tf_op | source)
XLA Modules:
  0.0 158.0 jit_solution(2216921866776839276)
XLA Ops:
  0.0 1.0 slice.6
  1.0 4.9 %collective-permute-start = (bf16[512,256]{1,0:T(8,128)(2,1)S(1)}, bf16[512,256]{1,0:T(8,128)(2,1)S(1)}, u32[]{:S(2)}, u32[]{:S(2)}) collective-permute-start(bf16[512,256]{1,0:T(8,128)(2,1)S(1)} %slice.6), channel_id=1, source_target_pairs={{0,2},{2,4},{4,6},{6,8},{8,10},{10,12},{12,14},{1,3},{3,5},{5,7},{... | collective-permute-start | bytes 786440 | tf_op jit(solution)/shard_map/ppermute | solution.py:25
  5.9 0.7 rev.3
  6.6 0.1 pad_maximum_fusion
  6.7 0.6 tile.10
  7.4 0.2 reshape.14
  7.5 0.1 copy.9
  7.7 3.7 %collective-permute-done.tail_ref = bf16[512,256]{1,0:T(8,128)(2,1)S(1)} collective-permute-done((bf16[512,256]{1,0:T(8,128)(2,1)S(1)}, bf16[512,256]{1,0:T(8,128)(2,1)S(1)}, u32[]{:S(2)}, u32[]{:S(2)}) %collective-permute-start) | collective-permute-done | bytes 262176 | tf_op jit(solution)/shard_map/ppermute | solution.py:25
  11.4 0.0 copy-start
  11.4 0.7 copy-done
  12.1 0.0 copy-start.2
  12.1 0.9 copy-done.2
  13.0 16.5 %shard_map.55 = (bf16[192,16,512]{2,1,0:T(8,128)(2,1)S(1)}, bf16[64,16,512]{2,1,0:T(8,128)(2,1)S(1)}) custom-call(s32[8]{0:T(128)S(1)} %copy-done, bf16[512,8192]{1,0:T(8,128)(2,1)} %rec_ref.1, bf16[512,256]{1,0:T(8,128)(2,1)S(1)} %collective-permute-done.tail_ref, bf16[512,256]{1,0:T(8,128)(2,1)S(1)} %bitcast.6, bf16[512,256]{1,0:T(8,128)(2,1)S(1)} %copy-done.2), custom_call_target="tpu_custom_call" | custom-call | flops 12884901888 | bytes 12582912 | tf_op jit(solution)/shard_map/pallas_call | solution.py:142
  29.5 0.0 copy-start.3
  29.5 0.0 copy-start.1
  29.5 76.6 %all_to_all.10.am_ref.bm_ref = bf16[8,12,2,16,512]{4,3,2,1,0:T(8,128)(2,1)S(1)} all-to-all(bf16[8,12,2,16,512]{4,3,2,1,0:T(8,128)(2,1)S(1)} %bitcast.4), channel_id=1, replica_groups=mesh['groups'=2,'tm'=8,'pair'=2] {'tm'}, dimensions={0} | all-to-all | bytes 6291456 | tf_op jit(solution)/shard_map/all_to_all | solution.py:258
  106.1 0.0 collective-permute-start.2
  106.1 29.8 %all_to_all.11.am_ref.bm_ref = bf16[8,4,2,16,512]{4,3,2,1,0:T(8,128)(2,1)} all-to-all(bf16[8,4,2,16,512]{4,3,2,1,0:T(8,128)(2,1)S(1)} %bitcast.5), channel_id=1, replica_groups=mesh['groups'=2,'tm'=8,'pair'=2] {'tm'}, dimensions={0} | all-to-all | bytes 2097152 | tf_op jit(solution)/shard_map/all_to_all | solution.py:258
  135.8 0.0 collective-permute-start.1
  135.8 0.0 copy-done.3
  135.8 0.1 copy.11.pb_ref
  135.9 0.0 collective-permute-done.2.ap_ref.bp_ref
  135.9 0.0 copy-done.1
  135.9 12.7 %shard_map.56.rest_0_ = f32[8,16,2,128,128]{4,3,2,1,0:T(8,128)} custom-call(s32[8,2]{1,0:T(8,128)S(1)} %copy.11.pb_ref, s32[8]{0:T(128)S(1)} %copy-done.1, s32[1]{0:T(128)} %bitcast.q_ref, bf16[8,12,2,16,512]{4,3,2,1,0:T(8,128)(2,1)S(1)} %all_to_all.10.am_ref.bm_ref, bf16[8,12,2,16,512]{4,3,2,1,0:T(8,128)(2,1)} %collective-permute-done.2.ap_ref.bp_ref, ...), custom_call_target="tpu_custom_call" | custom-call | flops 1610612736 | bytes 25165824 | tf_op jit(solution)/shard_map/pallas_call | solution.py:230
  148.6 0.0 collective-permute-done.1.ap_ref.bp_ref
  148.6 9.4 %shard_map.57 = f32[8,16,2,128,128]{4,3,2,1,0:T(8,128)} custom-call(s32[8,2]{1,0:T(8,128)S(1)} %copy.11.pb_ref, s32[8]{0:T(128)S(1)} %copy-done.1, s32[1]{0:T(128)} %bitcast.q_ref, bf16[8,4,2,16,512]{4,3,2,1,0:T(8,128)(2,1)} %all_to_all.11.am_ref.bm_ref, ...), custom_call_target="tpu_custom_call", output_to_operand_aliasing={{}: (7, {})} | custom-call | flops 536870912 | bytes 8388608 | tf_op jit(solution)/shard_map/pallas_call | solution.py:230
  (3 shorter events, 0.1 us)
Async XLA Ops:
  1.0 10.4 %collective-permute-start = (bf16[512,256]{1,0:T(8,128)(2,1)S(1)}, bf16[512,256]{1,0:T(8,128)(2,1)S(1)}, u32[]{:S(2)}, u32[]{:S(2)}) collective-permute-start(bf16[512,256]{1,0:T(8,128)(2,1)S(1)} %slice.6), channel_id=1, source_target_pairs={{0,2},{2,4},{4,6},{6,8},{8,10},{10,12},{12,14},{1,3},{3,5},{5,7},{... | collective-permute-start | bytes 786440 | tf_op jit(solution)/shard_map/ppermute | solution.py:25
  11.4 0.7 copy-start
  12.1 0.9 copy-start.2
  29.5 106.4 %copy-start.3 = (s32[8,2]{0,1:T(2,128)S(1)}, s32[8,2]{0,1:T(2,128)}, u32[]{:S(2)}) copy-start(s32[8,2]{0,1:T(2,128)} %param.8) | copy-start | bytes 196
  29.5 106.4 %copy-start.1 = (s32[8]{0:T(128)S(1)}, s32[8]{0:T(128)}, u32[]{:S(2)}) copy-start(s32[8]{0:T(128)} %kw_ref.3) | copy-start | bytes 100
  106.1 29.9 %collective-permute-start.2 = (bf16[8,12,2,16,512]{4,3,2,1,0:T(8,128)(2,1)S(1)}, bf16[8,12,2,16,512]{4,3,2,1,0:T(8,128)(2,1)}, u32[]{:S(2)}, u32[]{:S(2)}) collective-permute-start(bf16[8,12,2,16,512]{4,3,2,1,0:T(8,128)(2,1)S(1)} %all_to_all.10.am_ref.bm_ref), channel_id=1, source_target_pairs={{0,1},{1,0},{2,3},{3,2},{4,5},{5,4},{6,7},{7,6},{8,9},{9,8},{10,11... | collective-permute-start | bytes 9437192 | tf_op jit(solution)/shard_map/ppermute | solution.py:259
  135.8 12.8 %collective-permute-start.1 = (bf16[8,4,2,16,512]{4,3,2,1,0:T(8,128)(2,1)}, bf16[8,4,2,16,512]{4,3,2,1,0:T(8,128)(2,1)}, u32[]{:S(2)}, u32[]{:S(2)}) collective-permute-start(bf16[8,4,2,16,512]{4,3,2,1,0:T(8,128)(2,1)} %all_to_all.11.am_ref.bm_ref), channel_id=1, source_target_pairs={{0,1},{1,0},{2,3},{3,2},{4,5},{5,4},{6,7},{7,6},{8,9},{9,8},{10,11... | collective-permute-start | bytes 3145736 | tf_op jit(solution)/shard_map/ppermute | solution.py:259

commit v12 on v10

--- a/solution.py
+++ b/solution.py
@@ -235,7 +235,7 @@
     tail_rows = from_behind(recording[:, length - width :], "tm", 1)
     windows_dev = length // WIN
     bins_dev = NF // sections
-    small = max(bins_dev // 4, 1)
+    small = max(bins_dev // 2, 1)
     chunks = [0, bins_dev - small, bins_dev] if bins_dev > 1 else [0, bins_dev]
     whitened = whiten_front(recording, tail_rows, fir_taps, kept_windows, chunks)
     result = None

time: 158 us -> 156 us (0.987)
  blocking collectives: 106 us -> 54.2 us
  waiting for transfers between devices: 3.72 us -> 51.3 us
  starting transfers between devices: 4.89 us -> 8.7 us
    all_to_all x2 -> x1, blocking collectives: 106 us -> 54.2 us  [per_device(): lax.all_to_all(outgoing, 'tm', split_axis=0, concat_axis=0, tiled=True)]
    all_to_all x0 -> x1, waiting for transfers between devices: none -> 47.6 us  [per_device(): lax.all_to_all(outgoing, 'tm', split_axis=0, concat_axis=0, tiled=True)]
    all_to_all x0 -> x1, starting transfers between devices: none -> 3.74 us  [per_device(): lax.all_to_all(outgoing, 'tm', split_axis=0, concat_axis=0, tiled=True)]
  transfers between devices with their start and end apart: 3 -> 4, of which waited for: 1 -> 2; matrix products, arithmetic and copies ran while one was open for 1% -> 1% of each run, Pallas kernels for 8% -> 7%
where the time goes in v12:
time: 156 us
  blocking collectives  54.2 us (35%)
  waiting for transfers between devices  51.3 us (33%)
  Pallas kernels  37 us (24%)
  starting transfers between devices  8.7 us (6%)
  local copies, waits for them, and re-layouts  4.41 us (3%)
    all_to_all x1, blocking collectives, per_device(): lax.all_to_all(outgoing, 'tm', split_axis=0, concat_axis=0, tiled=True)  54.2 us
    all_to_all x1, waiting for transfers between devices, per_device(): lax.all_to_all(outgoing, 'tm', split_axis=0, concat_axis=0, tiled=True)  47.6 us
    pallas_call x2, Pallas kernels, stack_pairs(): pl.pallas_call(functools.partial(stack_kernel_for, blocks_per_half), grid...  20.6 us
    pallas_call x1, Pallas kernels, whiten_front(): pl.pallas_call(front_kernel, grid_spec=grid_spec, out_shape=[jax.ShapeDty...  16.4 us
    ppermute x1, starting transfers between devices, from_behind(): return lax.ppermute(array, axis, pairs)  4.89 us
    all_to_all x1, starting transfers between devices, per_device(): lax.all_to_all(outgoing, 'tm', split_axis=0, concat_axis=0, tiled=True)  3.74 us
    ppermute x1, waiting for transfers between devices, from_behind(): return lax.ppermute(array, axis, pairs)  3.72 us
  transfers between devices with their start and end apart: 4, of which 2 were waited for; matrix products, arithmetic and copies ran while one was open for 1% of the time, Pallas kernels for 7%

profile of v12, /device:TPU:0, one launch (start us, length us, event | category | flops | bytes accessed | tf_op | source)
XLA Modules:
  0.0 155.7 jit_solution(9704198797303887061)
XLA Ops:
  0.0 0.0 copy-start.3
  0.0 0.0 copy-start.2
  0.0 1.0 slice.6
  1.0 4.9 %collective-permute-start = (bf16[512,256]{1,0:T(8,128)(2,1)S(1)}, bf16[512,256]{1,0:T(8,128)(2,1)S(1)}, u32[]{:S(2)}, u32[]{:S(2)}) collective-permute-start(bf16[512,256]{1,0:T(8,128)(2,1)S(1)} %slice.6), channel_id=1, source_target_pairs={{0,2},{2,4},{4,6},{6,8},{8,10},{10,12},{12,14},{1,3},{3,5},{5,7},{... | collective-permute-start | bytes 786440 | tf_op jit(solution)/shard_map/ppermute | solution.py:25
  5.9 0.7 rev.3
  6.7 0.1 pad_maximum_fusion
  6.8 0.6 tile.10
  7.4 0.2 reshape.10
  7.6 0.1 copy.9
  7.7 3.7 %collective-permute-done.tail_ref = bf16[512,256]{1,0:T(8,128)(2,1)S(1)} collective-permute-done((bf16[512,256]{1,0:T(8,128)(2,1)S(1)}, bf16[512,256]{1,0:T(8,128)(2,1)S(1)}, u32[]{:S(2)}, u32[]{:S(2)}) %collective-permute-start) | collective-permute-done | bytes 262176 | tf_op jit(solution)/shard_map/ppermute | solution.py:25
  11.4 0.0 copy-done.3
  11.4 0.0 copy-done.2
  11.4 16.4 %shard_map.55 = (bf16[128,16,512]{2,1,0:T(8,128)(2,1)S(1)}, bf16[128,16,512]{2,1,0:T(8,128)(2,1)S(1)}) custom-call(s32[8]{0:T(128)S(1)} %copy-done.2, bf16[512,8192]{1,0:T(8,128)(2,1)} %rec_ref.1, bf16[512,256]{1,0:T(8,128)(2,1)S(1)} %collective-permute-done.tail_ref, bf16[512,256]{1,0:T(8,128)(2,1)S(1)} %bitcast.5, bf16[512,256]{1,0:T(8,128)(2,1)S(1)} %copy-done.3), custom_call_target="tpu_custom_call" | custom-call | flops 12884901888 | bytes 12582912 | tf_op jit(solution)/shard_map/pallas_call | solution.py:142
  27.9 0.0 copy-start.1
  27.9 54.2 %all_to_all.10.am_ref.bm_ref = bf16[8,8,2,16,512]{4,3,2,1,0:T(8,128)(2,1)} all-to-all(bf16[8,8,2,16,512]{4,3,2,1,0:T(8,128)(2,1)S(1)} %bitcast.4), channel_id=1, replica_groups=mesh['groups'=2,'tm'=8,'pair'=2] {'tm'}, dimensions={0} | all-to-all | bytes 4194304 | tf_op jit(solution)/shard_map/all_to_all | solution.py:244
  82.0 0.0 copy-done.1
  82.0 0.0 copy-start.4
  82.0 3.7 %all-to-all-start = ((bf16[8,8,2,16,512]{4,3,2,1,0:T(8,128)(2,1)}), bf16[8,8,2,16,512]{4,3,2,1,0:T(8,128)(2,1)S(1)}, u32[]{:S(2)}, u32[]{:S(2)}) async-start(bf16[8,8,2,16,512]{4,3,2,1,0:T(8,128)(2,1)} %bitcast.3), calls=%async_computation | async-start | bytes 4194304 | tf_op jit(solution)/shard_map/all_to_all | solution.py:244
  85.8 0.1 collective-permute-start.2
  85.9 47.6 %all-to-all-done.am_ref.bm_ref = bf16[8,8,2,16,512]{4,3,2,1,0:T(8,128)(2,1)S(1)} async-done(((bf16[8,8,2,16,512]{4,3,2,1,0:T(8,128)(2,1)}), bf16[8,8,2,16,512]{4,3,2,1,0:T(8,128)(2,1)S(1)}, u32[]{:S(2)}, u32[]{:S(2)}) %all-to-all-start) | async-done | bytes 2097184 | tf_op jit(solution)/shard_map/all_to_all | solution.py:244
  133.4 0.0 collective-permute-start.1
  133.4 0.0 copy-done.4
  133.4 0.1 copy.11.pb_ref
  133.5 0.0 collective-permute-done.2.ap_ref.bp_ref
  133.5 0.0 copy-start
  133.5 1.6 %copy-done = bf16[8,8,2,16,512]{4,3,2,1,0:T(8,128)(2,1)S(1)} copy-done((bf16[8,8,2,16,512]{4,3,2,1,0:T(8,128)(2,1)S(1)}, bf16[8,8,2,16,512]{4,3,2,1,0:T(8,128)(2,1)}, u32[]{:S(2)}) %copy-start) | copy-done | bytes 2097176
  135.1 10.3 %shard_map.56.rest_0_ = f32[8,16,2,128,128]{4,3,2,1,0:T(8,128)} custom-call(s32[8,2]{1,0:T(8,128)S(1)} %copy.11.pb_ref, s32[8]{0:T(128)S(1)} %copy-done.2, bf16[8,8,2,16,512]{4,3,2,1,0:T(8,128)(2,1)S(1)} %copy-done, bf16[8,8,2,16,512]{4,3,2,1,0:T(8,128)(2,1)} %collective-permute-done.2.ap_ref.bp_ref, bf16[8,8,2,16,512]{4,3,2,1,0:T(8,128)(2,1)S(1)} %copy-done, ...), custom_call_target="tpu_custom_call" | custom-call | flops 1073741824 | bytes 25165824 | tf_op jit(solution)/shard_map/pallas_call | solution.py:217
  145.4 0.0 collective-permute-done.1.ap_ref.bp_ref
  145.4 10.3 %shard_map.57 = f32[8,16,2,128,128]{4,3,2,1,0:T(8,128)} custom-call(s32[8,2]{1,0:T(8,128)S(1)} %copy.11.pb_ref, s32[8]{0:T(128)S(1)} %copy-done.2, bf16[8,8,2,16,512]{4,3,2,1,0:T(8,128)(2,1)S(1)} %all-to-all-done.am_ref.bm_ref, bf16[8,8,2,16,512]{4,3,2,1,0:T(8,128)(2,1)} %collective-permute-done.1.ap_ref.bp_ref, ...), custom_call_target="tpu_custom_call", output_to_operand_aliasing={{}: (6, {})} | custom-call | flops 1073741824 | bytes 25165824 | tf_op jit(solution)/shard_map/pallas_call | solution.py:217
  (3 shorter events, 0.1 us)
Async XLA Ops:
  0.0 11.4 %copy-start.3 = (bf16[512,256]{1,0:T(8,128)(2,1)S(1)}, bf16[512,256]{1,0:T(8,128)(2,1)}, u32[]{:S(2)}) copy-start(bf16[512,256]{1,0:T(8,128)(2,1)} %constant.6.clone.basis_ref) | copy-start | bytes 786436
  0.0 11.4 %copy-start.2 = (s32[8]{0:T(128)S(1)}, s32[8]{0:T(128)}, u32[]{:S(2)}) copy-start(s32[8]{0:T(128)} %kw_ref.3) | copy-start | bytes 100
  1.0 10.4 %collective-permute-start = (bf16[512,256]{1,0:T(8,128)(2,1)S(1)}, bf16[512,256]{1,0:T(8,128)(2,1)S(1)}, u32[]{:S(2)}, u32[]{:S(2)}) collective-permute-start(bf16[512,256]{1,0:T(8,128)(2,1)S(1)} %slice.6), channel_id=1, source_target_pairs={{0,2},{2,4},{4,6},{6,8},{8,10},{10,12},{12,14},{1,3},{3,5},{5,7},{... | collective-permute-start | bytes 786440 | tf_op jit(solution)/shard_map/ppermute | solution.py:25
  27.9 54.2 %copy-start.1 = (bf16[128,16,512]{2,1,0:T(8,128)(2,1)}, bf16[128,16,512]{2,1,0:T(8,128)(2,1)S(1)}, u32[]{:S(2)}) copy-start(bf16[128,16,512]{2,1,0:T(8,128)(2,1)S(1)} %get-tuple-element.7) | copy-start | bytes 6291460
  82.0 51.4 %copy-start.4 = (s32[8,2]{0,1:T(2,128)S(1)}, s32[8,2]{0,1:T(2,128)}, u32[]{:S(2)}) copy-start(s32[8,2]{0,1:T(2,128)} %param.8) | copy-start | bytes 196
  82.0 51.4 %all-to-all-start = ((bf16[8,8,2,16,512]{4,3,2,1,0:T(8,128)(2,1)}), bf16[8,8,2,16,512]{4,3,2,1,0:T(8,128)(2,1)S(1)}, u32[]{:S(2)}, u32[]{:S(2)}) async-start(bf16[8,8,2,16,512]{4,3,2,1,0:T(8,128)(2,1)} %bitcast.3), calls=%async_computation | async-start | bytes 4194304 | tf_op jit(solution)/shard_map/all_to_all | solution.py:244
  85.8 47.7 %collective-permute-start.2 = (bf16[8,8,2,16,512]{4,3,2,1,0:T(8,128)(2,1)}, bf16[8,8,2,16,512]{4,3,2,1,0:T(8,128)(2,1)}, u32[]{:S(2)}, u32[]{:S(2)}) collective-permute-start(bf16[8,8,2,16,512]{4,3,2,1,0:T(8,128)(2,1)} %all_to_all.10.am_ref.bm_ref), channel_id=1, source_target_pairs={{0,1},{1,0},{2,3},{3,2},{4,5},{5,4},{6,7},{7,6},{8,9},{9,8},{10,11... | collective-permute-start | bytes 6291464 | tf_op jit(solution)/shard_map/ppermute | solution.py:245
  133.4 12.0 %collective-permute-start.1 = (bf16[8,8,2,16,512]{4,3,2,1,0:T(8,128)(2,1)S(1)}, bf16[8,8,2,16,512]{4,3,2,1,0:T(8,128)(2,1)}, u32[]{:S(2)}, u32[]{:S(2)}) collective-permute-start(bf16[8,8,2,16,512]{4,3,2,1,0:T(8,128)(2,1)S(1)} %all-to-all-done.am_ref.bm_ref), channel_id=1, source_target_pairs={{0,1},{1,0},{2,3},{3,2},{4,5},{5,4},{6,7},{7,6},{8,9},{9,8},{10,11... | collective-permute-start | bytes 6291464 | tf_op jit(solution)/shard_map/ppermute | solution.py:245
  133.5 1.6 %copy-start = (bf16[8,8,2,16,512]{4,3,2,1,0:T(8,128)(2,1)S(1)}, bf16[8,8,2,16,512]{4,3,2,1,0:T(8,128)(2,1)}, u32[]{:S(2)}) copy-start(bf16[8,8,2,16,512]{4,3,2,1,0:T(8,128)(2,1)} %all_to_all.10.am_ref.bm_ref) | copy-start | bytes 6291460

commit v13 on v12

--- a/solution.py
+++ b/solution.py
@@ -167,21 +167,34 @@
     left_mine = pb_ref[p, 0] // half_blocks == mine
     right_mine = pb_ref[p, 1] // half_blocks == mine
 
-    def one_bin(jl, carry):
-        left = jnp.where(left_mine, am_ref[:, jl], ap_ref[:, jl]).reshape(segs * 2 * wins, blk)
-        right = jnp.where(right_mine, bm_ref[:, jl], bp_ref[:, jl])
-        swapped = jnp.concatenate([right[:, 1:2], -right[:, 0:1]], axis=1)
-        rhs = jnp.concatenate(
-            [right.reshape(segs * 2 * wins, blk), swapped.reshape(segs * 2 * wins, blk)], axis=1
-        )
-        out = lax.dot_general(
-            left, rhs, (((0,), (0,)), ((), ())), preferred_element_type=jnp.float32
-        )
-        o_ref[0, jl, 0] = out[:, :blk] * scale
-        o_ref[0, jl, 1] = out[:, blk:] * scale
-        return carry
-
-    lax.fori_loop(0, bins, one_bin, 0, unroll=True)
+    def stack_from(a_ref, b_ref):
+        def one_bin(jl, carry):
+            left = a_ref[:, jl].reshape(segs * 2 * wins, blk)
+            right = b_ref[:, jl]
+            swapped = jnp.concatenate([right[:, 1:2], -right[:, 0:1]], axis=1)
+            rhs = jnp.concatenate(
+                [right.reshape(segs * 2 * wins, blk), swapped.reshape(segs * 2 * wins, blk)],
+                axis=1,
+            )
+            out = lax.dot_general(
+                left, rhs, (((0,), (0,)), ((), ())), preferred_element_type=jnp.float32
+            )
+            o_ref[0, jl, 0] = out[:, :blk] * scale
+            o_ref[0, jl, 1] = out[:, blk:] * scale
+            return carry
+
+        lax.fori_loop(0, bins, one_bin, 0, unroll=True)
+
+    for left_here in (True, False):
+        for right_here in (True, False):
+            chosen = jnp.logical_and(left_mine == left_here, right_mine == right_here)
+            pl.when(chosen)(
+                functools.partial(
+                    stack_from,
+                    am_ref if left_here else ap_ref,
+                    bm_ref if right_here else bp_ref,
+                )
+            )
 
 
 def stack_pairs(local, partner, pair_blocks, kept_windows, chunk, all_bins, previous=None):

time: 156 us -> 156 us (level)
  transfers between devices with their start and end apart: 4 -> 4, of which waited for: 2 -> 2; matrix products, arithmetic and copies ran while one was open for 1% -> 1% of each run, Pallas kernels for 7% -> 6%
where the time goes in v13:
time: 156 us; the launch traced here: 155 us
  blocking collectives  54.2 us (35%)
  waiting for transfers between devices  51.2 us (33%)
  Pallas kernels  35.7 us (23%)
  starting transfers between devices  8.88 us (6%)
  local copies, waits for them, and re-layouts  4.41 us (3%)
    all_to_all x1, blocking collectives, per_device(): lax.all_to_all(outgoing, 'tm', split_axis=0, concat_axis=0, tiled=True)  54.2 us
    all_to_all x1, waiting for transfers between devices, per_device(): lax.all_to_all(outgoing, 'tm', split_axis=0, concat_axis=0, tiled=True)  47.5 us
    pallas_call x2, Pallas kernels, stack_pairs(): pl.pallas_call(functools.partial(stack_kernel_for, blocks_per_half), grid...  19.3 us
    pallas_call x1, Pallas kernels, whiten_front(): pl.pallas_call(front_kernel, grid_spec=grid_spec, out_shape=[jax.ShapeDty...  16.4 us
    ppermute x1, starting transfers between devices, from_behind(): return lax.ppermute(array, axis, pairs)  4.89 us
    all_to_all x1, starting transfers between devices, per_device(): lax.all_to_all(outgoing, 'tm', split_axis=0, concat_axis=0, tiled=True)  3.92 us
    ppermute x1, waiting for transfers between devices, from_behind(): return lax.ppermute(array, axis, pairs)  3.72 us
  transfers between devices with their start and end apart: 4, of which 2 were waited for; matrix products, arithmetic and copies ran while one was open for 1% of the time, Pallas kernels for 6%

profile of v13, /device:TPU:0, one launch (start us, length us, event | category | flops | bytes accessed | tf_op | source)
XLA Modules:
  0.0 154.6 jit_solution(14405264845872067464)
XLA Ops:
  0.0 0.0 copy-start.3
  0.0 0.0 copy-start.2
  0.0 1.0 slice.6
  1.0 4.9 %collective-permute-start = (bf16[512,256]{1,0:T(8,128)(2,1)S(1)}, bf16[512,256]{1,0:T(8,128)(2,1)S(1)}, u32[]{:S(2)}, u32[]{:S(2)}) collective-permute-start(bf16[512,256]{1,0:T(8,128)(2,1)S(1)} %slice.6), channel_id=1, source_target_pairs={{0,2},{2,4},{4,6},{6,8},{8,10},{10,12},{12,14},{1,3},{3,5},{5,7},{... | collective-permute-start | bytes 786440 | tf_op jit(solution)/shard_map/ppermute | solution.py:25
  5.9 0.7 rev.3
  6.7 0.1 pad_maximum_fusion
  6.8 0.6 tile.10
  7.4 0.2 reshape.10
  7.6 0.1 copy.9
  7.7 3.7 %collective-permute-done.tail_ref = bf16[512,256]{1,0:T(8,128)(2,1)S(1)} collective-permute-done((bf16[512,256]{1,0:T(8,128)(2,1)S(1)}, bf16[512,256]{1,0:T(8,128)(2,1)S(1)}, u32[]{:S(2)}, u32[]{:S(2)}) %collective-permute-start) | collective-permute-done | bytes 262176 | tf_op jit(solution)/shard_map/ppermute | solution.py:25
  11.4 0.0 copy-done.3
  11.4 0.0 copy-done.2
  11.4 16.4 %shard_map.55 = (bf16[128,16,512]{2,1,0:T(8,128)(2,1)S(1)}, bf16[128,16,512]{2,1,0:T(8,128)(2,1)S(1)}) custom-call(s32[8]{0:T(128)S(1)} %copy-done.2, bf16[512,8192]{1,0:T(8,128)(2,1)} %rec_ref.1, bf16[512,256]{1,0:T(8,128)(2,1)S(1)} %collective-permute-done.tail_ref, bf16[512,256]{1,0:T(8,128)(2,1)S(1)} %bitcast.5, bf16[512,256]{1,0:T(8,128)(2,1)S(1)} %copy-done.3), custom_call_target="tpu_custom_call" | custom-call | flops 12884901888 | bytes 12582912 | tf_op jit(solution)/shard_map/pallas_call | solution.py:142
  27.9 0.0 copy-start.1
  27.9 54.2 %all_to_all.10.am_ref.bm_ref = bf16[8,8,2,16,512]{4,3,2,1,0:T(8,128)(2,1)} all-to-all(bf16[8,8,2,16,512]{4,3,2,1,0:T(8,128)(2,1)S(1)} %bitcast.4), channel_id=1, replica_groups=mesh['groups'=2,'tm'=8,'pair'=2] {'tm'}, dimensions={0} | all-to-all | bytes 4194304 | tf_op jit(solution)/shard_map/all_to_all | solution.py:257
  82.0 0.0 copy-done.1
  82.0 0.0 copy-start.4
  82.0 3.9 %all-to-all-start = ((bf16[8,8,2,16,512]{4,3,2,1,0:T(8,128)(2,1)}), bf16[8,8,2,16,512]{4,3,2,1,0:T(8,128)(2,1)S(1)}, u32[]{:S(2)}, u32[]{:S(2)}) async-start(bf16[8,8,2,16,512]{4,3,2,1,0:T(8,128)(2,1)} %bitcast.3), calls=%async_computation | async-start | bytes 4194304 | tf_op jit(solution)/shard_map/all_to_all | solution.py:257
  86.0 0.1 collective-permute-start.2
  86.0 47.5 %all-to-all-done.am_ref.bm_ref = bf16[8,8,2,16,512]{4,3,2,1,0:T(8,128)(2,1)S(1)} async-done(((bf16[8,8,2,16,512]{4,3,2,1,0:T(8,128)(2,1)}), bf16[8,8,2,16,512]{4,3,2,1,0:T(8,128)(2,1)S(1)}, u32[]{:S(2)}, u32[]{:S(2)}) %all-to-all-start) | async-done | bytes 2097184 | tf_op jit(solution)/shard_map/all_to_all | solution.py:257
  133.5 0.0 collective-permute-start.1
  133.5 0.0 copy-done.4
  133.5 0.1 copy.11.pb_ref
  133.6 0.0 collective-permute-done.2.ap_ref.bp_ref
  133.6 0.0 copy-start
  133.6 1.6 %copy-done = bf16[8,8,2,16,512]{4,3,2,1,0:T(8,128)(2,1)S(1)} copy-done((bf16[8,8,2,16,512]{4,3,2,1,0:T(8,128)(2,1)S(1)}, bf16[8,8,2,16,512]{4,3,2,1,0:T(8,128)(2,1)}, u32[]{:S(2)}) %copy-start) | copy-done | bytes 2097176
  135.2 9.7 %shard_map.56.rest_0_ = f32[8,16,2,128,128]{4,3,2,1,0:T(8,128)} custom-call(s32[8,2]{1,0:T(8,128)S(1)} %copy.11.pb_ref, s32[8]{0:T(128)S(1)} %copy-done.2, bf16[8,8,2,16,512]{4,3,2,1,0:T(8,128)(2,1)S(1)} %copy-done, bf16[8,8,2,16,512]{4,3,2,1,0:T(8,128)(2,1)} %collective-permute-done.2.ap_ref.bp_ref, bf16[8,8,2,16,512]{4,3,2,1,0:T(8,128)(2,1)S(1)} %copy-done, ...), custom_call_target="tpu_custom_call" | custom-call | flops 1073741824 | bytes 25165824 | tf_op jit(solution)/shard_map/pallas_call | solution.py:230
  144.9 0.0 collective-permute-done.1.ap_ref.bp_ref
  144.9 9.7 %shard_map.57 = f32[8,16,2,128,128]{4,3,2,1,0:T(8,128)} custom-call(s32[8,2]{1,0:T(8,128)S(1)} %copy.11.pb_ref, s32[8]{0:T(128)S(1)} %copy-done.2, bf16[8,8,2,16,512]{4,3,2,1,0:T(8,128)(2,1)S(1)} %all-to-all-done.am_ref.bm_ref, bf16[8,8,2,16,512]{4,3,2,1,0:T(8,128)(2,1)} %collective-permute-done.1.ap_ref.bp_ref, ...), custom_call_target="tpu_custom_call", output_to_operand_aliasing={{}: (6, {})} | custom-call | flops 1073741824 | bytes 25165824 | tf_op jit(solution)/shard_map/pallas_call | solution.py:230
  (3 shorter events, 0.1 us)
Async XLA Ops:
  0.0 11.4 %copy-start.3 = (bf16[512,256]{1,0:T(8,128)(2,1)S(1)}, bf16[512,256]{1,0:T(8,128)(2,1)}, u32[]{:S(2)}) copy-start(bf16[512,256]{1,0:T(8,128)(2,1)} %constant.6.clone.basis_ref) | copy-start | bytes 786436
  0.0 11.4 %copy-start.2 = (s32[8]{0:T(128)S(1)}, s32[8]{0:T(128)}, u32[]{:S(2)}) copy-start(s32[8]{0:T(128)} %kw_ref.3) | copy-start | bytes 100
  1.0 10.4 %collective-permute-start = (bf16[512,256]{1,0:T(8,128)(2,1)S(1)}, bf16[512,256]{1,0:T(8,128)(2,1)S(1)}, u32[]{:S(2)}, u32[]{:S(2)}) collective-permute-start(bf16[512,256]{1,0:T(8,128)(2,1)S(1)} %slice.6), channel_id=1, source_target_pairs={{0,2},{2,4},{4,6},{6,8},{8,10},{10,12},{12,14},{1,3},{3,5},{5,7},{... | collective-permute-start | bytes 786440 | tf_op jit(solution)/shard_map/ppermute | solution.py:25
  27.9 54.2 %copy-start.1 = (bf16[128,16,512]{2,1,0:T(8,128)(2,1)}, bf16[128,16,512]{2,1,0:T(8,128)(2,1)S(1)}, u32[]{:S(2)}) copy-start(bf16[128,16,512]{2,1,0:T(8,128)(2,1)S(1)} %get-tuple-element.7) | copy-start | bytes 6291460
  82.0 51.5 %copy-start.4 = (s32[8,2]{0,1:T(2,128)S(1)}, s32[8,2]{0,1:T(2,128)}, u32[]{:S(2)}) copy-start(s32[8,2]{0,1:T(2,128)} %param.8) | copy-start | bytes 196
  82.0 51.5 %all-to-all-start = ((bf16[8,8,2,16,512]{4,3,2,1,0:T(8,128)(2,1)}), bf16[8,8,2,16,512]{4,3,2,1,0:T(8,128)(2,1)S(1)}, u32[]{:S(2)}, u32[]{:S(2)}) async-start(bf16[8,8,2,16,512]{4,3,2,1,0:T(8,128)(2,1)} %bitcast.3), calls=%async_computation | async-start | bytes 4194304 | tf_op jit(solution)/shard_map/all_to_all | solution.py:257
  86.0 47.6 %collective-permute-start.2 = (bf16[8,8,2,16,512]{4,3,2,1,0:T(8,128)(2,1)}, bf16[8,8,2,16,512]{4,3,2,1,0:T(8,128)(2,1)}, u32[]{:S(2)}, u32[]{:S(2)}) collective-permute-start(bf16[8,8,2,16,512]{4,3,2,1,0:T(8,128)(2,1)} %all_to_all.10.am_ref.bm_ref), channel_id=1, source_target_pairs={{0,1},{1,0},{2,3},{3,2},{4,5},{5,4},{6,7},{7,6},{8,9},{9,8},{10,11... | collective-permute-start | bytes 6291464 | tf_op jit(solution)/shard_map/ppermute | solution.py:258
  133.5 11.4 %collective-permute-start.1 = (bf16[8,8,2,16,512]{4,3,2,1,0:T(8,128)(2,1)S(1)}, bf16[8,8,2,16,512]{4,3,2,1,0:T(8,128)(2,1)}, u32[]{:S(2)}, u32[]{:S(2)}) collective-permute-start(bf16[8,8,2,16,512]{4,3,2,1,0:T(8,128)(2,1)S(1)} %all-to-all-done.am_ref.bm_ref), channel_id=1, source_target_pairs={{0,1},{1,0},{2,3},{3,2},{4,5},{5,4},{6,7},{7,6},{8,9},{9,8},{10,11... | collective-permute-start | bytes 6291464 | tf_op jit(solution)/shard_map/ppermute | solution.py:258
  133.6 1.6 %copy-start = (bf16[8,8,2,16,512]{4,3,2,1,0:T(8,128)(2,1)S(1)}, bf16[8,8,2,16,512]{4,3,2,1,0:T(8,128)(2,1)}, u32[]{:S(2)}) copy-start(bf16[8,8,2,16,512]{4,3,2,1,0:T(8,128)(2,1)} %all_to_all.10.am_ref.bm_ref) | copy-start | bytes 6291460

commit v14 on v12

--- a/solution.py
+++ b/solution.py
@@ -109,7 +109,7 @@
         start += o_ref.shape[0]
 
 
-def whiten_front(recording, tail_rows, fir_taps, kept_count, chunks, tile=512):
+def whiten_front(recording, tail_rows, fir_taps, kept_count, chunks, tile=256):
     channels, length = recording.shape
     width = tail_rows.shape[1]
     windows = length // WIN

time: 156 us -> 157 us (level)
  transfers between devices with their start and end apart: 4 -> 4, of which waited for: 2 -> 2; matrix products, arithmetic and copies ran while one was open for 1% -> 1% of each run, Pallas kernels for 7% -> 6%
where the time goes in v14:
time: 157 us; the launch traced here: 156 us
  blocking collectives  54.2 us (35%)
  waiting for transfers between devices  51.3 us (33%)
  Pallas kernels  37.4 us (24%)
  starting transfers between devices  8.7 us (6%)
  local copies, waits for them, and re-layouts  4.41 us (3%)
    all_to_all x1, blocking collectives, per_device(): lax.all_to_all(outgoing, 'tm', split_axis=0, concat_axis=0, tiled=True)  54.2 us
    all_to_all x1, waiting for transfers between devices, per_device(): lax.all_to_all(outgoing, 'tm', split_axis=0, concat_axis=0, tiled=True)  47.6 us
    pallas_call x2, Pallas kernels, stack_pairs(): pl.pallas_call(functools.partial(stack_kernel_for, blocks_per_half), grid...  20.1 us
    pallas_call x1, Pallas kernels, whiten_front(): pl.pallas_call(front_kernel, grid_spec=grid_spec, out_shape=[jax.ShapeDty...  17.3 us
    ppermute x1, starting transfers between devices, from_behind(): return lax.ppermute(array, axis, pairs)  4.89 us
    all_to_all x1, starting transfers between devices, per_device(): lax.all_to_all(outgoing, 'tm', split_axis=0, concat_axis=0, tiled=True)  3.74 us
    ppermute x1, waiting for transfers between devices, from_behind(): return lax.ppermute(array, axis, pairs)  3.72 us
  transfers between devices with their start and end apart: 4, of which 2 were waited for; matrix products, arithmetic and copies ran while one was open for 1% of the time, Pallas kernels for 6%

profile of v14, /device:TPU:0, one launch (start us, length us, event | category | flops | bytes accessed | tf_op | source)
XLA Modules:
  0.0 156.1 jit_solution(9826732440378741041)
XLA Ops:
  0.0 0.0 copy-start.3
  0.0 0.0 copy-start.2
  0.0 1.0 slice.6
  1.0 4.9 %collective-permute-start = (bf16[512,256]{1,0:T(8,128)(2,1)S(1)}, bf16[512,256]{1,0:T(8,128)(2,1)S(1)}, u32[]{:S(2)}, u32[]{:S(2)}) collective-permute-start(bf16[512,256]{1,0:T(8,128)(2,1)S(1)} %slice.6), channel_id=1, source_target_pairs={{0,2},{2,4},{4,6},{6,8},{8,10},{10,12},{12,14},{1,3},{3,5},{5,7},{... | collective-permute-start | bytes 786440 | tf_op jit(solution)/shard_map/ppermute | solution.py:25
  5.9 0.7 rev.3
  6.7 0.1 pad_maximum_fusion
  6.8 0.6 tile.10
  7.4 0.2 reshape.10
  7.6 0.1 copy.9
  7.7 3.7 %collective-permute-done.tail_ref = bf16[512,256]{1,0:T(8,128)(2,1)S(1)} collective-permute-done((bf16[512,256]{1,0:T(8,128)(2,1)S(1)}, bf16[512,256]{1,0:T(8,128)(2,1)S(1)}, u32[]{:S(2)}, u32[]{:S(2)}) %collective-permute-start) | collective-permute-done | bytes 262176 | tf_op jit(solution)/shard_map/ppermute | solution.py:25
  11.4 0.0 copy-done.3
  11.4 0.0 copy-done.2
  11.4 17.3 %shard_map.55 = (bf16[128,16,512]{2,1,0:T(8,128)(2,1)S(1)}, bf16[128,16,512]{2,1,0:T(8,128)(2,1)S(1)}) custom-call(s32[8]{0:T(128)S(1)} %copy-done.2, bf16[512,8192]{1,0:T(8,128)(2,1)} %rec_ref.1, bf16[512,256]{1,0:T(8,128)(2,1)S(1)} %collective-permute-done.tail_ref, bf16[512,256]{1,0:T(8,128)(2,1)S(1)} %bitcast.5, bf16[512,256]{1,0:T(8,128)(2,1)S(1)} %copy-done.3), custom_call_target="tpu_custom_call" | custom-call | flops 12884901888 | bytes 12582912 | tf_op jit(solution)/shard_map/pallas_call | solution.py:142
  28.7 0.0 copy-start.1
  28.8 54.2 %all_to_all.10.am_ref.bm_ref = bf16[8,8,2,16,512]{4,3,2,1,0:T(8,128)(2,1)} all-to-all(bf16[8,8,2,16,512]{4,3,2,1,0:T(8,128)(2,1)S(1)} %bitcast.4), channel_id=1, replica_groups=mesh['groups'=2,'tm'=8,'pair'=2] {'tm'}, dimensions={0} | all-to-all | bytes 4194304 | tf_op jit(solution)/shard_map/all_to_all | solution.py:244
  82.9 0.0 copy-done.1
  82.9 0.0 copy-start.4
  82.9 3.7 %all-to-all-start = ((bf16[8,8,2,16,512]{4,3,2,1,0:T(8,128)(2,1)}), bf16[8,8,2,16,512]{4,3,2,1,0:T(8,128)(2,1)S(1)}, u32[]{:S(2)}, u32[]{:S(2)}) async-start(bf16[8,8,2,16,512]{4,3,2,1,0:T(8,128)(2,1)} %bitcast.3), calls=%async_computation | async-start | bytes 4194304 | tf_op jit(solution)/shard_map/all_to_all | solution.py:244
  86.7 0.1 collective-permute-start.2
  86.7 47.6 %all-to-all-done.am_ref.bm_ref = bf16[8,8,2,16,512]{4,3,2,1,0:T(8,128)(2,1)S(1)} async-done(((bf16[8,8,2,16,512]{4,3,2,1,0:T(8,128)(2,1)}), bf16[8,8,2,16,512]{4,3,2,1,0:T(8,128)(2,1)S(1)}, u32[]{:S(2)}, u32[]{:S(2)}) %all-to-all-start) | async-done | bytes 2097184 | tf_op jit(solution)/shard_map/all_to_all | solution.py:244
  134.3 0.0 collective-permute-start.1
  134.3 0.0 copy-done.4
  134.3 0.1 copy.11.pb_ref
  134.4 0.0 collective-permute-done.2.ap_ref.bp_ref
  134.4 0.0 copy-start
  134.4 1.6 %copy-done = bf16[8,8,2,16,512]{4,3,2,1,0:T(8,128)(2,1)S(1)} copy-done((bf16[8,8,2,16,512]{4,3,2,1,0:T(8,128)(2,1)S(1)}, bf16[8,8,2,16,512]{4,3,2,1,0:T(8,128)(2,1)}, u32[]{:S(2)}) %copy-start) | copy-done | bytes 2097176
  136.0 10.0 %shard_map.56.rest_0_ = f32[8,16,2,128,128]{4,3,2,1,0:T(8,128)} custom-call(s32[8,2]{1,0:T(8,128)S(1)} %copy.11.pb_ref, s32[8]{0:T(128)S(1)} %copy-done.2, bf16[8,8,2,16,512]{4,3,2,1,0:T(8,128)(2,1)S(1)} %copy-done, bf16[8,8,2,16,512]{4,3,2,1,0:T(8,128)(2,1)} %collective-permute-done.2.ap_ref.bp_ref, bf16[8,8,2,16,512]{4,3,2,1,0:T(8,128)(2,1)S(1)} %copy-done, ...), custom_call_target="tpu_custom_call" | custom-call | flops 1073741824 | bytes 25165824 | tf_op jit(solution)/shard_map/pallas_call | solution.py:217
  146.0 0.0 collective-permute-done.1.ap_ref.bp_ref
  146.0 10.1 %shard_map.57 = f32[8,16,2,128,128]{4,3,2,1,0:T(8,128)} custom-call(s32[8,2]{1,0:T(8,128)S(1)} %copy.11.pb_ref, s32[8]{0:T(128)S(1)} %copy-done.2, bf16[8,8,2,16,512]{4,3,2,1,0:T(8,128)(2,1)S(1)} %all-to-all-done.am_ref.bm_ref, bf16[8,8,2,16,512]{4,3,2,1,0:T(8,128)(2,1)} %collective-permute-done.1.ap_ref.bp_ref, ...), custom_call_target="tpu_custom_call", output_to_operand_aliasing={{}: (6, {})} | custom-call | flops 1073741824 | bytes 25165824 | tf_op jit(solution)/shard_map/pallas_call | solution.py:217
  (3 shorter events, 0.1 us)
Async XLA Ops:
  0.0 11.4 %copy-start.3 = (bf16[512,256]{1,0:T(8,128)(2,1)S(1)}, bf16[512,256]{1,0:T(8,128)(2,1)}, u32[]{:S(2)}) copy-start(bf16[512,256]{1,0:T(8,128)(2,1)} %constant.6.clone.basis_ref) | copy-start | bytes 786436
  0.0 11.4 %copy-start.2 = (s32[8]{0:T(128)S(1)}, s32[8]{0:T(128)}, u32[]{:S(2)}) copy-start(s32[8]{0:T(128)} %kw_ref.3) | copy-start | bytes 100
  1.0 10.4 %collective-permute-start = (bf16[512,256]{1,0:T(8,128)(2,1)S(1)}, bf16[512,256]{1,0:T(8,128)(2,1)S(1)}, u32[]{:S(2)}, u32[]{:S(2)}) collective-permute-start(bf16[512,256]{1,0:T(8,128)(2,1)S(1)} %slice.6), channel_id=1, source_target_pairs={{0,2},{2,4},{4,6},{6,8},{8,10},{10,12},{12,14},{1,3},{3,5},{5,7},{... | collective-permute-start | bytes 786440 | tf_op jit(solution)/shard_map/ppermute | solution.py:25
  28.7 54.2 %copy-start.1 = (bf16[128,16,512]{2,1,0:T(8,128)(2,1)}, bf16[128,16,512]{2,1,0:T(8,128)(2,1)S(1)}, u32[]{:S(2)}) copy-start(bf16[128,16,512]{2,1,0:T(8,128)(2,1)S(1)} %get-tuple-element.7) | copy-start | bytes 6291460
  82.9 51.4 %copy-start.4 = (s32[8,2]{0,1:T(2,128)S(1)}, s32[8,2]{0,1:T(2,128)}, u32[]{:S(2)}) copy-start(s32[8,2]{0,1:T(2,128)} %param.8) | copy-start | bytes 196
  82.9 51.4 %all-to-all-start = ((bf16[8,8,2,16,512]{4,3,2,1,0:T(8,128)(2,1)}), bf16[8,8,2,16,512]{4,3,2,1,0:T(8,128)(2,1)S(1)}, u32[]{:S(2)}, u32[]{:S(2)}) async-start(bf16[8,8,2,16,512]{4,3,2,1,0:T(8,128)(2,1)} %bitcast.3), calls=%async_computation | async-start | bytes 4194304 | tf_op jit(solution)/shard_map/all_to_all | solution.py:244
  86.7 47.7 %collective-permute-start.2 = (bf16[8,8,2,16,512]{4,3,2,1,0:T(8,128)(2,1)}, bf16[8,8,2,16,512]{4,3,2,1,0:T(8,128)(2,1)}, u32[]{:S(2)}, u32[]{:S(2)}) collective-permute-start(bf16[8,8,2,16,512]{4,3,2,1,0:T(8,128)(2,1)} %all_to_all.10.am_ref.bm_ref), channel_id=1, source_target_pairs={{0,1},{1,0},{2,3},{3,2},{4,5},{5,4},{6,7},{7,6},{8,9},{9,8},{10,11... | collective-permute-start | bytes 6291464 | tf_op jit(solution)/shard_map/ppermute | solution.py:245
  134.3 11.7 %collective-permute-start.1 = (bf16[8,8,2,16,512]{4,3,2,1,0:T(8,128)(2,1)S(1)}, bf16[8,8,2,16,512]{4,3,2,1,0:T(8,128)(2,1)}, u32[]{:S(2)}, u32[]{:S(2)}) collective-permute-start(bf16[8,8,2,16,512]{4,3,2,1,0:T(8,128)(2,1)S(1)} %all-to-all-done.am_ref.bm_ref), channel_id=1, source_target_pairs={{0,1},{1,0},{2,3},{3,2},{4,5},{5,4},{6,7},{7,6},{8,9},{9,8},{10,11... | collective-permute-start | bytes 6291464 | tf_op jit(solution)/shard_map/ppermute | solution.py:245
  134.4 1.6 %copy-start = (bf16[8,8,2,16,512]{4,3,2,1,0:T(8,128)(2,1)S(1)}, bf16[8,8,2,16,512]{4,3,2,1,0:T(8,128)(2,1)}, u32[]{:S(2)}) copy-start(bf16[8,8,2,16,512]{4,3,2,1,0:T(8,128)(2,1)} %all_to_all.10.am_ref.bm_ref) | copy-start | bytes 6291460

commit v15 on v12

--- a/solution.py
+++ b/solution.py
@@ -68,20 +68,23 @@
     return basis_table.reshape(length, 2 * bins).astype(ml_dtypes.bfloat16)
 
 
-def front_kernel(cnt_ref, rec_ref, tail_ref, toep_ref, basis_ref, *rest):
-    outs, (scr_ref, inv_ref) = rest[:-2], rest[-2:]
+def front_kernel(cnt_ref, rec_ref, toep_ref, basis_ref, *rest):
+    outs, f1_ref, (scr_ref, inv_ref) = rest[:-3], rest[-3], rest[-2:]
     tile, length = rec_ref.shape
-    width = tail_ref.shape[1]
+    width = toep_ref.shape[1]
     bins2 = basis_ref.shape[1]
     windows = length // WIN
     toep = toep_ref[...]
     basis = basis_ref[...]
     count = cnt_ref[lax.axis_index("tm")]
-    for w in range(windows):
-        if w == 0:
-            ext0 = jnp.concatenate([tail_ref[...], rec_ref[:, 0:width]], axis=1)
-        else:
-            ext0 = rec_ref[:, WIN * w - width : WIN * w + width]
+    f1_ref[...] = jnp.dot(
+        rec_ref[:, 0 : 2 * width], toep, preferred_element_type=jnp.float32
+    ).astype(jnp.bfloat16)
+    for h in range(tile // CH_BLK):
+        scr_ref[h, pl.ds(0, bins2), :] = jnp.zeros((bins2, CH_BLK), jnp.float32)
+    inv_ref[pl.ds(0, 1), :] = jnp.zeros((1, tile), jnp.float32)
+    for w in range(1, windows):
+        ext0 = rec_ref[:, WIN * w - width : WIN * w + width]
         ext1 = rec_ref[:, WIN * w : WIN * w + 2 * width]
         f0 = jnp.dot(ext0, toep, preferred_element_type=jnp.float32).astype(jnp.bfloat16)
         f1 = jnp.dot(ext1, toep, preferred_element_type=jnp.float32).astype(jnp.bfloat16)
@@ -109,6 +112,67 @@
         start += o_ref.shape[0]
 
 
+def first_window_kernel(count_parts, cnt_ref, tail_ref, rec_ref, f1_ref, toep_ref, basis_ref, *rest):
+    ins, outs, w0_ref = rest[:count_parts], rest[count_parts : 2 * count_parts], rest[-1]
+    bins2 = basis_ref.shape[1]
+    count = cnt_ref[lax.axis_index("tm")]
+    ext0 = jnp.concatenate([tail_ref[...], rec_ref[...]], axis=1)
+    f0 = jnp.dot(ext0, toep_ref[...], preferred_element_type=jnp.float32).astype(jnp.bfloat16)
+    spec = jnp.dot(
+        jnp.concatenate([f0, f1_ref[...]], axis=1), basis_ref[...], preferred_element_type=jnp.float32
+    ).T
+    power = jnp.sum(spec * spec, axis=0, keepdims=True) * (1.0 / bins2)
+    keep = jnp.where(count > 0, 1.0, 0.0).astype(jnp.float32)
+    w0_ref[...] = spec * (lax.rsqrt(power + whiten_eps) * keep)
+    start = 0
+    for i_ref, o_ref in zip(ins, outs):
+
+        def one_row(k, carry, i_ref=i_ref, o_ref=o_ref, start=start):
+            held = i_ref[k]
+            first = w0_ref[pl.ds(start + k, 1), :].astype(held.dtype)
+            rowid = lax.broadcasted_iota(jnp.int32, held.shape, 0)
+            o_ref[k] = jnp.where(rowid == 0, first, held)
+            return carry
+
+        lax.fori_loop(0, o_ref.shape[0], one_row, 0, unroll=8)
+        start += o_ref.shape[0]
+
+
+def fill_first_window(parts, recording, tail_rows, f1, toep, basis, kept_count):
+    channels, width = tail_rows.shape
+    bins2 = basis.shape[1]
+    count_parts = len(parts)
+    full = lambda shape: pl.BlockSpec(shape, lambda i, c: (0,) * len(shape))
+    grid_spec = pltpu.PrefetchScalarGridSpec(
+        num_scalar_prefetch=1,
+        grid=(1,),
+        in_specs=[
+            full(tail_rows.shape),
+            pl.BlockSpec((channels, width), lambda i, c: (0, 0)),
+            full(f1.shape),
+            full(toep.shape),
+            full(basis.shape),
+        ]
+        + [full(p.shape) for p in parts],
+        out_specs=[full(p.shape) for p in parts],
+        scratch_shapes=[pltpu.VMEM((bins2, channels), jnp.float32)],
+    )
+    return pl.pallas_call(
+        functools.partial(first_window_kernel, count_parts),
+        grid_spec=grid_spec,
+        out_shape=[jax.ShapeDtypeStruct(p.shape, p.dtype) for p in parts],
+        input_output_aliases={6 + i: i for i in range(count_parts)},
+        compiler_params=pltpu.CompilerParams(
+            dimension_semantics=("arbitrary",), vmem_limit_bytes=48 * 1024 * 1024
+        ),
+        cost_estimate=pl.CostEstimate(
+            flops=2 * channels * 3 * (2 * width) * bins2,
+            bytes_accessed=4 * sum(p.size for p in parts),
+            transcendentals=channels,
+        ),
+    )(kept_count, tail_rows, recording, f1, toep, basis, *parts)
+
+
 def whiten_front(recording, tail_rows, fir_taps, kept_count, chunks, tile=512):
     channels, length = recording.shape
     width = tail_rows.shape[1]
@@ -128,21 +192,22 @@
         grid=(channels // tile,),
         in_specs=[
             pl.BlockSpec((tile, length), lambda i, c: (i, 0)),
-            pl.BlockSpec((tile, width), lambda i, c: (i, 0)),
             pl.BlockSpec(toep.shape, lambda i, c: (0, 0)),
             pl.BlockSpec(basis.shape, lambda i, c: (0, 0)),
         ],
-        out_specs=[pl.BlockSpec((r, windows, tile), lambda i, c: (0, 0, i)) for r in rows],
+        out_specs=[pl.BlockSpec((r, windows, tile), lambda i, c: (0, 0, i)) for r in rows]
+        + [pl.BlockSpec((tile, width), lambda i, c: (i, 0))],
         scratch_shapes=[
             pltpu.VMEM((tile // CH_BLK, windows * bins2, CH_BLK), jnp.float32),
             pltpu.VMEM((windows, tile), jnp.float32),
         ],
     )
     flops = 2 * channels * windows * 3 * (2 * width) * bins2 * 2
-    return pl.pallas_call(
+    *parts, f1 = pl.pallas_call(
         front_kernel,
         grid_spec=grid_spec,
-        out_shape=[jax.ShapeDtypeStruct((r, windows, channels), jnp.bfloat16) for r in rows],
+        out_shape=[jax.ShapeDtypeStruct((r, windows, channels), jnp.bfloat16) for r in rows]
+        + [jax.ShapeDtypeStruct((channels, width), jnp.bfloat16)],
         compiler_params=pltpu.CompilerParams(
             dimension_semantics=("arbitrary",), vmem_limit_bytes=48 * 1024 * 1024
         ),
@@ -151,7 +216,8 @@
             bytes_accessed=channels * length * 2 + bins2 * windows * channels * 2,
             transcendentals=channels * windows,
         ),
-    )(kept_count, recording, tail_rows, toep, basis)
+    )(kept_count, recording, toep, basis)
+    return fill_first_window(parts, recording, tail_rows, f1, toep, basis, kept_count)
 
 
 def stack_kernel_for(half_blocks, pb_ref, kw_ref, am_ref, ap_ref, bm_ref, bp_ref, *rest):

time: 156 us -> 155 us (level); the launches traced: 156 us -> 152 us
  waiting for transfers between devices: 51.3 us -> 47.6 us
  Pallas kernels: 37 us -> 38.7 us
    ppermute x1, waiting for transfers between devices: 3.72 us -> 0.01 us  [from_behind(): return lax.ppermute(array, axis, pairs)]
    pallas_call x0 -> x1, Pallas kernels: none -> 3.59 us  [fill_first_window(): pl.pallas_call(functools.partial(first_window_kernel, count_parts), grid_...]
    pallas_call x2, Pallas kernels: 20.6 us -> 18.9 us  [stack_pairs(): pl.pallas_call(functools.partial(stack_kernel_for, blocks_per_half), grid...]
  transfers between devices with their start and end apart: 4 -> 4, of which waited for: 2 -> 1; matrix products, arithmetic and copies ran while one was open for 1% -> 1% of each run, Pallas kernels for 7% -> 17%
where the time goes in v15:
time: 155 us; the launch traced here: 152 us
  blocking collectives  52.8 us (34%)
  waiting for transfers between devices  47.6 us (31%)
  Pallas kernels  38.7 us (25%)
  starting transfers between devices  8.7 us (6%)
  local copies, waits for them, and re-layouts  4.41 us (3%)
    all_to_all x1, blocking collectives, per_device(): lax.all_to_all(outgoing, 'tm', split_axis=0, concat_axis=0, tiled=True)  52.8 us
    all_to_all x1, waiting for transfers between devices, per_device(): lax.all_to_all(outgoing, 'tm', split_axis=0, concat_axis=0, tiled=True)  47.6 us
    pallas_call x2, Pallas kernels, stack_pairs(): pl.pallas_call(functools.partial(stack_kernel_for, blocks_per_half), grid...  18.9 us
    pallas_call x1, Pallas kernels, whiten_front(): pl.pallas_call(front_kernel, grid_spec=grid_spec, out_shape=[jax.ShapeDty...  16.2 us
    ppermute x1, starting transfers between devices, from_behind(): return lax.ppermute(array, axis, pairs)  4.89 us
    all_to_all x1, starting transfers between devices, per_device(): lax.all_to_all(outgoing, 'tm', split_axis=0, concat_axis=0, tiled=True)  3.74 us
    pallas_call x1, Pallas kernels, fill_first_window(): pl.pallas_call(functools.partial(first_window_kernel, count_parts), grid_...  3.59 us
  transfers between devices with their start and end apart: 4, of which 1 were waited for; matrix products, arithmetic and copies ran while one was open for 1% of the time, Pallas kernels for 17%

profile of v15, /device:TPU:0, one launch (start us, length us, event | category | flops | bytes accessed | tf_op | source)
XLA Modules:
  0.0 152.4 jit_solution(11548834398960849817)
XLA Ops:
  0.0 0.0 copy-start.2
  0.0 0.0 copy-start.3
  0.0 1.0 slice.6
  1.0 4.9 %collective-permute-start = (bf16[512,256]{1,0:T(8,128)(2,1)S(1)}, bf16[512,256]{1,0:T(8,128)(2,1)S(1)}, u32[]{:S(2)}, u32[]{:S(2)}) collective-permute-start(bf16[512,256]{1,0:T(8,128)(2,1)S(1)} %slice.6), channel_id=1, source_target_pairs={{0,2},{2,4},{4,6},{6,8},{8,10},{10,12},{12,14},{1,3},{3,5},{5,7},{... | collective-permute-start | bytes 786440 | tf_op jit(solution)/shard_map/ppermute | solution.py:25
  5.9 0.7 rev.3
  6.7 0.1 pad_maximum_fusion
  6.8 0.6 tile.10
  7.4 0.2 reshape.10
  7.6 0.1 copy.11
  7.7 0.0 copy-done.2
  7.7 0.0 copy-done.3
  7.7 16.2 %shard_map.55 = (bf16[128,16,512]{2,1,0:T(8,128)(2,1)S(1)}, bf16[128,16,512]{2,1,0:T(8,128)(2,1)S(1)}, bf16[512,256]{1,0:T(8,128)(2,1)S(1)}) custom-call(s32[8]{0:T(128)S(1)} %copy-done.3, bf16[512,8192]{1,0:T(8,128)(2,1)} %rec_ref.3, bf16[512,256]{1,0:T(8,128)(2,1)S(1)} %bitcast.5, bf16[512,256]{1,0:T(8,128)(2,1)S(1)} %copy-done.2), custom_call_target="tpu_custom_call" | custom-call | flops 12884901888 | bytes 12582912 | tf_op jit(solution)/shard_map/pallas_call | solution.py:206
  23.9 0.0 collective-permute-done.tail_ref
  23.9 3.6 %shard_map.56 = (bf16[128,16,512]{2,1,0:T(8,128)(2,1)S(1)}, bf16[128,16,512]{2,1,0:T(8,128)(2,1)S(1)}) custom-call(s32[8]{0:T(128)S(1)} %copy-done.3, bf16[512,256]{1,0:T(8,128)(2,1)S(1)} %collective-permute-done.tail_ref, bf16[512,8192]{1,0:T(8,128)(2,1)} %rec_ref.3, ...), custom_call_target="tpu_custom_call", output_to_operand_aliasing={{0}: (6, {}), {1}: (7, {})} | custom-call | flops 402653184 | bytes 8388608 | tf_op jit(solution)/shard_map/pallas_call | solution.py:160
  27.5 0.0 copy-start.1
  27.6 52.8 %all_to_all.10.am_ref.bm_ref = bf16[8,8,2,16,512]{4,3,2,1,0:T(8,128)(2,1)} all-to-all(bf16[8,8,2,16,512]{4,3,2,1,0:T(8,128)(2,1)S(1)} %bitcast.3), channel_id=1, replica_groups=mesh['groups'=2,'tm'=8,'pair'=2] {'tm'}, dimensions={0} | all-to-all | bytes 4194304 | tf_op jit(solution)/shard_map/all_to_all | solution.py:310
  80.4 0.0 copy-done.1
  80.4 0.0 copy-start.4
  80.4 3.7 %all-to-all-start = ((bf16[8,8,2,16,512]{4,3,2,1,0:T(8,128)(2,1)}), bf16[8,8,2,16,512]{4,3,2,1,0:T(8,128)(2,1)S(1)}, u32[]{:S(2)}, u32[]{:S(2)}) async-start(bf16[8,8,2,16,512]{4,3,2,1,0:T(8,128)(2,1)} %bitcast.4), calls=%async_computation | async-start | bytes 4194304 | tf_op jit(solution)/shard_map/all_to_all | solution.py:310
  84.1 0.1 collective-permute-start.2
  84.2 47.6 %all-to-all-done.am_ref.bm_ref = bf16[8,8,2,16,512]{4,3,2,1,0:T(8,128)(2,1)S(1)} async-done(((bf16[8,8,2,16,512]{4,3,2,1,0:T(8,128)(2,1)}), bf16[8,8,2,16,512]{4,3,2,1,0:T(8,128)(2,1)S(1)}, u32[]{:S(2)}, u32[]{:S(2)}) %all-to-all-start) | async-done | bytes 2097184 | tf_op jit(solution)/shard_map/all_to_all | solution.py:310
  131.8 0.0 collective-permute-start.1
  131.8 0.0 copy-done.4
  131.8 0.1 copy.13.pb_ref
  131.9 0.0 collective-permute-done.2.ap_ref.bp_ref
  131.9 0.0 copy-start
  131.9 1.6 %copy-done = bf16[8,8,2,16,512]{4,3,2,1,0:T(8,128)(2,1)S(1)} copy-done((bf16[8,8,2,16,512]{4,3,2,1,0:T(8,128)(2,1)S(1)}, bf16[8,8,2,16,512]{4,3,2,1,0:T(8,128)(2,1)}, u32[]{:S(2)}) %copy-start) | copy-done | bytes 2097176
  133.5 9.5 %shard_map.57.rest_0_ = f32[8,16,2,128,128]{4,3,2,1,0:T(8,128)} custom-call(s32[8,2]{1,0:T(8,128)S(1)} %copy.13.pb_ref, s32[8]{0:T(128)S(1)} %copy-done.3, bf16[8,8,2,16,512]{4,3,2,1,0:T(8,128)(2,1)S(1)} %copy-done, bf16[8,8,2,16,512]{4,3,2,1,0:T(8,128)(2,1)} %collective-permute-done.2.ap_ref.bp_ref, bf16[8,8,2,16,512]{4,3,2,1,0:T(8,128)(2,1)S(1)} %copy-done, ...), custom_call_target="tpu_custom_call" | custom-call | flops 1073741824 | bytes 25165824 | tf_op jit(solution)/shard_map/pallas_call | solution.py:283
  143.0 0.0 collective-permute-done.1.ap_ref.bp_ref
  143.0 9.5 %shard_map.58 = f32[8,16,2,128,128]{4,3,2,1,0:T(8,128)} custom-call(s32[8,2]{1,0:T(8,128)S(1)} %copy.13.pb_ref, s32[8]{0:T(128)S(1)} %copy-done.3, bf16[8,8,2,16,512]{4,3,2,1,0:T(8,128)(2,1)S(1)} %all-to-all-done.am_ref.bm_ref, bf16[8,8,2,16,512]{4,3,2,1,0:T(8,128)(2,1)} %collective-permute-done.1.ap_ref.bp_ref, ...), custom_call_target="tpu_custom_call", output_to_operand_aliasing={{}: (6, {})} | custom-call | flops 1073741824 | bytes 25165824 | tf_op jit(solution)/shard_map/pallas_call | solution.py:283
  (3 shorter events, 0.1 us)
Async XLA Ops:
  0.0 7.7 %copy-start.2 = (bf16[512,256]{1,0:T(8,128)(2,1)S(1)}, bf16[512,256]{1,0:T(8,128)(2,1)}, u32[]{:S(2)}) copy-start(bf16[512,256]{1,0:T(8,128)(2,1)} %constant.6.clone.basis_ref) | copy-start | bytes 786436
  0.0 7.7 %copy-start.3 = (s32[8]{0:T(128)S(1)}, s32[8]{0:T(128)}, u32[]{:S(2)}) copy-start(s32[8]{0:T(128)} %kw_ref.3) | copy-start | bytes 100
  1.0 22.9 %collective-permute-start = (bf16[512,256]{1,0:T(8,128)(2,1)S(1)}, bf16[512,256]{1,0:T(8,128)(2,1)S(1)}, u32[]{:S(2)}, u32[]{:S(2)}) collective-permute-start(bf16[512,256]{1,0:T(8,128)(2,1)S(1)} %slice.6), channel_id=1, source_target_pairs={{0,2},{2,4},{4,6},{6,8},{8,10},{10,12},{12,14},{1,3},{3,5},{5,7},{... | collective-permute-start | bytes 786440 | tf_op jit(solution)/shard_map/ppermute | solution.py:25
  27.5 52.8 %copy-start.1 = (bf16[128,16,512]{2,1,0:T(8,128)(2,1)}, bf16[128,16,512]{2,1,0:T(8,128)(2,1)S(1)}, u32[]{:S(2)}) copy-start(bf16[128,16,512]{2,1,0:T(8,128)(2,1)S(1)} %get-tuple-element.13) | copy-start | bytes 6291460
  80.4 51.5 %copy-start.4 = (s32[8,2]{0,1:T(2,128)S(1)}, s32[8,2]{0,1:T(2,128)}, u32[]{:S(2)}) copy-start(s32[8,2]{0,1:T(2,128)} %param.8) | copy-start | bytes 196
  80.4 51.4 %all-to-all-start = ((bf16[8,8,2,16,512]{4,3,2,1,0:T(8,128)(2,1)}), bf16[8,8,2,16,512]{4,3,2,1,0:T(8,128)(2,1)S(1)}, u32[]{:S(2)}, u32[]{:S(2)}) async-start(bf16[8,8,2,16,512]{4,3,2,1,0:T(8,128)(2,1)} %bitcast.4), calls=%async_computation | async-start | bytes 4194304 | tf_op jit(solution)/shard_map/all_to_all | solution.py:310
  84.1 47.8 %collective-permute-start.2 = (bf16[8,8,2,16,512]{4,3,2,1,0:T(8,128)(2,1)}, bf16[8,8,2,16,512]{4,3,2,1,0:T(8,128)(2,1)}, u32[]{:S(2)}, u32[]{:S(2)}) collective-permute-start(bf16[8,8,2,16,512]{4,3,2,1,0:T(8,128)(2,1)} %all_to_all.10.am_ref.bm_ref), channel_id=1, source_target_pairs={{0,1},{1,0},{2,3},{3,2},{4,5},{5,4},{6,7},{7,6},{8,9},{9,8},{10,11... | collective-permute-start | bytes 6291464 | tf_op jit(solution)/shard_map/ppermute | solution.py:311
  131.8 11.1 %collective-permute-start.1 = (bf16[8,8,2,16,512]{4,3,2,1,0:T(8,128)(2,1)S(1)}, bf16[8,8,2,16,512]{4,3,2,1,0:T(8,128)(2,1)}, u32[]{:S(2)}, u32[]{:S(2)}) collective-permute-start(bf16[8,8,2,16,512]{4,3,2,1,0:T(8,128)(2,1)S(1)} %all-to-all-done.am_ref.bm_ref), channel_id=1, source_target_pairs={{0,1},{1,0},{2,3},{3,2},{4,5},{5,4},{6,7},{7,6},{8,9},{9,8},{10,11... | collective-permute-start | bytes 6291464 | tf_op jit(solution)/shard_map/ppermute | solution.py:311
  131.9 1.6 %copy-start = (bf16[8,8,2,16,512]{4,3,2,1,0:T(8,128)(2,1)S(1)}, bf16[8,8,2,16,512]{4,3,2,1,0:T(8,128)(2,1)}, u32[]{:S(2)}) copy-start(bf16[8,8,2,16,512]{4,3,2,1,0:T(8,128)(2,1)} %all_to_all.10.am_ref.bm_ref) | copy-start | bytes 6291460

commit v16 on v15

--- a/solution.py
+++ b/solution.py
@@ -112,40 +112,53 @@
         start += o_ref.shape[0]
 
 
-def first_window_kernel(count_parts, cnt_ref, tail_ref, rec_ref, f1_ref, toep_ref, basis_ref, *rest):
+def first_window_kernel(count_parts, part_rows, cnt_ref, tail_ref, rec_ref, f1_ref, toep_ref, basis_ref, *rest):
     ins, outs, w0_ref = rest[:count_parts], rest[count_parts : 2 * count_parts], rest[-1]
     bins2 = basis_ref.shape[1]
-    count = cnt_ref[lax.axis_index("tm")]
-    ext0 = jnp.concatenate([tail_ref[...], rec_ref[...]], axis=1)
-    f0 = jnp.dot(ext0, toep_ref[...], preferred_element_type=jnp.float32).astype(jnp.bfloat16)
-    spec = jnp.dot(
-        jnp.concatenate([f0, f1_ref[...]], axis=1), basis_ref[...], preferred_element_type=jnp.float32
-    ).T
-    power = jnp.sum(spec * spec, axis=0, keepdims=True) * (1.0 / bins2)
-    keep = jnp.where(count > 0, 1.0, 0.0).astype(jnp.float32)
-    w0_ref[...] = spec * (lax.rsqrt(power + whiten_eps) * keep)
+    step = pl.program_id(0)
+
+    @pl.when(step == 0)
+    def _():
+        count = cnt_ref[lax.axis_index("tm")]
+        ext0 = jnp.concatenate([tail_ref[...], rec_ref[...]], axis=1)
+        f0 = jnp.dot(ext0, toep_ref[...], preferred_element_type=jnp.float32).astype(jnp.bfloat16)
+        spec = jnp.dot(
+            jnp.concatenate([f0, f1_ref[...]], axis=1),
+            basis_ref[...],
+            preferred_element_type=jnp.float32,
+        ).T
+        power = jnp.sum(spec * spec, axis=0, keepdims=True) * (1.0 / bins2)
+        keep = jnp.where(count > 0, 1.0, 0.0).astype(jnp.float32)
+        w0_ref[...] = spec * (lax.rsqrt(power + whiten_eps) * keep)
+
     start = 0
-    for i_ref, o_ref in zip(ins, outs):
-
-        def one_row(k, carry, i_ref=i_ref, o_ref=o_ref, start=start):
+    for i_ref, o_ref, total in zip(ins, outs, part_rows):
+        base = start + step * o_ref.shape[0]
+
+        def one_row(k, carry, i_ref=i_ref, o_ref=o_ref, base=base):
             held = i_ref[k]
-            first = w0_ref[pl.ds(start + k, 1), :].astype(held.dtype)
+            first = w0_ref[pl.ds(base + k, 1), :].astype(held.dtype)
             rowid = lax.broadcasted_iota(jnp.int32, held.shape, 0)
             o_ref[k] = jnp.where(rowid == 0, first, held)
             return carry
 
         lax.fori_loop(0, o_ref.shape[0], one_row, 0, unroll=8)
-        start += o_ref.shape[0]
+        start += total
 
 
 def fill_first_window(parts, recording, tail_rows, f1, toep, basis, kept_count):
     channels, width = tail_rows.shape
     bins2 = basis.shape[1]
     count_parts = len(parts)
+    part_rows = tuple(p.shape[0] for p in parts)
+    steps = 4
+    for r in part_rows:
+        steps = math.gcd(steps, r)
     full = lambda shape: pl.BlockSpec(shape, lambda i, c: (0,) * len(shape))
+    piece = lambda p: pl.BlockSpec((p.shape[0] // steps,) + p.shape[1:], lambda i, c: (i, 0, 0))
     grid_spec = pltpu.PrefetchScalarGridSpec(
         num_scalar_prefetch=1,
-        grid=(1,),
+        grid=(steps,),
         in_specs=[
             full(tail_rows.shape),
             pl.BlockSpec((channels, width), lambda i, c: (0, 0)),
@@ -153,12 +166,12 @@
             full(toep.shape),
             full(basis.shape),
         ]
-        + [full(p.shape) for p in parts],
-        out_specs=[full(p.shape) for p in parts],
+        + [piece(p) for p in parts],
+        out_specs=[piece(p) for p in parts],
         scratch_shapes=[pltpu.VMEM((bins2, channels), jnp.float32)],
     )
     return pl.pallas_call(
-        functools.partial(first_window_kernel, count_parts),
+        functools.partial(first_window_kernel, count_parts, part_rows),
         grid_spec=grid_spec,
         out_shape=[jax.ShapeDtypeStruct(p.shape, p.dtype) for p in parts],
         input_output_aliases={6 + i: i for i in range(count_parts)},

time: 155 us -> 155 us (level)
  no operation moved by 1% of the time
where the time goes in v16:
time: 155 us; the launch traced here: 154 us
  blocking collectives  52.8 us (34%)
  waiting for transfers between devices  47.6 us (31%)
  Pallas kernels  40.1 us (26%)
  starting transfers between devices  8.7 us (6%)
  local copies, waits for them, and re-layouts  4.41 us (3%)
    all_to_all x1, blocking collectives, per_device(): lax.all_to_all(outgoing, 'tm', split_axis=0, concat_axis=0, tiled=True)  52.8 us
    all_to_all x1, waiting for transfers between devices, per_device(): lax.all_to_all(outgoing, 'tm', split_axis=0, concat_axis=0, tiled=True)  47.6 us
    pallas_call x2, Pallas kernels, stack_pairs(): pl.pallas_call(functools.partial(stack_kernel_for, blocks_per_half), grid...  20.3 us
    pallas_call x1, Pallas kernels, whiten_front(): pl.pallas_call(front_kernel, grid_spec=grid_spec, out_shape=[jax.ShapeDty...  16.2 us
    ppermute x1, starting transfers between devices, from_behind(): return lax.ppermute(array, axis, pairs)  4.89 us
    all_to_all x1, starting transfers between devices, per_device(): lax.all_to_all(outgoing, 'tm', split_axis=0, concat_axis=0, tiled=True)  3.74 us
    pallas_call x1, Pallas kernels, fill_first_window(): pl.pallas_call(functools.partial(first_window_kernel, count_parts, part_r...  3.7 us
  transfers between devices with their start and end apart: 4, of which 1 were waited for; matrix products, arithmetic and copies ran while one was open for 1% of the time, Pallas kernels for 17%

profile of v16, /device:TPU:0, one launch (start us, length us, event | category | flops | bytes accessed | tf_op | source)
XLA Modules:
  0.0 153.9 jit_solution(11625496143153815264)
XLA Ops:
  0.0 0.0 copy-start.2
  0.0 0.0 copy-start.3
  0.0 1.0 slice.6
  1.0 4.9 %collective-permute-start = (bf16[512,256]{1,0:T(8,128)(2,1)S(1)}, bf16[512,256]{1,0:T(8,128)(2,1)S(1)}, u32[]{:S(2)}, u32[]{:S(2)}) collective-permute-start(bf16[512,256]{1,0:T(8,128)(2,1)S(1)} %slice.6), channel_id=1, source_target_pairs={{0,2},{2,4},{4,6},{6,8},{8,10},{10,12},{12,14},{1,3},{3,5},{5,7},{... | collective-permute-start | bytes 786440 | tf_op jit(solution)/shard_map/ppermute | solution.py:25
  5.9 0.7 rev.3
  6.7 0.1 pad_maximum_fusion
  6.8 0.6 tile.10
  7.4 0.2 reshape.10
  7.6 0.1 copy.11
  7.7 0.0 copy-done.2
  7.7 0.0 copy-done.3
  7.7 16.2 %shard_map.55 = (bf16[128,16,512]{2,1,0:T(8,128)(2,1)S(1)}, bf16[128,16,512]{2,1,0:T(8,128)(2,1)S(1)}, bf16[512,256]{1,0:T(8,128)(2,1)S(1)}) custom-call(s32[8]{0:T(128)S(1)} %copy-done.3, bf16[512,8192]{1,0:T(8,128)(2,1)} %rec_ref.3, bf16[512,256]{1,0:T(8,128)(2,1)S(1)} %bitcast.5, bf16[512,256]{1,0:T(8,128)(2,1)S(1)} %copy-done.2), custom_call_target="tpu_custom_call" | custom-call | flops 12884901888 | bytes 12582912 | tf_op jit(solution)/shard_map/pallas_call | solution.py:219
  23.9 0.0 collective-permute-done.tail_ref
  23.9 3.7 %shard_map.56 = (bf16[128,16,512]{2,1,0:T(8,128)(2,1)S(1)}, bf16[128,16,512]{2,1,0:T(8,128)(2,1)S(1)}) custom-call(s32[8]{0:T(128)S(1)} %copy-done.3, bf16[512,256]{1,0:T(8,128)(2,1)S(1)} %collective-permute-done.tail_ref, bf16[512,8192]{1,0:T(8,128)(2,1)} %rec_ref.3, ...), custom_call_target="tpu_custom_call", output_to_operand_aliasing={{0}: (6, {}), {1}: (7, {})} | custom-call | flops 402653184 | bytes 8388608 | tf_op jit(solution)/shard_map/pallas_call | solution.py:173
  27.7 0.0 copy-start.1
  27.7 52.8 %all_to_all.10.am_ref.bm_ref = bf16[8,8,2,16,512]{4,3,2,1,0:T(8,128)(2,1)} all-to-all(bf16[8,8,2,16,512]{4,3,2,1,0:T(8,128)(2,1)S(1)} %bitcast.3), channel_id=1, replica_groups=mesh['groups'=2,'tm'=8,'pair'=2] {'tm'}, dimensions={0} | all-to-all | bytes 4194304 | tf_op jit(solution)/shard_map/all_to_all | solution.py:323
  80.5 0.0 copy-done.1
  80.5 0.0 copy-start.4
  80.5 3.7 %all-to-all-start = ((bf16[8,8,2,16,512]{4,3,2,1,0:T(8,128)(2,1)}), bf16[8,8,2,16,512]{4,3,2,1,0:T(8,128)(2,1)S(1)}, u32[]{:S(2)}, u32[]{:S(2)}) async-start(bf16[8,8,2,16,512]{4,3,2,1,0:T(8,128)(2,1)} %bitcast.4), calls=%async_computation | async-start | bytes 4194304 | tf_op jit(solution)/shard_map/all_to_all | solution.py:323
  84.2 0.1 collective-permute-start.2
  84.3 47.6 %all-to-all-done.am_ref.bm_ref = bf16[8,8,2,16,512]{4,3,2,1,0:T(8,128)(2,1)S(1)} async-done(((bf16[8,8,2,16,512]{4,3,2,1,0:T(8,128)(2,1)}), bf16[8,8,2,16,512]{4,3,2,1,0:T(8,128)(2,1)S(1)}, u32[]{:S(2)}, u32[]{:S(2)}) %all-to-all-start) | async-done | bytes 2097184 | tf_op jit(solution)/shard_map/all_to_all | solution.py:323
  131.9 0.0 collective-permute-start.1
  131.9 0.0 copy-done.4
  131.9 0.1 copy.13.pb_ref
  132.0 0.0 collective-permute-done.2.ap_ref.bp_ref
  132.0 0.0 copy-start
  132.0 1.6 %copy-done = bf16[8,8,2,16,512]{4,3,2,1,0:T(8,128)(2,1)S(1)} copy-done((bf16[8,8,2,16,512]{4,3,2,1,0:T(8,128)(2,1)S(1)}, bf16[8,8,2,16,512]{4,3,2,1,0:T(8,128)(2,1)}, u32[]{:S(2)}) %copy-start) | copy-done | bytes 2097176
  133.6 10.1 %shard_map.57.rest_0_ = f32[8,16,2,128,128]{4,3,2,1,0:T(8,128)} custom-call(s32[8,2]{1,0:T(8,128)S(1)} %copy.13.pb_ref, s32[8]{0:T(128)S(1)} %copy-done.3, bf16[8,8,2,16,512]{4,3,2,1,0:T(8,128)(2,1)S(1)} %copy-done, bf16[8,8,2,16,512]{4,3,2,1,0:T(8,128)(2,1)} %collective-permute-done.2.ap_ref.bp_ref, bf16[8,8,2,16,512]{4,3,2,1,0:T(8,128)(2,1)S(1)} %copy-done, ...), custom_call_target="tpu_custom_call" | custom-call | flops 1073741824 | bytes 25165824 | tf_op jit(solution)/shard_map/pallas_call | solution.py:296
  143.7 0.0 collective-permute-done.1.ap_ref.bp_ref
  143.7 10.1 %shard_map.58 = f32[8,16,2,128,128]{4,3,2,1,0:T(8,128)} custom-call(s32[8,2]{1,0:T(8,128)S(1)} %copy.13.pb_ref, s32[8]{0:T(128)S(1)} %copy-done.3, bf16[8,8,2,16,512]{4,3,2,1,0:T(8,128)(2,1)S(1)} %all-to-all-done.am_ref.bm_ref, bf16[8,8,2,16,512]{4,3,2,1,0:T(8,128)(2,1)} %collective-permute-done.1.ap_ref.bp_ref, ...), custom_call_target="tpu_custom_call", output_to_operand_aliasing={{}: (6, {})} | custom-call | flops 1073741824 | bytes 25165824 | tf_op jit(solution)/shard_map/pallas_call | solution.py:296
  (3 shorter events, 0.1 us)
Async XLA Ops:
  0.0 7.7 %copy-start.2 = (bf16[512,256]{1,0:T(8,128)(2,1)S(1)}, bf16[512,256]{1,0:T(8,128)(2,1)}, u32[]{:S(2)}) copy-start(bf16[512,256]{1,0:T(8,128)(2,1)} %constant.6.clone.basis_ref) | copy-start | bytes 786436
  0.0 7.7 %copy-start.3 = (s32[8]{0:T(128)S(1)}, s32[8]{0:T(128)}, u32[]{:S(2)}) copy-start(s32[8]{0:T(128)} %kw_ref.3) | copy-start | bytes 100
  1.0 22.9 %collective-permute-start = (bf16[512,256]{1,0:T(8,128)(2,1)S(1)}, bf16[512,256]{1,0:T(8,128)(2,1)S(1)}, u32[]{:S(2)}, u32[]{:S(2)}) collective-permute-start(bf16[512,256]{1,0:T(8,128)(2,1)S(1)} %slice.6), channel_id=1, source_target_pairs={{0,2},{2,4},{4,6},{6,8},{8,10},{10,12},{12,14},{1,3},{3,5},{5,7},{... | collective-permute-start | bytes 786440 | tf_op jit(solution)/shard_map/ppermute | solution.py:25
  27.7 52.8 %copy-start.1 = (bf16[128,16,512]{2,1,0:T(8,128)(2,1)}, bf16[128,16,512]{2,1,0:T(8,128)(2,1)S(1)}, u32[]{:S(2)}) copy-start(bf16[128,16,512]{2,1,0:T(8,128)(2,1)S(1)} %get-tuple-element.13) | copy-start | bytes 6291460
  80.5 51.5 %copy-start.4 = (s32[8,2]{0,1:T(2,128)S(1)}, s32[8,2]{0,1:T(2,128)}, u32[]{:S(2)}) copy-start(s32[8,2]{0,1:T(2,128)} %param.8) | copy-start | bytes 196
  80.5 51.4 %all-to-all-start = ((bf16[8,8,2,16,512]{4,3,2,1,0:T(8,128)(2,1)}), bf16[8,8,2,16,512]{4,3,2,1,0:T(8,128)(2,1)S(1)}, u32[]{:S(2)}, u32[]{:S(2)}) async-start(bf16[8,8,2,16,512]{4,3,2,1,0:T(8,128)(2,1)} %bitcast.4), calls=%async_computation | async-start | bytes 4194304 | tf_op jit(solution)/shard_map/all_to_all | solution.py:323
  84.2 47.8 %collective-permute-start.2 = (bf16[8,8,2,16,512]{4,3,2,1,0:T(8,128)(2,1)}, bf16[8,8,2,16,512]{4,3,2,1,0:T(8,128)(2,1)}, u32[]{:S(2)}, u32[]{:S(2)}) collective-permute-start(bf16[8,8,2,16,512]{4,3,2,1,0:T(8,128)(2,1)} %all_to_all.10.am_ref.bm_ref), channel_id=1, source_target_pairs={{0,1},{1,0},{2,3},{3,2},{4,5},{5,4},{6,7},{7,6},{8,9},{9,8},{10,11... | collective-permute-start | bytes 6291464 | tf_op jit(solution)/shard_map/ppermute | solution.py:324
  131.9 11.8 %collective-permute-start.1 = (bf16[8,8,2,16,512]{4,3,2,1,0:T(8,128)(2,1)S(1)}, bf16[8,8,2,16,512]{4,3,2,1,0:T(8,128)(2,1)}, u32[]{:S(2)}, u32[]{:S(2)}) collective-permute-start(bf16[8,8,2,16,512]{4,3,2,1,0:T(8,128)(2,1)S(1)} %all-to-all-done.am_ref.bm_ref), channel_id=1, source_target_pairs={{0,1},{1,0},{2,3},{3,2},{4,5},{5,4},{6,7},{7,6},{8,9},{9,8},{10,11... | collective-permute-start | bytes 6291464 | tf_op jit(solution)/shard_map/ppermute | solution.py:324
  132.0 1.6 %copy-start = (bf16[8,8,2,16,512]{4,3,2,1,0:T(8,128)(2,1)S(1)}, bf16[8,8,2,16,512]{4,3,2,1,0:T(8,128)(2,1)}, u32[]{:S(2)}) copy-start(bf16[8,8,2,16,512]{4,3,2,1,0:T(8,128)(2,1)} %all_to_all.10.am_ref.bm_ref) | copy-start | bytes 6291460

commit v17 on v15

--- a/solution.py
+++ b/solution.py
@@ -173,9 +173,9 @@
     )(kept_count, tail_rows, recording, f1, toep, basis, *parts)
 
 
-def whiten_front(recording, tail_rows, fir_taps, kept_count, chunks, tile=512):
+def whiten_front(recording, fir_taps, kept_count, chunks, tile=512):
     channels, length = recording.shape
-    width = tail_rows.shape[1]
+    width = fir_taps.shape[0]
     windows = length // WIN
     toep = toeplitz(fir_taps)
     sections = lax.axis_size("tm")
@@ -217,6 +217,8 @@
             transcendentals=channels * windows,
         ),
     )(kept_count, recording, toep, basis)
+    tail_source, f1 = lax.optimization_barrier((recording[:, length - width :], f1))
+    tail_rows = from_behind(tail_source, "tm", 1)
     return fill_first_window(parts, recording, tail_rows, f1, toep, basis, kept_count)
 
 
@@ -298,12 +300,11 @@
     channels, length = recording.shape
     width = fir_taps.shape[0]
     sections = lax.axis_size("tm")
-    tail_rows = from_behind(recording[:, length - width :], "tm", 1)
     windows_dev = length // WIN
     bins_dev = NF // sections
     small = max(bins_dev // 2, 1)
     chunks = [0, bins_dev - small, bins_dev] if bins_dev > 1 else [0, bins_dev]
-    whitened = whiten_front(recording, tail_rows, fir_taps, kept_windows, chunks)
+    whitened = whiten_front(recording, fir_taps, kept_windows, chunks)
     result = None
     for lo, hi, part in zip(chunks[:-1], chunks[1:], whitened):
         outgoing = part.reshape(sections, hi - lo, 2, windows_dev, channels)

time: 155 us -> 162 us (1.045)
  waiting for transfers between devices: 47.6 us -> 53.1 us
    ppermute x1, waiting for transfers between devices: 0.01 us -> 5.53 us  [from_behind(): return lax.ppermute(array, axis, pairs)]
  transfers between devices with their start and end apart: 4 -> 4, of which waited for: 1 -> 2; matrix products, arithmetic and copies ran while one was open for 1% -> 0% of each run, Pallas kernels for 17% -> 6%
where the time goes in v17:
time: 162 us; the launch traced here: 161 us
  blocking collectives  54.2 us (33%)
  waiting for transfers between devices  53.1 us (33%)
  Pallas kernels  40.3 us (25%)
  starting transfers between devices  8.7 us (5%)
  local copies, waits for them, and re-layouts  4.41 us (3%)
    all_to_all x1, blocking collectives, per_device(): lax.all_to_all(outgoing, 'tm', split_axis=0, concat_axis=0, tiled=True)  54.2 us
    all_to_all x1, waiting for transfers between devices, per_device(): lax.all_to_all(outgoing, 'tm', split_axis=0, concat_axis=0, tiled=True)  47.6 us
    pallas_call x2, Pallas kernels, stack_pairs(): pl.pallas_call(functools.partial(stack_kernel_for, blocks_per_half), grid...  20.5 us
    pallas_call x1, Pallas kernels, whiten_front(): pl.pallas_call(front_kernel, grid_spec=grid_spec, out_shape=[jax.ShapeDty...  16.2 us
    ppermute x1, waiting for transfers between devices, from_behind(): return lax.ppermute(array, axis, pairs)  5.53 us
    ppermute x1, starting transfers between devices, from_behind(): return lax.ppermute(array, axis, pairs)  4.89 us
    all_to_all x1, starting transfers between devices, per_device(): lax.all_to_all(outgoing, 'tm', split_axis=0, concat_axis=0, tiled=True)  3.74 us
    pallas_call x1, Pallas kernels, fill_first_window(): pl.pallas_call(functools.partial(first_window_kernel, count_parts), grid_...  3.59 us
  transfers between devices with their start and end apart: 4, of which 2 were waited for; matrix products, arithmetic and copies ran while one was open for 0% of the time, Pallas kernels for 6%

profile of v17, /device:TPU:0, one launch (start us, length us, event | category | flops | bytes accessed | tf_op | source)
XLA Modules:
  0.0 160.8 jit_solution(3578962352459393935)
XLA Ops:
  0.0 0.0 copy-start.2
  0.0 0.0 copy-start.3
  0.0 0.8 rev.3
  0.8 1.0 slice.6
  1.8 0.1 pad_maximum_fusion
  1.9 0.6 tile.10
  2.5 0.2 reshape.10
  2.7 0.1 copy.11
  2.8 0.0 copy-done.2
  2.9 0.0 copy-done.3
  2.9 16.2 %shard_map.55 = (bf16[128,16,512]{2,1,0:T(8,128)(2,1)S(1)}, bf16[128,16,512]{2,1,0:T(8,128)(2,1)S(1)}, bf16[512,256]{1,0:T(8,128)(2,1)S(1)}) custom-call(s32[8]{0:T(128)S(1)} %copy-done.3, bf16[512,8192]{1,0:T(8,128)(2,1)} %rec_ref.3, bf16[512,256]{1,0:T(8,128)(2,1)S(1)} %bitcast.5, bf16[512,256]{1,0:T(8,128)(2,1)S(1)} %copy-done.2), custom_call_target="tpu_custom_call" | custom-call | flops 12884901888 | bytes 12582912 | tf_op jit(solution)/shard_map/pallas_call | solution.py:206
  19.1 4.9 %collective-permute-start = (bf16[512,256]{1,0:T(8,128)(2,1)S(1)}, bf16[512,256]{1,0:T(8,128)(2,1)S(1)}, u32[]{:S(2)}, u32[]{:S(2)}) collective-permute-start(bf16[512,256]{1,0:T(8,128)(2,1)S(1)} %slice.6), channel_id=1, source_target_pairs={{0,2},{2,4},{4,6},{6,8},{8,10},{10,12},{12,14},{1,3},{3,5},{5,7},{... | collective-permute-start | bytes 786440 | tf_op jit(solution)/shard_map/ppermute | solution.py:25
  24.0 5.5 %collective-permute-done.tail_ref = bf16[512,256]{1,0:T(8,128)(2,1)S(1)} collective-permute-done((bf16[512,256]{1,0:T(8,128)(2,1)S(1)}, bf16[512,256]{1,0:T(8,128)(2,1)S(1)}, u32[]{:S(2)}, u32[]{:S(2)}) %collective-permute-start) | collective-permute-done | bytes 262176 | tf_op jit(solution)/shard_map/ppermute | solution.py:25
  29.5 3.6 %shard_map.56 = (bf16[128,16,512]{2,1,0:T(8,128)(2,1)S(1)}, bf16[128,16,512]{2,1,0:T(8,128)(2,1)S(1)}) custom-call(s32[8]{0:T(128)S(1)} %copy-done.3, bf16[512,256]{1,0:T(8,128)(2,1)S(1)} %collective-permute-done.tail_ref, bf16[512,8192]{1,0:T(8,128)(2,1)} %rec_ref.3, ...), custom_call_target="tpu_custom_call", output_to_operand_aliasing={{0}: (6, {}), {1}: (7, {})} | custom-call | flops 402653184 | bytes 8388608 | tf_op jit(solution)/shard_map/pallas_call | solution.py:160
  33.1 0.0 copy-start.1
  33.1 54.2 %all_to_all.10.am_ref.bm_ref = bf16[8,8,2,16,512]{4,3,2,1,0:T(8,128)(2,1)} all-to-all(bf16[8,8,2,16,512]{4,3,2,1,0:T(8,128)(2,1)S(1)} %bitcast.3), channel_id=1, replica_groups=mesh['groups'=2,'tm'=8,'pair'=2] {'tm'}, dimensions={0} | all-to-all | bytes 4194304 | tf_op jit(solution)/shard_map/all_to_all | solution.py:311
  87.3 0.0 copy-done.1
  87.3 0.0 copy-start.4
  87.3 3.7 %all-to-all-start = ((bf16[8,8,2,16,512]{4,3,2,1,0:T(8,128)(2,1)}), bf16[8,8,2,16,512]{4,3,2,1,0:T(8,128)(2,1)S(1)}, u32[]{:S(2)}, u32[]{:S(2)}) async-start(bf16[8,8,2,16,512]{4,3,2,1,0:T(8,128)(2,1)} %bitcast.4), calls=%async_computation | async-start | bytes 4194304 | tf_op jit(solution)/shard_map/all_to_all | solution.py:311
  91.0 0.1 collective-permute-start.2
  91.1 47.6 %all-to-all-done.am_ref.bm_ref = bf16[8,8,2,16,512]{4,3,2,1,0:T(8,128)(2,1)S(1)} async-done(((bf16[8,8,2,16,512]{4,3,2,1,0:T(8,128)(2,1)}), bf16[8,8,2,16,512]{4,3,2,1,0:T(8,128)(2,1)S(1)}, u32[]{:S(2)}, u32[]{:S(2)}) %all-to-all-start) | async-done | bytes 2097184 | tf_op jit(solution)/shard_map/all_to_all | solution.py:311
  138.7 0.0 collective-permute-start.1
  138.7 0.0 copy-done.4
  138.7 0.1 copy.13.pb_ref
  138.8 0.0 collective-permute-done.2.ap_ref.bp_ref
  138.8 0.0 copy-start
  138.8 1.6 copy-done
  140.4 10.2 %shard_map.57.rest_0_ = f32[8,16,2,128,128]{4,3,2,1,0:T(8,128)} custom-call(s32[8,2]{1,0:T(8,128)S(1)} %copy.13.pb_ref, s32[8]{0:T(128)S(1)} %copy-done.3, bf16[8,8,2,16,512]{4,3,2,1,0:T(8,128)(2,1)S(1)} %copy-done, bf16[8,8,2,16,512]{4,3,2,1,0:T(8,128)(2,1)} %collective-permute-done.2.ap_ref.bp_ref, bf16[8,8,2,16,512]{4,3,2,1,0:T(8,128)(2,1)S(1)} %copy-done, ...), custom_call_target="tpu_custom_call" | custom-call | flops 1073741824 | bytes 25165824 | tf_op jit(solution)/shard_map/pallas_call | solution.py:285
  150.6 0.0 collective-permute-done.1.ap_ref.bp_ref
  150.6 10.2 %shard_map.58 = f32[8,16,2,128,128]{4,3,2,1,0:T(8,128)} custom-call(s32[8,2]{1,0:T(8,128)S(1)} %copy.13.pb_ref, s32[8]{0:T(128)S(1)} %copy-done.3, bf16[8,8,2,16,512]{4,3,2,1,0:T(8,128)(2,1)S(1)} %all-to-all-done.am_ref.bm_ref, bf16[8,8,2,16,512]{4,3,2,1,0:T(8,128)(2,1)} %collective-permute-done.1.ap_ref.bp_ref, ...), custom_call_target="tpu_custom_call", output_to_operand_aliasing={{}: (6, {})} | custom-call | flops 1073741824 | bytes 25165824 | tf_op jit(solution)/shard_map/pallas_call | solution.py:285
  (3 shorter events, 0.1 us)
Async XLA Ops:
  0.0 2.8 %copy-start.2 = (bf16[512,256]{1,0:T(8,128)(2,1)S(1)}, bf16[512,256]{1,0:T(8,128)(2,1)}, u32[]{:S(2)}) copy-start(bf16[512,256]{1,0:T(8,128)(2,1)} %constant.6.clone.basis_ref) | copy-start | bytes 786436
  0.0 2.9 %copy-start.3 = (s32[8]{0:T(128)S(1)}, s32[8]{0:T(128)}, u32[]{:S(2)}) copy-start(s32[8]{0:T(128)} %kw_ref.3) | copy-start | bytes 100
  19.1 10.4 %collective-permute-start = (bf16[512,256]{1,0:T(8,128)(2,1)S(1)}, bf16[512,256]{1,0:T(8,128)(2,1)S(1)}, u32[]{:S(2)}, u32[]{:S(2)}) collective-permute-start(bf16[512,256]{1,0:T(8,128)(2,1)S(1)} %slice.6), channel_id=1, source_target_pairs={{0,2},{2,4},{4,6},{6,8},{8,10},{10,12},{12,14},{1,3},{3,5},{5,7},{... | collective-permute-start | bytes 786440 | tf_op jit(solution)/shard_map/ppermute | solution.py:25
  33.1 54.2 %copy-start.1 = (bf16[128,16,512]{2,1,0:T(8,128)(2,1)}, bf16[128,16,512]{2,1,0:T(8,128)(2,1)S(1)}, u32[]{:S(2)}) copy-start(bf16[128,16,512]{2,1,0:T(8,128)(2,1)S(1)} %get-tuple-element.17) | copy-start | bytes 6291460
  87.3 51.4 %copy-start.4 = (s32[8,2]{0,1:T(2,128)S(1)}, s32[8,2]{0,1:T(2,128)}, u32[]{:S(2)}) copy-start(s32[8,2]{0,1:T(2,128)} %param.8) | copy-start | bytes 196
  87.3 51.4 %all-to-all-start = ((bf16[8,8,2,16,512]{4,3,2,1,0:T(8,128)(2,1)}), bf16[8,8,2,16,512]{4,3,2,1,0:T(8,128)(2,1)S(1)}, u32[]{:S(2)}, u32[]{:S(2)}) async-start(bf16[8,8,2,16,512]{4,3,2,1,0:T(8,128)(2,1)} %bitcast.4), calls=%async_computation | async-start | bytes 4194304 | tf_op jit(solution)/shard_map/all_to_all | solution.py:311
  91.0 47.7 %collective-permute-start.2 = (bf16[8,8,2,16,512]{4,3,2,1,0:T(8,128)(2,1)}, bf16[8,8,2,16,512]{4,3,2,1,0:T(8,128)(2,1)}, u32[]{:S(2)}, u32[]{:S(2)}) collective-permute-start(bf16[8,8,2,16,512]{4,3,2,1,0:T(8,128)(2,1)} %all_to_all.10.am_ref.bm_ref), channel_id=1, source_target_pairs={{0,1},{1,0},{2,3},{3,2},{4,5},{5,4},{6,7},{7,6},{8,9},{9,8},{10,11... | collective-permute-start | bytes 6291464 | tf_op jit(solution)/shard_map/ppermute | solution.py:312
  138.7 11.9 %collective-permute-start.1 = (bf16[8,8,2,16,512]{4,3,2,1,0:T(8,128)(2,1)S(1)}, bf16[8,8,2,16,512]{4,3,2,1,0:T(8,128)(2,1)}, u32[]{:S(2)}, u32[]{:S(2)}) collective-permute-start(bf16[8,8,2,16,512]{4,3,2,1,0:T(8,128)(2,1)S(1)} %all-to-all-done.am_ref.bm_ref), channel_id=1, source_target_pairs={{0,1},{1,0},{2,3},{3,2},{4,5},{5,4},{6,7},{7,6},{8,9},{9,8},{10,11... | collective-permute-start | bytes 6291464 | tf_op jit(solution)/shard_map/ppermute | solution.py:312
  138.8 1.6 copy-start

commit v18 on v15

--- a/solution.py
+++ b/solution.py
@@ -68,13 +68,23 @@
     return basis_table.reshape(length, 2 * bins).astype(ml_dtypes.bfloat16)
 
 
+def build_toeplitz(taps_ref):
+    width = taps_ref.shape[1]
+    row = jnp.concatenate(
+        [taps_ref[...].astype(jnp.float32), jnp.zeros((1, width), jnp.float32)], axis=1
+    )
+    grid = jnp.broadcast_to(row, (2 * width, 2 * width))
+    rolled = pltpu.roll(grid, width, 1, stride=1, stride_axis=0)
+    return rolled[:, :width].astype(jnp.bfloat16)
+
+
 def front_kernel(cnt_ref, rec_ref, toep_ref, basis_ref, *rest):
     outs, f1_ref, (scr_ref, inv_ref) = rest[:-3], rest[-3], rest[-2:]
     tile, length = rec_ref.shape
     width = toep_ref.shape[1]
     bins2 = basis_ref.shape[1]
     windows = length // WIN
-    toep = toep_ref[...]
+    toep = build_toeplitz(toep_ref)
     basis = basis_ref[...]
     count = cnt_ref[lax.axis_index("tm")]
     f1_ref[...] = jnp.dot(
@@ -117,7 +127,9 @@
     bins2 = basis_ref.shape[1]
     count = cnt_ref[lax.axis_index("tm")]
     ext0 = jnp.concatenate([tail_ref[...], rec_ref[...]], axis=1)
-    f0 = jnp.dot(ext0, toep_ref[...], preferred_element_type=jnp.float32).astype(jnp.bfloat16)
+    f0 = jnp.dot(ext0, build_toeplitz(toep_ref), preferred_element_type=jnp.float32).astype(
+        jnp.bfloat16
+    )
     spec = jnp.dot(
         jnp.concatenate([f0, f1_ref[...]], axis=1), basis_ref[...], preferred_element_type=jnp.float32
     ).T
@@ -177,7 +189,7 @@
     channels, length = recording.shape
     width = tail_rows.shape[1]
     windows = length // WIN
-    toep = toeplitz(fir_taps)
+    toep = fir_taps.reshape(1, -1)
     sections = lax.axis_size("tm")
     bins_dev = NF // sections
     basis = dft_table(WIN, NF, FLO).reshape(WIN, sections, bins_dev, 2)

time: 155 us -> 155 us (level)
    unnamed x11 -> x13, local copies, waits for them, and re-layouts: 1.69 us -> 3.29 us
  transfers between devices with their start and end apart: 4 -> 4, of which waited for: 1 -> 1; matrix products, arithmetic and copies ran while one was open for 1% -> 0% of each run, Pallas kernels for 17% -> 17%
where the time goes in v18:
time: 155 us; the launch traced here: 154 us
  blocking collectives  52.8 us (34%)
  waiting for transfers between devices  47.6 us (31%)
  Pallas kernels  39.7 us (26%)
  starting transfers between devices  8.7 us (6%)
  local copies, waits for them, and re-layouts  4.92 us (3%)
    all_to_all x1, blocking collectives, per_device(): lax.all_to_all(outgoing, 'tm', split_axis=0, concat_axis=0, tiled=True)  52.8 us
    all_to_all x1, waiting for transfers between devices, per_device(): lax.all_to_all(outgoing, 'tm', split_axis=0, concat_axis=0, tiled=True)  47.6 us
    pallas_call x2, Pallas kernels, stack_pairs(): pl.pallas_call(functools.partial(stack_kernel_for, blocks_per_half), grid...  19.8 us
    pallas_call x1, Pallas kernels, whiten_front(): pl.pallas_call(front_kernel, grid_spec=grid_spec, out_shape=[jax.ShapeDty...  16.2 us
    ppermute x1, starting transfers between devices, from_behind(): return lax.ppermute(array, axis, pairs)  4.89 us
    all_to_all x1, starting transfers between devices, per_device(): lax.all_to_all(outgoing, 'tm', split_axis=0, concat_axis=0, tiled=True)  3.74 us
    pallas_call x1, Pallas kernels, fill_first_window(): pl.pallas_call(functools.partial(first_window_kernel, count_parts), grid_...  3.67 us
    unnamed x13, local copies, waits for them, and re-layouts  3.29 us
  transfers between devices with their start and end apart: 4, of which 1 were waited for; matrix products, arithmetic and copies ran while one was open for 0% of the time, Pallas kernels for 17%

profile of v18, /device:TPU:0, one launch (start us, length us, event | category | flops | bytes accessed | tf_op | source)
XLA Modules:
  0.0 153.8 jit_solution(15112110581108492563)
XLA Ops:
  0.0 1.0 slice.3
  1.0 4.9 %collective-permute-start = (bf16[512,256]{1,0:T(8,128)(2,1)S(1)}, bf16[512,256]{1,0:T(8,128)(2,1)S(1)}, u32[]{:S(2)}, u32[]{:S(2)}) collective-permute-start(bf16[512,256]{1,0:T(8,128)(2,1)S(1)} %slice.3), channel_id=1, source_target_pairs={{0,2},{2,4},{4,6},{6,8},{8,10},{10,12},{12,14},{1,3},{3,5},{5,7},{... | collective-permute-start | bytes 786440 | tf_op jit(solution)/shard_map/ppermute | solution.py:25
  5.9 0.7 reshape.9.toep_ref
  6.5 0.0 copy-start.2
  6.5 0.9 copy-done.2
  7.5 0.0 copy-start.3
  7.5 0.7 copy-done.3
  8.1 16.2 %shard_map.55 = (bf16[128,16,512]{2,1,0:T(8,128)(2,1)S(1)}, bf16[128,16,512]{2,1,0:T(8,128)(2,1)S(1)}, bf16[512,256]{1,0:T(8,128)(2,1)S(1)}) custom-call(s32[8]{0:T(128)S(1)} %copy-done.3, bf16[512,8192]{1,0:T(8,128)(2,1)} %rec_ref.3, bf16[1,256]{1,0:T(2,128)(2,1)S(1)} %reshape.9.toep_ref, bf16[512,256]{1,0:T(8,128)(2,1)S(1)} %copy-done.2), custom_call_target="tpu_custom_call" | custom-call | flops 12884901888 | bytes 12582912 | tf_op jit(solution)/shard_map/pallas_call | solution.py:218
  24.4 0.0 collective-permute-done.tail_ref
  24.4 3.7 %shard_map.56 = (bf16[128,16,512]{2,1,0:T(8,128)(2,1)S(1)}, bf16[128,16,512]{2,1,0:T(8,128)(2,1)S(1)}) custom-call(s32[8]{0:T(128)S(1)} %copy-done.3, bf16[512,256]{1,0:T(8,128)(2,1)S(1)} %collective-permute-done.tail_ref, bf16[512,8192]{1,0:T(8,128)(2,1)} %rec_ref.3, ...), custom_call_target="tpu_custom_call", output_to_operand_aliasing={{0}: (6, {}), {1}: (7, {})} | custom-call | flops 402653184 | bytes 8388608 | tf_op jit(solution)/shard_map/pallas_call | solution.py:172
  28.1 0.0 copy-start.1
  28.1 52.8 %all_to_all.10.am_ref.bm_ref = bf16[8,8,2,16,512]{4,3,2,1,0:T(8,128)(2,1)} all-to-all(bf16[8,8,2,16,512]{4,3,2,1,0:T(8,128)(2,1)S(1)} %bitcast.2), channel_id=1, replica_groups=mesh['groups'=2,'tm'=8,'pair'=2] {'tm'}, dimensions={0} | all-to-all | bytes 4194304 | tf_op jit(solution)/shard_map/all_to_all | solution.py:322
  80.9 0.0 copy-done.1
  80.9 0.0 copy-start.5
  80.9 0.0 copy-start.4
  80.9 3.7 %all-to-all-start = ((bf16[8,8,2,16,512]{4,3,2,1,0:T(8,128)(2,1)}), bf16[8,8,2,16,512]{4,3,2,1,0:T(8,128)(2,1)S(1)}, u32[]{:S(2)}, u32[]{:S(2)}) async-start(bf16[8,8,2,16,512]{4,3,2,1,0:T(8,128)(2,1)} %bitcast.3), calls=%async_computation | async-start | bytes 4194304 | tf_op jit(solution)/shard_map/all_to_all | solution.py:322
  84.6 0.1 collective-permute-start.2
  84.7 47.6 %all-to-all-done.am_ref.bm_ref = bf16[8,8,2,16,512]{4,3,2,1,0:T(8,128)(2,1)S(1)} async-done(((bf16[8,8,2,16,512]{4,3,2,1,0:T(8,128)(2,1)}), bf16[8,8,2,16,512]{4,3,2,1,0:T(8,128)(2,1)S(1)}, u32[]{:S(2)}, u32[]{:S(2)}) %all-to-all-start) | async-done | bytes 2097184 | tf_op jit(solution)/shard_map/all_to_all | solution.py:322
  132.3 0.0 collective-permute-start.1
  132.3 0.0 copy-done.5
  132.3 0.1 copy.10.pb_ref
  132.4 0.0 collective-permute-done.2.ap_ref.bp_ref
  132.4 0.0 copy-done.4
  132.4 0.0 copy-start
  132.4 1.6 %copy-done = bf16[8,8,2,16,512]{4,3,2,1,0:T(8,128)(2,1)S(1)} copy-done((bf16[8,8,2,16,512]{4,3,2,1,0:T(8,128)(2,1)S(1)}, bf16[8,8,2,16,512]{4,3,2,1,0:T(8,128)(2,1)}, u32[]{:S(2)}) %copy-start) | copy-done | bytes 2097176
  134.0 9.9 %shard_map.57.rest_0_ = f32[8,16,2,128,128]{4,3,2,1,0:T(8,128)} custom-call(s32[8,2]{1,0:T(8,128)S(1)} %copy.10.pb_ref, s32[8]{0:T(128)S(1)} %copy-done.4, bf16[8,8,2,16,512]{4,3,2,1,0:T(8,128)(2,1)S(1)} %copy-done, bf16[8,8,2,16,512]{4,3,2,1,0:T(8,128)(2,1)} %collective-permute-done.2.ap_ref.bp_ref, bf16[8,8,2,16,512]{4,3,2,1,0:T(8,128)(2,1)S(1)} %copy-done, ...), custom_call_target="tpu_custom_call" | custom-call | flops 1073741824 | bytes 25165824 | tf_op jit(solution)/shard_map/pallas_call | solution.py:295
  143.9 0.0 collective-permute-done.1.ap_ref.bp_ref
  143.9 9.9 %shard_map.58 = f32[8,16,2,128,128]{4,3,2,1,0:T(8,128)} custom-call(s32[8,2]{1,0:T(8,128)S(1)} %copy.10.pb_ref, s32[8]{0:T(128)S(1)} %copy-done.4, bf16[8,8,2,16,512]{4,3,2,1,0:T(8,128)(2,1)S(1)} %all-to-all-done.am_ref.bm_ref, bf16[8,8,2,16,512]{4,3,2,1,0:T(8,128)(2,1)} %collective-permute-done.1.ap_ref.bp_ref, ...), custom_call_target="tpu_custom_call", output_to_operand_aliasing={{}: (6, {})} | custom-call | flops 1073741824 | bytes 25165824 | tf_op jit(solution)/shard_map/pallas_call | solution.py:295
Async XLA Ops:
  1.0 23.4 %collective-permute-start = (bf16[512,256]{1,0:T(8,128)(2,1)S(1)}, bf16[512,256]{1,0:T(8,128)(2,1)S(1)}, u32[]{:S(2)}, u32[]{:S(2)}) collective-permute-start(bf16[512,256]{1,0:T(8,128)(2,1)S(1)} %slice.3), channel_id=1, source_target_pairs={{0,2},{2,4},{4,6},{6,8},{8,10},{10,12},{12,14},{1,3},{3,5},{5,7},{... | collective-permute-start | bytes 786440 | tf_op jit(solution)/shard_map/ppermute | solution.py:25
  6.5 0.9 copy-start.2
  7.5 0.7 copy-start.3
  28.1 52.8 %copy-start.1 = (bf16[128,16,512]{2,1,0:T(8,128)(2,1)}, bf16[128,16,512]{2,1,0:T(8,128)(2,1)S(1)}, u32[]{:S(2)}) copy-start(bf16[128,16,512]{2,1,0:T(8,128)(2,1)S(1)} %get-tuple-element.13) | copy-start | bytes 6291460
  80.9 51.5 %copy-start.5 = (s32[8,2]{0,1:T(2,128)S(1)}, s32[8,2]{0,1:T(2,128)}, u32[]{:S(2)}) copy-start(s32[8,2]{0,1:T(2,128)} %param.8) | copy-start | bytes 196
  80.9 51.5 %copy-start.4 = (s32[8]{0:T(128)S(1)}, s32[8]{0:T(128)}, u32[]{:S(2)}) copy-start(s32[8]{0:T(128)} %kw_ref.3) | copy-start | bytes 100
  80.9 51.4 %all-to-all-start = ((bf16[8,8,2,16,512]{4,3,2,1,0:T(8,128)(2,1)}), bf16[8,8,2,16,512]{4,3,2,1,0:T(8,128)(2,1)S(1)}, u32[]{:S(2)}, u32[]{:S(2)}) async-start(bf16[8,8,2,16,512]{4,3,2,1,0:T(8,128)(2,1)} %bitcast.3), calls=%async_computation | async-start | bytes 4194304 | tf_op jit(solution)/shard_map/all_to_all | solution.py:322
  84.6 47.8 %collective-permute-start.2 = (bf16[8,8,2,16,512]{4,3,2,1,0:T(8,128)(2,1)}, bf16[8,8,2,16,512]{4,3,2,1,0:T(8,128)(2,1)}, u32[]{:S(2)}, u32[]{:S(2)}) collective-permute-start(bf16[8,8,2,16,512]{4,3,2,1,0:T(8,128)(2,1)} %all_to_all.10.am_ref.bm_ref), channel_id=1, source_target_pairs={{0,1},{1,0},{2,3},{3,2},{4,5},{5,4},{6,7},{7,6},{8,9},{9,8},{10,11... | collective-permute-start | bytes 6291464 | tf_op jit(solution)/shard_map/ppermute | solution.py:323
  132.3 11.6 %collective-permute-start.1 = (bf16[8,8,2,16,512]{4,3,2,1,0:T(8,128)(2,1)S(1)}, bf16[8,8,2,16,512]{4,3,2,1,0:T(8,128)(2,1)}, u32[]{:S(2)}, u32[]{:S(2)}) collective-permute-start(bf16[8,8,2,16,512]{4,3,2,1,0:T(8,128)(2,1)S(1)} %all-to-all-done.am_ref.bm_ref), channel_id=1, source_target_pairs={{0,1},{1,0},{2,3},{3,2},{4,5},{5,4},{6,7},{7,6},{8,9},{9,8},{10,11... | collective-permute-start | bytes 6291464 | tf_op jit(solution)/shard_map/ppermute | solution.py:323
  132.4 1.6 %copy-start = (bf16[8,8,2,16,512]{4,3,2,1,0:T(8,128)(2,1)S(1)}, bf16[8,8,2,16,512]{4,3,2,1,0:T(8,128)(2,1)}, u32[]{:S(2)}) copy-start(bf16[8,8,2,16,512]{4,3,2,1,0:T(8,128)(2,1)} %all_to_all.10.am_ref.bm_ref) | copy-start | bytes 6291460

commit v19 on v15

--- a/solution.py
+++ b/solution.py
@@ -286,7 +286,7 @@
         out_shape=jax.ShapeDtypeStruct((npairs, all_bins, 2, CH_BLK, CH_BLK), jnp.float32),
         input_output_aliases=aliases,
         compiler_params=pltpu.CompilerParams(
-            dimension_semantics=("arbitrary",), vmem_limit_bytes=48 * 1024 * 1024
+            dimension_semantics=("arbitrary",), vmem_limit_bytes=67043328
         ),
         cost_estimate=pl.CostEstimate(
             flops=flops, bytes_accessed=out_bytes + in_bytes, transcendentals=0

time: 155 us -> 161 us (1.039)
  Pallas kernels: 38.7 us -> 45.7 us
    pallas_call x2, Pallas kernels: 18.9 us -> 22.7 us  [stack_pairs(): pl.pallas_call(functools.partial(stack_kernel_for, blocks_per_half), grid...]
    pallas_call x1, Pallas kernels: 3.59 us -> 5.48 us  [fill_first_window(): pl.pallas_call(functools.partial(first_window_kernel, count_parts), grid_...]
  transfers between devices with their start and end apart: 4 -> 4, of which waited for: 1 -> 1; matrix products, arithmetic and copies ran while one was open for 1% -> 2% of each run, Pallas kernels for 17% -> 18%
where the time goes in v19:
time: 161 us; the launch traced here: 159 us
  blocking collectives  52.7 us (33%)
  waiting for transfers between devices  47.3 us (29%)
  Pallas kernels  45.7 us (28%)
  starting transfers between devices  9.45 us (6%)
  local copies, waits for them, and re-layouts  3.41 us (2%)
    all_to_all x1, blocking collectives, per_device(): lax.all_to_all(outgoing, 'tm', split_axis=0, concat_axis=0, tiled=True)  52.7 us
    all_to_all x1, waiting for transfers between devices, per_device(): lax.all_to_all(outgoing, 'tm', split_axis=0, concat_axis=0, tiled=True)  47.3 us
    pallas_call x2, Pallas kernels, stack_pairs(): pl.pallas_call(functools.partial(stack_kernel_for, blocks_per_half), grid...  22.7 us
    pallas_call x1, Pallas kernels, whiten_front(): pl.pallas_call(front_kernel, grid_spec=grid_spec, out_shape=[jax.ShapeDty...  17.5 us
    pallas_call x1, Pallas kernels, fill_first_window(): pl.pallas_call(functools.partial(first_window_kernel, count_parts), grid_...  5.48 us
    ppermute x1, starting transfers between devices, from_behind(): return lax.ppermute(array, axis, pairs)  4.89 us
    all_to_all x1, starting transfers between devices, per_device(): lax.all_to_all(outgoing, 'tm', split_axis=0, concat_axis=0, tiled=True)  4.49 us
  transfers between devices with their start and end apart: 4, of which 1 were waited for; matrix products, arithmetic and copies ran while one was open for 2% of the time, Pallas kernels for 18%

profile of v19, /device:TPU:0, one launch (start us, length us, event | category | flops | bytes accessed | tf_op | source)
XLA Modules:
  0.0 158.7 jit_solution(11232689649702900680)
XLA Ops:
  0.0 0.0 copy-start
  0.0 0.0 copy-start.1
  0.0 1.0 slice.6
  1.0 4.9 %collective-permute-start = (bf16[512,256]{1,0:T(8,128)(2,1)S(1)}, bf16[512,256]{1,0:T(8,128)(2,1)S(1)}, u32[]{:S(2)}, u32[]{:S(2)}) collective-permute-start(bf16[512,256]{1,0:T(8,128)(2,1)S(1)} %slice.6), channel_id=1, source_target_pairs={{0,2},{2,4},{4,6},{6,8},{8,10},{10,12},{12,14},{1,3},{3,5},{5,7},{... | collective-permute-start | bytes 786440 | tf_op jit(solution)/shard_map/ppermute | solution.py:25
  5.9 0.7 rev.3
  6.7 0.1 pad_maximum_fusion
  6.8 0.6 tile.10
  7.4 0.2 reshape.10
  7.6 0.1 copy.11
  7.7 0.0 copy-done
  7.7 0.0 copy-done.1
  7.8 17.5 %shard_map.55 = (bf16[128,16,512]{2,1,0:T(8,128)(2,1)S(1)}, bf16[128,16,512]{2,1,0:T(8,128)(2,1)}, bf16[512,256]{1,0:T(8,128)(2,1)S(1)}) custom-call(s32[8]{0:T(128)S(1)} %copy-done.1, bf16[512,8192]{1,0:T(8,128)(2,1)} %rec_ref.3, bf16[512,256]{1,0:T(8,128)(2,1)S(1)} %bitcast.4, bf16[512,256]{1,0:T(8,128)(2,1)S(1)} %copy-done), custom_call_target="tpu_custom_call" | custom-call | flops 12884901888 | bytes 12582912 | tf_op jit(solution)/shard_map/pallas_call | solution.py:206
  25.3 0.0 collective-permute-done.tail_ref
  25.3 5.5 %shard_map.56 = (bf16[128,16,512]{2,1,0:T(8,128)(2,1)S(1)}, bf16[128,16,512]{2,1,0:T(8,128)(2,1)}) custom-call(s32[8]{0:T(128)S(1)} %copy-done.1, bf16[512,256]{1,0:T(8,128)(2,1)S(1)} %collective-permute-done.tail_ref, bf16[512,8192]{1,0:T(8,128)(2,1)} %rec_ref.3, ...), custom_call_target="tpu_custom_call", output_to_operand_aliasing={{0}: (6, {}), {1}: (7, {})} | custom-call | flops 402653184 | bytes 8388608 | tf_op jit(solution)/shard_map/pallas_call | solution.py:160
  30.7 52.7 %all_to_all.10.am_ref.bm_ref = bf16[8,8,2,16,512]{4,3,2,1,0:T(8,128)(2,1)S(1)} all-to-all(bf16[8,8,2,16,512]{4,3,2,1,0:T(8,128)(2,1)S(1)} %bitcast.3), channel_id=1, replica_groups=mesh['groups'=2,'tm'=8,'pair'=2] {'tm'}, dimensions={0} | all-to-all | bytes 4194304 | tf_op jit(solution)/shard_map/all_to_all | solution.py:310
  83.4 0.0 copy-start.2
  83.4 0.0 copy-start.3
  83.4 4.5 %all-to-all-start = ((bf16[8,8,2,16,512]{4,3,2,1,0:T(8,128)(2,1)}), bf16[8,8,2,16,512]{4,3,2,1,0:T(8,128)(2,1)}, u32[]{:S(2)}, u32[]{:S(2)}) async-start(bf16[8,8,2,16,512]{4,3,2,1,0:T(8,128)(2,1)} %bitcast.1), calls=%async_computation | async-start | bytes 4194304 | tf_op jit(solution)/shard_map/all_to_all | solution.py:310
  87.9 0.0 copy-done.2
  88.0 0.1 collective-permute-start.2
  88.0 47.3 %all-to-all-done.am_ref.bm_ref = bf16[8,8,2,16,512]{4,3,2,1,0:T(8,128)(2,1)} async-done(((bf16[8,8,2,16,512]{4,3,2,1,0:T(8,128)(2,1)}), bf16[8,8,2,16,512]{4,3,2,1,0:T(8,128)(2,1)}, u32[]{:S(2)}, u32[]{:S(2)}) %all-to-all-start) | async-done | bytes 2097184 | tf_op jit(solution)/shard_map/all_to_all | solution.py:310
  135.3 0.0 collective-permute-start.1
  135.3 0.0 copy-done.3
  135.3 0.7 copy.13.pb_ref
  136.0 0.0 collective-permute-done.2.ap_ref.bp_ref
  136.0 11.2 %shard_map.57.rest_0_ = f32[8,16,2,128,128]{4,3,2,1,0:T(8,128)} custom-call(s32[8,2]{1,0:T(8,128)} %copy.13.pb_ref, s32[8]{0:T(128)} %kw_ref.3, bf16[8,8,2,16,512]{4,3,2,1,0:T(8,128)(2,1)} %copy-done.2, bf16[8,8,2,16,512]{4,3,2,1,0:T(8,128)(2,1)} %collective-permute-done.2.ap_ref.bp_ref, bf16[8,8,2,16,512]{4,3,2,1,0:T(8,128)(2,1)} %copy-done.2, ...), custom_call_target="tpu_custom_call" | custom-call | flops 1073741824 | bytes 25165824 | tf_op jit(solution)/shard_map/pallas_call | solution.py:283
  147.2 0.0 collective-permute-done.1.ap_ref.bp_ref
  147.2 11.5 %shard_map.58 = f32[8,16,2,128,128]{4,3,2,1,0:T(8,128)} custom-call(s32[8,2]{1,0:T(8,128)} %copy.13.pb_ref, s32[8]{0:T(128)} %kw_ref.3, bf16[8,8,2,16,512]{4,3,2,1,0:T(8,128)(2,1)} %all-to-all-done.am_ref.bm_ref, bf16[8,8,2,16,512]{4,3,2,1,0:T(8,128)(2,1)} %collective-permute-done.1.ap_ref.bp_ref, ...), custom_call_target="tpu_custom_call", output_to_operand_aliasing={{}: (6, {})} | custom-call | flops 1073741824 | bytes 25165824 | tf_op jit(solution)/shard_map/pallas_call | solution.py:283
  (3 shorter events, 0.1 us)
Async XLA Ops:
  0.0 7.7 %copy-start = (bf16[512,256]{1,0:T(8,128)(2,1)S(1)}, bf16[512,256]{1,0:T(8,128)(2,1)}, u32[]{:S(2)}) copy-start(bf16[512,256]{1,0:T(8,128)(2,1)} %constant.6.clone.basis_ref) | copy-start | bytes 786436
  0.0 7.7 %copy-start.1 = (s32[8]{0:T(128)S(1)}, s32[8]{0:T(128)}, u32[]{:S(2)}) copy-start(s32[8]{0:T(128)} %kw_ref.3) | copy-start | bytes 100
  1.0 24.2 %collective-permute-start = (bf16[512,256]{1,0:T(8,128)(2,1)S(1)}, bf16[512,256]{1,0:T(8,128)(2,1)S(1)}, u32[]{:S(2)}, u32[]{:S(2)}) collective-permute-start(bf16[512,256]{1,0:T(8,128)(2,1)S(1)} %slice.6), channel_id=1, source_target_pairs={{0,2},{2,4},{4,6},{6,8},{8,10},{10,12},{12,14},{1,3},{3,5},{5,7},{... | collective-permute-start | bytes 786440 | tf_op jit(solution)/shard_map/ppermute | solution.py:25
  83.4 4.5 %copy-start.2 = (bf16[8,8,2,16,512]{4,3,2,1,0:T(8,128)(2,1)}, bf16[8,8,2,16,512]{4,3,2,1,0:T(8,128)(2,1)S(1)}, u32[]{:S(2)}) copy-start(bf16[8,8,2,16,512]{4,3,2,1,0:T(8,128)(2,1)S(1)} %all_to_all.10.am_ref.bm_ref) | copy-start | bytes 6291460
  83.4 51.9 %copy-start.3 = (s32[8,2]{0,1:T(2,128)S(1)}, s32[8,2]{0,1:T(2,128)}, u32[]{:S(2)}) copy-start(s32[8,2]{0,1:T(2,128)} %param.8) | copy-start | bytes 196
  83.4 51.9 %all-to-all-start = ((bf16[8,8,2,16,512]{4,3,2,1,0:T(8,128)(2,1)}), bf16[8,8,2,16,512]{4,3,2,1,0:T(8,128)(2,1)}, u32[]{:S(2)}, u32[]{:S(2)}) async-start(bf16[8,8,2,16,512]{4,3,2,1,0:T(8,128)(2,1)} %bitcast.1), calls=%async_computation | async-start | bytes 4194304 | tf_op jit(solution)/shard_map/all_to_all | solution.py:310
  88.0 48.0 %collective-permute-start.2 = (bf16[8,8,2,16,512]{4,3,2,1,0:T(8,128)(2,1)S(1)}, bf16[8,8,2,16,512]{4,3,2,1,0:T(8,128)(2,1)}, u32[]{:S(2)}, u32[]{:S(2)}) collective-permute-start(bf16[8,8,2,16,512]{4,3,2,1,0:T(8,128)(2,1)S(1)} %all_to_all.10.am_ref.bm_ref), channel_id=1, source_target_pairs={{0,1},{1,0},{2,3},{3,2},{4,5},{5,4},{6,7},{7,6},{8,9},{9,8},{10,11... | collective-permute-start | bytes 6291464 | tf_op jit(solution)/shard_map/ppermute | solution.py:311
  135.3 11.9 %collective-permute-start.1 = (bf16[8,8,2,16,512]{4,3,2,1,0:T(8,128)(2,1)}, bf16[8,8,2,16,512]{4,3,2,1,0:T(8,128)(2,1)}, u32[]{:S(2)}, u32[]{:S(2)}) collective-permute-start(bf16[8,8,2,16,512]{4,3,2,1,0:T(8,128)(2,1)} %all-to-all-done.am_ref.bm_ref), channel_id=1, source_target_pairs={{0,1},{1,0},{2,3},{3,2},{4,5},{5,4},{6,7},{7,6},{8,9},{9,8},{10,11... | collective-permute-start | bytes 6291464 | tf_op jit(solution)/shard_map/ppermute | solution.py:311

commit v20 on v15

--- a/solution.py
+++ b/solution.py
@@ -108,7 +108,7 @@
                 o_ref[k, :, CH_BLK * h : CH_BLK * (h + 1)] = part.astype(o_ref.dtype)
             return carry
 
-        lax.fori_loop(0, o_ref.shape[0], one_row, 0, unroll=16)
+        lax.fori_loop(0, o_ref.shape[0], one_row, 0, unroll=32)
         start += o_ref.shape[0]
 
 

time: 155 us -> 154 us (level); the launches traced: 152 us -> 153 us
  no operation moved by 1% of the time
where the time goes in v20:
time: 154 us; the launch traced here: 153 us
  blocking collectives  52.8 us (34%)
  waiting for transfers between devices  47.6 us (31%)
  Pallas kernels  39.3 us (26%)
  starting transfers between devices  8.7 us (6%)
  local copies, waits for them, and re-layouts  4.41 us (3%)
    all_to_all x1, blocking collectives, per_device(): lax.all_to_all(outgoing, 'tm', split_axis=0, concat_axis=0, tiled=True)  52.8 us
    all_to_all x1, waiting for transfers between devices, per_device(): lax.all_to_all(outgoing, 'tm', split_axis=0, concat_axis=0, tiled=True)  47.6 us
    pallas_call x2, Pallas kernels, stack_pairs(): pl.pallas_call(functools.partial(stack_kernel_for, blocks_per_half), grid...  19.6 us
    pallas_call x1, Pallas kernels, whiten_front(): pl.pallas_call(front_kernel, grid_spec=grid_spec, out_shape=[jax.ShapeDty...  16 us
    ppermute x1, starting transfers between devices, from_behind(): return lax.ppermute(array, axis, pairs)  4.89 us
    all_to_all x1, starting transfers between devices, per_device(): lax.all_to_all(outgoing, 'tm', split_axis=0, concat_axis=0, tiled=True)  3.74 us
    pallas_call x1, Pallas kernels, fill_first_window(): pl.pallas_call(functools.partial(first_window_kernel, count_parts), grid_...  3.59 us
  transfers between devices with their start and end apart: 4, of which 1 were waited for; matrix products, arithmetic and copies ran while one was open for 1% of the time, Pallas kernels for 17%

profile of v20, /device:TPU:0, one launch (start us, length us, event | category | flops | bytes accessed | tf_op | source)
XLA Modules:
  0.0 153.0 jit_solution(12690039878308207835)
XLA Ops:
  0.0 0.0 copy-start.2
  0.0 0.0 copy-start.3
  0.0 1.0 slice.6
  1.0 4.9 %collective-permute-start = (bf16[512,256]{1,0:T(8,128)(2,1)S(1)}, bf16[512,256]{1,0:T(8,128)(2,1)S(1)}, u32[]{:S(2)}, u32[]{:S(2)}) collective-permute-start(bf16[512,256]{1,0:T(8,128)(2,1)S(1)} %slice.6), channel_id=1, source_target_pairs={{0,2},{2,4},{4,6},{6,8},{8,10},{10,12},{12,14},{1,3},{3,5},{5,7},{... | collective-permute-start | bytes 786440 | tf_op jit(solution)/shard_map/ppermute | solution.py:25
  5.9 0.7 rev.3
  6.7 0.1 pad_maximum_fusion
  6.8 0.6 tile.10
  7.4 0.2 reshape.10
  7.6 0.1 copy.11
  7.7 0.0 copy-done.2
  7.7 0.0 copy-done.3
  7.7 16.0 %shard_map.55 = (bf16[128,16,512]{2,1,0:T(8,128)(2,1)S(1)}, bf16[128,16,512]{2,1,0:T(8,128)(2,1)S(1)}, bf16[512,256]{1,0:T(8,128)(2,1)S(1)}) custom-call(s32[8]{0:T(128)S(1)} %copy-done.3, bf16[512,8192]{1,0:T(8,128)(2,1)} %rec_ref.3, bf16[512,256]{1,0:T(8,128)(2,1)S(1)} %bitcast.5, bf16[512,256]{1,0:T(8,128)(2,1)S(1)} %copy-done.2), custom_call_target="tpu_custom_call" | custom-call | flops 12884901888 | bytes 12582912 | tf_op jit(solution)/shard_map/pallas_call | solution.py:206
  23.8 0.0 collective-permute-done.tail_ref
  23.8 3.6 %shard_map.56 = (bf16[128,16,512]{2,1,0:T(8,128)(2,1)S(1)}, bf16[128,16,512]{2,1,0:T(8,128)(2,1)S(1)}) custom-call(s32[8]{0:T(128)S(1)} %copy-done.3, bf16[512,256]{1,0:T(8,128)(2,1)S(1)} %collective-permute-done.tail_ref, bf16[512,8192]{1,0:T(8,128)(2,1)} %rec_ref.3, ...), custom_call_target="tpu_custom_call", output_to_operand_aliasing={{0}: (6, {}), {1}: (7, {})} | custom-call | flops 402653184 | bytes 8388608 | tf_op jit(solution)/shard_map/pallas_call | solution.py:160
  27.4 0.0 copy-start.1
  27.4 52.8 %all_to_all.10.am_ref.bm_ref = bf16[8,8,2,16,512]{4,3,2,1,0:T(8,128)(2,1)} all-to-all(bf16[8,8,2,16,512]{4,3,2,1,0:T(8,128)(2,1)S(1)} %bitcast.3), channel_id=1, replica_groups=mesh['groups'=2,'tm'=8,'pair'=2] {'tm'}, dimensions={0} | all-to-all | bytes 4194304 | tf_op jit(solution)/shard_map/all_to_all | solution.py:310
  80.2 0.0 copy-done.1
  80.2 0.0 copy-start.4
  80.2 3.7 %all-to-all-start = ((bf16[8,8,2,16,512]{4,3,2,1,0:T(8,128)(2,1)}), bf16[8,8,2,16,512]{4,3,2,1,0:T(8,128)(2,1)S(1)}, u32[]{:S(2)}, u32[]{:S(2)}) async-start(bf16[8,8,2,16,512]{4,3,2,1,0:T(8,128)(2,1)} %bitcast.4), calls=%async_computation | async-start | bytes 4194304 | tf_op jit(solution)/shard_map/all_to_all | solution.py:310
  84.0 0.1 collective-permute-start.2
  84.0 47.6 %all-to-all-done.am_ref.bm_ref = bf16[8,8,2,16,512]{4,3,2,1,0:T(8,128)(2,1)S(1)} async-done(((bf16[8,8,2,16,512]{4,3,2,1,0:T(8,128)(2,1)}), bf16[8,8,2,16,512]{4,3,2,1,0:T(8,128)(2,1)S(1)}, u32[]{:S(2)}, u32[]{:S(2)}) %all-to-all-start) | async-done | bytes 2097184 | tf_op jit(solution)/shard_map/all_to_all | solution.py:310
  131.7 0.0 collective-permute-start.1
  131.7 0.0 copy-done.4
  131.7 0.1 copy.13.pb_ref
  131.7 0.0 collective-permute-done.2.ap_ref.bp_ref
  131.8 0.0 copy-start
  131.8 1.6 %copy-done = bf16[8,8,2,16,512]{4,3,2,1,0:T(8,128)(2,1)S(1)} copy-done((bf16[8,8,2,16,512]{4,3,2,1,0:T(8,128)(2,1)S(1)}, bf16[8,8,2,16,512]{4,3,2,1,0:T(8,128)(2,1)}, u32[]{:S(2)}) %copy-start) | copy-done | bytes 2097176
  133.3 9.8 %shard_map.57.rest_0_ = f32[8,16,2,128,128]{4,3,2,1,0:T(8,128)} custom-call(s32[8,2]{1,0:T(8,128)S(1)} %copy.13.pb_ref, s32[8]{0:T(128)S(1)} %copy-done.3, bf16[8,8,2,16,512]{4,3,2,1,0:T(8,128)(2,1)S(1)} %copy-done, bf16[8,8,2,16,512]{4,3,2,1,0:T(8,128)(2,1)} %collective-permute-done.2.ap_ref.bp_ref, bf16[8,8,2,16,512]{4,3,2,1,0:T(8,128)(2,1)S(1)} %copy-done, ...), custom_call_target="tpu_custom_call" | custom-call | flops 1073741824 | bytes 25165824 | tf_op jit(solution)/shard_map/pallas_call | solution.py:283
  143.2 0.0 collective-permute-done.1.ap_ref.bp_ref
  143.2 9.8 %shard_map.58 = f32[8,16,2,128,128]{4,3,2,1,0:T(8,128)} custom-call(s32[8,2]{1,0:T(8,128)S(1)} %copy.13.pb_ref, s32[8]{0:T(128)S(1)} %copy-done.3, bf16[8,8,2,16,512]{4,3,2,1,0:T(8,128)(2,1)S(1)} %all-to-all-done.am_ref.bm_ref, bf16[8,8,2,16,512]{4,3,2,1,0:T(8,128)(2,1)} %collective-permute-done.1.ap_ref.bp_ref, ...), custom_call_target="tpu_custom_call", output_to_operand_aliasing={{}: (6, {})} | custom-call | flops 1073741824 | bytes 25165824 | tf_op jit(solution)/shard_map/pallas_call | solution.py:283
  (3 shorter events, 0.1 us)
Async XLA Ops:
  0.0 7.7 %copy-start.2 = (bf16[512,256]{1,0:T(8,128)(2,1)S(1)}, bf16[512,256]{1,0:T(8,128)(2,1)}, u32[]{:S(2)}) copy-start(bf16[512,256]{1,0:T(8,128)(2,1)} %constant.6.clone.basis_ref) | copy-start | bytes 786436
  0.0 7.7 %copy-start.3 = (s32[8]{0:T(128)S(1)}, s32[8]{0:T(128)}, u32[]{:S(2)}) copy-start(s32[8]{0:T(128)} %kw_ref.3) | copy-start | bytes 100
  1.0 22.8 %collective-permute-start = (bf16[512,256]{1,0:T(8,128)(2,1)S(1)}, bf16[512,256]{1,0:T(8,128)(2,1)S(1)}, u32[]{:S(2)}, u32[]{:S(2)}) collective-permute-start(bf16[512,256]{1,0:T(8,128)(2,1)S(1)} %slice.6), channel_id=1, source_target_pairs={{0,2},{2,4},{4,6},{6,8},{8,10},{10,12},{12,14},{1,3},{3,5},{5,7},{... | collective-permute-start | bytes 786440 | tf_op jit(solution)/shard_map/ppermute | solution.py:25
  27.4 52.8 %copy-start.1 = (bf16[128,16,512]{2,1,0:T(8,128)(2,1)}, bf16[128,16,512]{2,1,0:T(8,128)(2,1)S(1)}, u32[]{:S(2)}) copy-start(bf16[128,16,512]{2,1,0:T(8,128)(2,1)S(1)} %get-tuple-element.13) | copy-start | bytes 6291460
  80.2 51.5 %copy-start.4 = (s32[8,2]{0,1:T(2,128)S(1)}, s32[8,2]{0,1:T(2,128)}, u32[]{:S(2)}) copy-start(s32[8,2]{0,1:T(2,128)} %param.8) | copy-start | bytes 196
  80.2 51.4 %all-to-all-start = ((bf16[8,8,2,16,512]{4,3,2,1,0:T(8,128)(2,1)}), bf16[8,8,2,16,512]{4,3,2,1,0:T(8,128)(2,1)S(1)}, u32[]{:S(2)}, u32[]{:S(2)}) async-start(bf16[8,8,2,16,512]{4,3,2,1,0:T(8,128)(2,1)} %bitcast.4), calls=%async_computation | async-start | bytes 4194304 | tf_op jit(solution)/shard_map/all_to_all | solution.py:310
  84.0 47.8 %collective-permute-start.2 = (bf16[8,8,2,16,512]{4,3,2,1,0:T(8,128)(2,1)}, bf16[8,8,2,16,512]{4,3,2,1,0:T(8,128)(2,1)}, u32[]{:S(2)}, u32[]{:S(2)}) collective-permute-start(bf16[8,8,2,16,512]{4,3,2,1,0:T(8,128)(2,1)} %all_to_all.10.am_ref.bm_ref), channel_id=1, source_target_pairs={{0,1},{1,0},{2,3},{3,2},{4,5},{5,4},{6,7},{7,6},{8,9},{9,8},{10,11... | collective-permute-start | bytes 6291464 | tf_op jit(solution)/shard_map/ppermute | solution.py:311
  131.7 11.5 %collective-permute-start.1 = (bf16[8,8,2,16,512]{4,3,2,1,0:T(8,128)(2,1)S(1)}, bf16[8,8,2,16,512]{4,3,2,1,0:T(8,128)(2,1)}, u32[]{:S(2)}, u32[]{:S(2)}) collective-permute-start(bf16[8,8,2,16,512]{4,3,2,1,0:T(8,128)(2,1)S(1)} %all-to-all-done.am_ref.bm_ref), channel_id=1, source_target_pairs={{0,1},{1,0},{2,3},{3,2},{4,5},{5,4},{6,7},{7,6},{8,9},{9,8},{10,11... | collective-permute-start | bytes 6291464 | tf_op jit(solution)/shard_map/ppermute | solution.py:311
  131.8 1.6 %copy-start = (bf16[8,8,2,16,512]{4,3,2,1,0:T(8,128)(2,1)S(1)}, bf16[8,8,2,16,512]{4,3,2,1,0:T(8,128)(2,1)}, u32[]{:S(2)}) copy-start(bf16[8,8,2,16,512]{4,3,2,1,0:T(8,128)(2,1)} %all_to_all.10.am_ref.bm_ref) | copy-start | bytes 6291460

commit v21 on v20

--- a/solution.py
+++ b/solution.py
@@ -134,7 +134,7 @@
             o_ref[k] = jnp.where(rowid == 0, first, held)
             return carry
 
-        lax.fori_loop(0, o_ref.shape[0], one_row, 0, unroll=8)
+        lax.fori_loop(0, o_ref.shape[0], one_row, 0, unroll=32)
         start += o_ref.shape[0]
 
 

time: 154 us -> 154 us (level)
  no operation moved by 1% of the time
where the time goes in v21:
time: 154 us; the launch traced here: 153 us
  blocking collectives  52.8 us (34%)
  waiting for transfers between devices  47.6 us (31%)
  Pallas kernels  39.7 us (26%)
  starting transfers between devices  8.7 us (6%)
  local copies, waits for them, and re-layouts  4.41 us (3%)
    all_to_all x1, blocking collectives, per_device(): lax.all_to_all(outgoing, 'tm', split_axis=0, concat_axis=0, tiled=True)  52.8 us
    all_to_all x1, waiting for transfers between devices, per_device(): lax.all_to_all(outgoing, 'tm', split_axis=0, concat_axis=0, tiled=True)  47.6 us
    pallas_call x2, Pallas kernels, stack_pairs(): pl.pallas_call(functools.partial(stack_kernel_for, blocks_per_half), grid...  20.1 us
    pallas_call x1, Pallas kernels, whiten_front(): pl.pallas_call(front_kernel, grid_spec=grid_spec, out_shape=[jax.ShapeDty...  16 us
    ppermute x1, starting transfers between devices, from_behind(): return lax.ppermute(array, axis, pairs)  4.89 us
    all_to_all x1, starting transfers between devices, per_device(): lax.all_to_all(outgoing, 'tm', split_axis=0, concat_axis=0, tiled=True)  3.74 us
    pallas_call x1, Pallas kernels, fill_first_window(): pl.pallas_call(functools.partial(first_window_kernel, count_parts), grid_...  3.58 us
  transfers between devices with their start and end apart: 4, of which 1 were waited for; matrix products, arithmetic and copies ran while one was open for 1% of the time, Pallas kernels for 17%

profile of v21, /device:TPU:0, one launch (start us, length us, event | category | flops | bytes accessed | tf_op | source)
XLA Modules:
  0.0 153.4 jit_solution(4372056016871211326)
XLA Ops:
  0.0 0.0 copy-start.2
  0.0 0.0 copy-start.3
  0.0 1.0 slice.6
  1.0 4.9 %collective-permute-start = (bf16[512,256]{1,0:T(8,128)(2,1)S(1)}, bf16[512,256]{1,0:T(8,128)(2,1)S(1)}, u32[]{:S(2)}, u32[]{:S(2)}) collective-permute-start(bf16[512,256]{1,0:T(8,128)(2,1)S(1)} %slice.6), channel_id=1, source_target_pairs={{0,2},{2,4},{4,6},{6,8},{8,10},{10,12},{12,14},{1,3},{3,5},{5,7},{... | collective-permute-start | bytes 786440 | tf_op jit(solution)/shard_map/ppermute | solution.py:25
  5.9 0.7 rev.3
  6.7 0.1 pad_maximum_fusion
  6.8 0.6 tile.10
  7.4 0.2 reshape.10
  7.6 0.1 copy.11
  7.7 0.0 copy-done.2
  7.7 0.0 copy-done.3
  7.7 16.0 %shard_map.55 = (bf16[128,16,512]{2,1,0:T(8,128)(2,1)S(1)}, bf16[128,16,512]{2,1,0:T(8,128)(2,1)S(1)}, bf16[512,256]{1,0:T(8,128)(2,1)S(1)}) custom-call(s32[8]{0:T(128)S(1)} %copy-done.3, bf16[512,8192]{1,0:T(8,128)(2,1)} %rec_ref.3, bf16[512,256]{1,0:T(8,128)(2,1)S(1)} %bitcast.5, bf16[512,256]{1,0:T(8,128)(2,1)S(1)} %copy-done.2), custom_call_target="tpu_custom_call" | custom-call | flops 12884901888 | bytes 12582912 | tf_op jit(solution)/shard_map/pallas_call | solution.py:206
  23.8 0.0 collective-permute-done.tail_ref
  23.8 3.6 %shard_map.56 = (bf16[128,16,512]{2,1,0:T(8,128)(2,1)S(1)}, bf16[128,16,512]{2,1,0:T(8,128)(2,1)S(1)}) custom-call(s32[8]{0:T(128)S(1)} %copy-done.3, bf16[512,256]{1,0:T(8,128)(2,1)S(1)} %collective-permute-done.tail_ref, bf16[512,8192]{1,0:T(8,128)(2,1)} %rec_ref.3, ...), custom_call_target="tpu_custom_call", output_to_operand_aliasing={{0}: (6, {}), {1}: (7, {})} | custom-call | flops 402653184 | bytes 8388608 | tf_op jit(solution)/shard_map/pallas_call | solution.py:160
  27.4 0.0 copy-start.1
  27.4 52.8 %all_to_all.10.am_ref.bm_ref = bf16[8,8,2,16,512]{4,3,2,1,0:T(8,128)(2,1)} all-to-all(bf16[8,8,2,16,512]{4,3,2,1,0:T(8,128)(2,1)S(1)} %bitcast.3), channel_id=1, replica_groups=mesh['groups'=2,'tm'=8,'pair'=2] {'tm'}, dimensions={0} | all-to-all | bytes 4194304 | tf_op jit(solution)/shard_map/all_to_all | solution.py:310
  80.2 0.0 copy-done.1
  80.2 0.0 copy-start.4
  80.2 3.7 %all-to-all-start = ((bf16[8,8,2,16,512]{4,3,2,1,0:T(8,128)(2,1)}), bf16[8,8,2,16,512]{4,3,2,1,0:T(8,128)(2,1)S(1)}, u32[]{:S(2)}, u32[]{:S(2)}) async-start(bf16[8,8,2,16,512]{4,3,2,1,0:T(8,128)(2,1)} %bitcast.4), calls=%async_computation | async-start | bytes 4194304 | tf_op jit(solution)/shard_map/all_to_all | solution.py:310
  83.9 0.1 collective-permute-start.2
  84.0 47.6 %all-to-all-done.am_ref.bm_ref = bf16[8,8,2,16,512]{4,3,2,1,0:T(8,128)(2,1)S(1)} async-done(((bf16[8,8,2,16,512]{4,3,2,1,0:T(8,128)(2,1)}), bf16[8,8,2,16,512]{4,3,2,1,0:T(8,128)(2,1)S(1)}, u32[]{:S(2)}, u32[]{:S(2)}) %all-to-all-start) | async-done | bytes 2097184 | tf_op jit(solution)/shard_map/all_to_all | solution.py:310
  131.6 0.0 collective-permute-start.1
  131.6 0.0 copy-done.4
  131.6 0.1 copy.13.pb_ref
  131.7 0.0 collective-permute-done.2.ap_ref.bp_ref
  131.7 0.0 copy-start
  131.7 1.6 %copy-done = bf16[8,8,2,16,512]{4,3,2,1,0:T(8,128)(2,1)S(1)} copy-done((bf16[8,8,2,16,512]{4,3,2,1,0:T(8,128)(2,1)S(1)}, bf16[8,8,2,16,512]{4,3,2,1,0:T(8,128)(2,1)}, u32[]{:S(2)}) %copy-start) | copy-done | bytes 2097176
  133.3 10.0 %shard_map.57.rest_0_ = f32[8,16,2,128,128]{4,3,2,1,0:T(8,128)} custom-call(s32[8,2]{1,0:T(8,128)S(1)} %copy.13.pb_ref, s32[8]{0:T(128)S(1)} %copy-done.3, bf16[8,8,2,16,512]{4,3,2,1,0:T(8,128)(2,1)S(1)} %copy-done, bf16[8,8,2,16,512]{4,3,2,1,0:T(8,128)(2,1)} %collective-permute-done.2.ap_ref.bp_ref, bf16[8,8,2,16,512]{4,3,2,1,0:T(8,128)(2,1)S(1)} %copy-done, ...), custom_call_target="tpu_custom_call" | custom-call | flops 1073741824 | bytes 25165824 | tf_op jit(solution)/shard_map/pallas_call | solution.py:283
  143.4 0.0 collective-permute-done.1.ap_ref.bp_ref
  143.4 10.0 %shard_map.58 = f32[8,16,2,128,128]{4,3,2,1,0:T(8,128)} custom-call(s32[8,2]{1,0:T(8,128)S(1)} %copy.13.pb_ref, s32[8]{0:T(128)S(1)} %copy-done.3, bf16[8,8,2,16,512]{4,3,2,1,0:T(8,128)(2,1)S(1)} %all-to-all-done.am_ref.bm_ref, bf16[8,8,2,16,512]{4,3,2,1,0:T(8,128)(2,1)} %collective-permute-done.1.ap_ref.bp_ref, ...), custom_call_target="tpu_custom_call", output_to_operand_aliasing={{}: (6, {})} | custom-call | flops 1073741824 | bytes 25165824 | tf_op jit(solution)/shard_map/pallas_call | solution.py:283
  (3 shorter events, 0.1 us)
Async XLA Ops:
  0.0 7.7 %copy-start.2 = (bf16[512,256]{1,0:T(8,128)(2,1)S(1)}, bf16[512,256]{1,0:T(8,128)(2,1)}, u32[]{:S(2)}) copy-start(bf16[512,256]{1,0:T(8,128)(2,1)} %constant.6.clone.basis_ref) | copy-start | bytes 786436
  0.0 7.7 %copy-start.3 = (s32[8]{0:T(128)S(1)}, s32[8]{0:T(128)}, u32[]{:S(2)}) copy-start(s32[8]{0:T(128)} %kw_ref.3) | copy-start | bytes 100
  1.0 22.8 %collective-permute-start = (bf16[512,256]{1,0:T(8,128)(2,1)S(1)}, bf16[512,256]{1,0:T(8,128)(2,1)S(1)}, u32[]{:S(2)}, u32[]{:S(2)}) collective-permute-start(bf16[512,256]{1,0:T(8,128)(2,1)S(1)} %slice.6), channel_id=1, source_target_pairs={{0,2},{2,4},{4,6},{6,8},{8,10},{10,12},{12,14},{1,3},{3,5},{5,7},{... | collective-permute-start | bytes 786440 | tf_op jit(solution)/shard_map/ppermute | solution.py:25
  27.4 52.8 %copy-start.1 = (bf16[128,16,512]{2,1,0:T(8,128)(2,1)}, bf16[128,16,512]{2,1,0:T(8,128)(2,1)S(1)}, u32[]{:S(2)}) copy-start(bf16[128,16,512]{2,1,0:T(8,128)(2,1)S(1)} %get-tuple-element.13) | copy-start | bytes 6291460
  80.2 51.5 %copy-start.4 = (s32[8,2]{0,1:T(2,128)S(1)}, s32[8,2]{0,1:T(2,128)}, u32[]{:S(2)}) copy-start(s32[8,2]{0,1:T(2,128)} %param.8) | copy-start | bytes 196
  80.2 51.4 %all-to-all-start = ((bf16[8,8,2,16,512]{4,3,2,1,0:T(8,128)(2,1)}), bf16[8,8,2,16,512]{4,3,2,1,0:T(8,128)(2,1)S(1)}, u32[]{:S(2)}, u32[]{:S(2)}) async-start(bf16[8,8,2,16,512]{4,3,2,1,0:T(8,128)(2,1)} %bitcast.4), calls=%async_computation | async-start | bytes 4194304 | tf_op jit(solution)/shard_map/all_to_all | solution.py:310
  83.9 47.8 %collective-permute-start.2 = (bf16[8,8,2,16,512]{4,3,2,1,0:T(8,128)(2,1)}, bf16[8,8,2,16,512]{4,3,2,1,0:T(8,128)(2,1)}, u32[]{:S(2)}, u32[]{:S(2)}) collective-permute-start(bf16[8,8,2,16,512]{4,3,2,1,0:T(8,128)(2,1)} %all_to_all.10.am_ref.bm_ref), channel_id=1, source_target_pairs={{0,1},{1,0},{2,3},{3,2},{4,5},{5,4},{6,7},{7,6},{8,9},{9,8},{10,11... | collective-permute-start | bytes 6291464 | tf_op jit(solution)/shard_map/ppermute | solution.py:311
  131.6 11.7 %collective-permute-start.1 = (bf16[8,8,2,16,512]{4,3,2,1,0:T(8,128)(2,1)S(1)}, bf16[8,8,2,16,512]{4,3,2,1,0:T(8,128)(2,1)}, u32[]{:S(2)}, u32[]{:S(2)}) collective-permute-start(bf16[8,8,2,16,512]{4,3,2,1,0:T(8,128)(2,1)S(1)} %all-to-all-done.am_ref.bm_ref), channel_id=1, source_target_pairs={{0,1},{1,0},{2,3},{3,2},{4,5},{5,4},{6,7},{7,6},{8,9},{9,8},{10,11... | collective-permute-start | bytes 6291464 | tf_op jit(solution)/shard_map/ppermute | solution.py:311
  131.7 1.6 %copy-start = (bf16[8,8,2,16,512]{4,3,2,1,0:T(8,128)(2,1)S(1)}, bf16[8,8,2,16,512]{4,3,2,1,0:T(8,128)(2,1)}, u32[]{:S(2)}) copy-start(bf16[8,8,2,16,512]{4,3,2,1,0:T(8,128)(2,1)} %all_to_all.10.am_ref.bm_ref) | copy-start | bytes 6291460

commit v22 on v20

--- a/solution.py
+++ b/solution.py
@@ -108,7 +108,7 @@
                 o_ref[k, :, CH_BLK * h : CH_BLK * (h + 1)] = part.astype(o_ref.dtype)
             return carry
 
-        lax.fori_loop(0, o_ref.shape[0], one_row, 0, unroll=32)
+        lax.fori_loop(0, o_ref.shape[0], one_row, 0, unroll=64)
         start += o_ref.shape[0]
 
 

time: 154 us -> 154 us (level)
  no operation moved by 1% of the time
where the time goes in v22:
time: 154 us
  blocking collectives  52.8 us (34%)
  waiting for transfers between devices  47.6 us (31%)
  Pallas kernels  39.8 us (26%)
  starting transfers between devices  8.7 us (6%)
  local copies, waits for them, and re-layouts  4.41 us (3%)
    all_to_all x1, blocking collectives, per_device(): lax.all_to_all(outgoing, 'tm', split_axis=0, concat_axis=0, tiled=True)  52.8 us
    all_to_all x1, waiting for transfers between devices, per_device(): lax.all_to_all(outgoing, 'tm', split_axis=0, concat_axis=0, tiled=True)  47.6 us
    pallas_call x2, Pallas kernels, stack_pairs(): pl.pallas_call(functools.partial(stack_kernel_for, blocks_per_half), grid...  20.3 us
    pallas_call x1, Pallas kernels, whiten_front(): pl.pallas_call(front_kernel, grid_spec=grid_spec, out_shape=[jax.ShapeDty...  15.9 us
    ppermute x1, starting transfers between devices, from_behind(): return lax.ppermute(array, axis, pairs)  4.89 us
    all_to_all x1, starting transfers between devices, per_device(): lax.all_to_all(outgoing, 'tm', split_axis=0, concat_axis=0, tiled=True)  3.74 us
    pallas_call x1, Pallas kernels, fill_first_window(): pl.pallas_call(functools.partial(first_window_kernel, count_parts), grid_...  3.59 us
  transfers between devices with their start and end apart: 4, of which 1 were waited for; matrix products, arithmetic and copies ran while one was open for 1% of the time, Pallas kernels for 17%

profile of v22, /device:TPU:0, one launch (start us, length us, event | category | flops | bytes accessed | tf_op | source)
XLA Modules:
  0.0 153.5 jit_solution(10362761747327978804)
XLA Ops:
  0.0 0.0 copy-start.2
  0.0 0.0 copy-start.3
  0.0 1.0 slice.6
  1.0 4.9 %collective-permute-start = (bf16[512,256]{1,0:T(8,128)(2,1)S(1)}, bf16[512,256]{1,0:T(8,128)(2,1)S(1)}, u32[]{:S(2)}, u32[]{:S(2)}) collective-permute-start(bf16[512,256]{1,0:T(8,128)(2,1)S(1)} %slice.6), channel_id=1, source_target_pairs={{0,2},{2,4},{4,6},{6,8},{8,10},{10,12},{12,14},{1,3},{3,5},{5,7},{... | collective-permute-start | bytes 786440 | tf_op jit(solution)/shard_map/ppermute | solution.py:25
  5.9 0.7 rev.3
  6.7 0.1 pad_maximum_fusion
  6.8 0.6 tile.10
  7.4 0.2 reshape.10
  7.6 0.1 copy.11
  7.7 0.0 copy-done.2
  7.7 0.0 copy-done.3
  7.7 15.9 %shard_map.55 = (bf16[128,16,512]{2,1,0:T(8,128)(2,1)S(1)}, bf16[128,16,512]{2,1,0:T(8,128)(2,1)S(1)}, bf16[512,256]{1,0:T(8,128)(2,1)S(1)}) custom-call(s32[8]{0:T(128)S(1)} %copy-done.3, bf16[512,8192]{1,0:T(8,128)(2,1)} %rec_ref.3, bf16[512,256]{1,0:T(8,128)(2,1)S(1)} %bitcast.5, bf16[512,256]{1,0:T(8,128)(2,1)S(1)} %copy-done.2), custom_call_target="tpu_custom_call" | custom-call | flops 12884901888 | bytes 12582912 | tf_op jit(solution)/shard_map/pallas_call | solution.py:206
  23.7 0.0 collective-permute-done.tail_ref
  23.7 3.6 %shard_map.56 = (bf16[128,16,512]{2,1,0:T(8,128)(2,1)S(1)}, bf16[128,16,512]{2,1,0:T(8,128)(2,1)S(1)}) custom-call(s32[8]{0:T(128)S(1)} %copy-done.3, bf16[512,256]{1,0:T(8,128)(2,1)S(1)} %collective-permute-done.tail_ref, bf16[512,8192]{1,0:T(8,128)(2,1)} %rec_ref.3, ...), custom_call_target="tpu_custom_call", output_to_operand_aliasing={{0}: (6, {}), {1}: (7, {})} | custom-call | flops 402653184 | bytes 8388608 | tf_op jit(solution)/shard_map/pallas_call | solution.py:160
  27.3 0.0 copy-start.1
  27.3 52.8 %all_to_all.10.am_ref.bm_ref = bf16[8,8,2,16,512]{4,3,2,1,0:T(8,128)(2,1)} all-to-all(bf16[8,8,2,16,512]{4,3,2,1,0:T(8,128)(2,1)S(1)} %bitcast.3), channel_id=1, replica_groups=mesh['groups'=2,'tm'=8,'pair'=2] {'tm'}, dimensions={0} | all-to-all | bytes 4194304 | tf_op jit(solution)/shard_map/all_to_all | solution.py:310
  80.1 0.0 copy-done.1
  80.1 0.0 copy-start.4
  80.1 3.7 %all-to-all-start = ((bf16[8,8,2,16,512]{4,3,2,1,0:T(8,128)(2,1)}), bf16[8,8,2,16,512]{4,3,2,1,0:T(8,128)(2,1)S(1)}, u32[]{:S(2)}, u32[]{:S(2)}) async-start(bf16[8,8,2,16,512]{4,3,2,1,0:T(8,128)(2,1)} %bitcast.4), calls=%async_computation | async-start | bytes 4194304 | tf_op jit(solution)/shard_map/all_to_all | solution.py:310
  83.9 0.1 collective-permute-start.2
  84.0 47.6 %all-to-all-done.am_ref.bm_ref = bf16[8,8,2,16,512]{4,3,2,1,0:T(8,128)(2,1)S(1)} async-done(((bf16[8,8,2,16,512]{4,3,2,1,0:T(8,128)(2,1)}), bf16[8,8,2,16,512]{4,3,2,1,0:T(8,128)(2,1)S(1)}, u32[]{:S(2)}, u32[]{:S(2)}) %all-to-all-start) | async-done | bytes 2097184 | tf_op jit(solution)/shard_map/all_to_all | solution.py:310
  131.6 0.0 collective-permute-start.1
  131.6 0.0 copy-done.4
  131.6 0.1 copy.13.pb_ref
  131.7 0.0 collective-permute-done.2.ap_ref.bp_ref
  131.7 0.0 copy-start
  131.7 1.6 %copy-done = bf16[8,8,2,16,512]{4,3,2,1,0:T(8,128)(2,1)S(1)} copy-done((bf16[8,8,2,16,512]{4,3,2,1,0:T(8,128)(2,1)S(1)}, bf16[8,8,2,16,512]{4,3,2,1,0:T(8,128)(2,1)}, u32[]{:S(2)}) %copy-start) | copy-done | bytes 2097176
  133.3 10.1 %shard_map.57.rest_0_ = f32[8,16,2,128,128]{4,3,2,1,0:T(8,128)} custom-call(s32[8,2]{1,0:T(8,128)S(1)} %copy.13.pb_ref, s32[8]{0:T(128)S(1)} %copy-done.3, bf16[8,8,2,16,512]{4,3,2,1,0:T(8,128)(2,1)S(1)} %copy-done, bf16[8,8,2,16,512]{4,3,2,1,0:T(8,128)(2,1)} %collective-permute-done.2.ap_ref.bp_ref, bf16[8,8,2,16,512]{4,3,2,1,0:T(8,128)(2,1)S(1)} %copy-done, ...), custom_call_target="tpu_custom_call" | custom-call | flops 1073741824 | bytes 25165824 | tf_op jit(solution)/shard_map/pallas_call | solution.py:283
  143.4 0.0 collective-permute-done.1.ap_ref.bp_ref
  143.4 10.2 %shard_map.58 = f32[8,16,2,128,128]{4,3,2,1,0:T(8,128)} custom-call(s32[8,2]{1,0:T(8,128)S(1)} %copy.13.pb_ref, s32[8]{0:T(128)S(1)} %copy-done.3, bf16[8,8,2,16,512]{4,3,2,1,0:T(8,128)(2,1)S(1)} %all-to-all-done.am_ref.bm_ref, bf16[8,8,2,16,512]{4,3,2,1,0:T(8,128)(2,1)} %collective-permute-done.1.ap_ref.bp_ref, ...), custom_call_target="tpu_custom_call", output_to_operand_aliasing={{}: (6, {})} | custom-call | flops 1073741824 | bytes 25165824 | tf_op jit(solution)/shard_map/pallas_call | solution.py:283
  (3 shorter events, 0.1 us)
Async XLA Ops:
  0.0 7.7 %copy-start.2 = (bf16[512,256]{1,0:T(8,128)(2,1)S(1)}, bf16[512,256]{1,0:T(8,128)(2,1)}, u32[]{:S(2)}) copy-start(bf16[512,256]{1,0:T(8,128)(2,1)} %constant.6.clone.basis_ref) | copy-start | bytes 786436
  0.0 7.7 %copy-start.3 = (s32[8]{0:T(128)S(1)}, s32[8]{0:T(128)}, u32[]{:S(2)}) copy-start(s32[8]{0:T(128)} %kw_ref.3) | copy-start | bytes 100
  1.0 22.7 %collective-permute-start = (bf16[512,256]{1,0:T(8,128)(2,1)S(1)}, bf16[512,256]{1,0:T(8,128)(2,1)S(1)}, u32[]{:S(2)}, u32[]{:S(2)}) collective-permute-start(bf16[512,256]{1,0:T(8,128)(2,1)S(1)} %slice.6), channel_id=1, source_target_pairs={{0,2},{2,4},{4,6},{6,8},{8,10},{10,12},{12,14},{1,3},{3,5},{5,7},{... | collective-permute-start | bytes 786440 | tf_op jit(solution)/shard_map/ppermute | solution.py:25
  27.3 52.8 %copy-start.1 = (bf16[128,16,512]{2,1,0:T(8,128)(2,1)}, bf16[128,16,512]{2,1,0:T(8,128)(2,1)S(1)}, u32[]{:S(2)}) copy-start(bf16[128,16,512]{2,1,0:T(8,128)(2,1)S(1)} %get-tuple-element.13) | copy-start | bytes 6291460
  80.1 51.5 %copy-start.4 = (s32[8,2]{0,1:T(2,128)S(1)}, s32[8,2]{0,1:T(2,128)}, u32[]{:S(2)}) copy-start(s32[8,2]{0,1:T(2,128)} %param.8) | copy-start | bytes 196
  80.1 51.5 %all-to-all-start = ((bf16[8,8,2,16,512]{4,3,2,1,0:T(8,128)(2,1)}), bf16[8,8,2,16,512]{4,3,2,1,0:T(8,128)(2,1)S(1)}, u32[]{:S(2)}, u32[]{:S(2)}) async-start(bf16[8,8,2,16,512]{4,3,2,1,0:T(8,128)(2,1)} %bitcast.4), calls=%async_computation | async-start | bytes 4194304 | tf_op jit(solution)/shard_map/all_to_all | solution.py:310
  83.9 47.8 %collective-permute-start.2 = (bf16[8,8,2,16,512]{4,3,2,1,0:T(8,128)(2,1)}, bf16[8,8,2,16,512]{4,3,2,1,0:T(8,128)(2,1)}, u32[]{:S(2)}, u32[]{:S(2)}) collective-permute-start(bf16[8,8,2,16,512]{4,3,2,1,0:T(8,128)(2,1)} %all_to_all.10.am_ref.bm_ref), channel_id=1, source_target_pairs={{0,1},{1,0},{2,3},{3,2},{4,5},{5,4},{6,7},{7,6},{8,9},{9,8},{10,11... | collective-permute-start | bytes 6291464 | tf_op jit(solution)/shard_map/ppermute | solution.py:311
  131.6 11.8 %collective-permute-start.1 = (bf16[8,8,2,16,512]{4,3,2,1,0:T(8,128)(2,1)S(1)}, bf16[8,8,2,16,512]{4,3,2,1,0:T(8,128)(2,1)}, u32[]{:S(2)}, u32[]{:S(2)}) collective-permute-start(bf16[8,8,2,16,512]{4,3,2,1,0:T(8,128)(2,1)S(1)} %all-to-all-done.am_ref.bm_ref), channel_id=1, source_target_pairs={{0,1},{1,0},{2,3},{3,2},{4,5},{5,4},{6,7},{7,6},{8,9},{9,8},{10,11... | collective-permute-start | bytes 6291464 | tf_op jit(solution)/shard_map/ppermute | solution.py:311
  131.7 1.6 %copy-start = (bf16[8,8,2,16,512]{4,3,2,1,0:T(8,128)(2,1)S(1)}, bf16[8,8,2,16,512]{4,3,2,1,0:T(8,128)(2,1)}, u32[]{:S(2)}) copy-start(bf16[8,8,2,16,512]{4,3,2,1,0:T(8,128)(2,1)} %all_to_all.10.am_ref.bm_ref) | copy-start | bytes 6291460

commit v23 on v22

--- a/solution.py
+++ b/solution.py
@@ -108,7 +108,7 @@
                 o_ref[k, :, CH_BLK * h : CH_BLK * (h + 1)] = part.astype(o_ref.dtype)
             return carry
 
-        lax.fori_loop(0, o_ref.shape[0], one_row, 0, unroll=64)
+        lax.fori_loop(0, o_ref.shape[0], one_row, 0, unroll=True)
         start += o_ref.shape[0]
 
 

time: 154 us -> 157 us (1.019)
  Pallas kernels: 39.8 us -> 42 us
    pallas_call x1, Pallas kernels: 15.9 us -> 18.2 us  [whiten_front(): pl.pallas_call(front_kernel, grid_spec=grid_spec, out_shape=[jax.ShapeDty...]
  transfers between devices with their start and end apart: 4 -> 4, of which waited for: 1 -> 1; matrix products, arithmetic and copies ran while one was open for 1% -> 1% of each run, Pallas kernels for 17% -> 18%
where the time goes in v23:
time: 157 us; the launch traced here: 156 us
  blocking collectives  52.8 us (34%)
  waiting for transfers between devices  47.6 us (30%)
  Pallas kernels  42 us (27%)
  starting transfers between devices  8.7 us (6%)
  local copies, waits for them, and re-layouts  4.41 us (3%)
    all_to_all x1, blocking collectives, per_device(): lax.all_to_all(outgoing, 'tm', split_axis=0, concat_axis=0, tiled=True)  52.8 us
    all_to_all x1, waiting for transfers between devices, per_device(): lax.all_to_all(outgoing, 'tm', split_axis=0, concat_axis=0, tiled=True)  47.6 us
    pallas_call x2, Pallas kernels, stack_pairs(): pl.pallas_call(functools.partial(stack_kernel_for, blocks_per_half), grid...  20.2 us
    pallas_call x1, Pallas kernels, whiten_front(): pl.pallas_call(front_kernel, grid_spec=grid_spec, out_shape=[jax.ShapeDty...  18.2 us
    ppermute x1, starting transfers between devices, from_behind(): return lax.ppermute(array, axis, pairs)  4.89 us
    all_to_all x1, starting transfers between devices, per_device(): lax.all_to_all(outgoing, 'tm', split_axis=0, concat_axis=0, tiled=True)  3.74 us
    pallas_call x1, Pallas kernels, fill_first_window(): pl.pallas_call(functools.partial(first_window_kernel, count_parts), grid_...  3.59 us
  transfers between devices with their start and end apart: 4, of which 1 were waited for; matrix products, arithmetic and copies ran while one was open for 1% of the time, Pallas kernels for 18%

profile of v23, /device:TPU:0, one launch (start us, length us, event | category | flops | bytes accessed | tf_op | source)
XLA Modules:
  0.0 155.8 jit_solution(5386592381662691076)
XLA Ops:
  0.0 0.0 copy-start.2
  0.0 0.0 copy-start.3
  0.0 1.0 slice.6
  1.0 4.9 %collective-permute-start = (bf16[512,256]{1,0:T(8,128)(2,1)S(1)}, bf16[512,256]{1,0:T(8,128)(2,1)S(1)}, u32[]{:S(2)}, u32[]{:S(2)}) collective-permute-start(bf16[512,256]{1,0:T(8,128)(2,1)S(1)} %slice.6), channel_id=1, source_target_pairs={{0,2},{2,4},{4,6},{6,8},{8,10},{10,12},{12,14},{1,3},{3,5},{5,7},{... | collective-permute-start | bytes 786440 | tf_op jit(solution)/shard_map/ppermute | solution.py:25
  5.9 0.7 rev.3
  6.7 0.1 pad_maximum_fusion
  6.8 0.6 tile.10
  7.4 0.2 reshape.10
  7.6 0.1 copy.11
  7.7 0.0 copy-done.2
  7.7 0.0 copy-done.3
  7.7 18.2 %shard_map.55 = (bf16[128,16,512]{2,1,0:T(8,128)(2,1)S(1)}, bf16[128,16,512]{2,1,0:T(8,128)(2,1)S(1)}, bf16[512,256]{1,0:T(8,128)(2,1)S(1)}) custom-call(s32[8]{0:T(128)S(1)} %copy-done.3, bf16[512,8192]{1,0:T(8,128)(2,1)} %rec_ref.3, bf16[512,256]{1,0:T(8,128)(2,1)S(1)} %bitcast.5, bf16[512,256]{1,0:T(8,128)(2,1)S(1)} %copy-done.2), custom_call_target="tpu_custom_call" | custom-call | flops 12884901888 | bytes 12582912 | tf_op jit(solution)/shard_map/pallas_call | solution.py:206
  26.0 0.0 collective-permute-done.tail_ref
  26.0 3.6 %shard_map.56 = (bf16[128,16,512]{2,1,0:T(8,128)(2,1)S(1)}, bf16[128,16,512]{2,1,0:T(8,128)(2,1)S(1)}) custom-call(s32[8]{0:T(128)S(1)} %copy-done.3, bf16[512,256]{1,0:T(8,128)(2,1)S(1)} %collective-permute-done.tail_ref, bf16[512,8192]{1,0:T(8,128)(2,1)} %rec_ref.3, ...), custom_call_target="tpu_custom_call", output_to_operand_aliasing={{0}: (6, {}), {1}: (7, {})} | custom-call | flops 402653184 | bytes 8388608 | tf_op jit(solution)/shard_map/pallas_call | solution.py:160
  29.6 0.0 copy-start.1
  29.6 52.8 %all_to_all.10.am_ref.bm_ref = bf16[8,8,2,16,512]{4,3,2,1,0:T(8,128)(2,1)} all-to-all(bf16[8,8,2,16,512]{4,3,2,1,0:T(8,128)(2,1)S(1)} %bitcast.3), channel_id=1, replica_groups=mesh['groups'=2,'tm'=8,'pair'=2] {'tm'}, dimensions={0} | all-to-all | bytes 4194304 | tf_op jit(solution)/shard_map/all_to_all | solution.py:310
  82.4 0.0 copy-done.1
  82.4 0.0 copy-start.4
  82.4 3.7 %all-to-all-start = ((bf16[8,8,2,16,512]{4,3,2,1,0:T(8,128)(2,1)}), bf16[8,8,2,16,512]{4,3,2,1,0:T(8,128)(2,1)S(1)}, u32[]{:S(2)}, u32[]{:S(2)}) async-start(bf16[8,8,2,16,512]{4,3,2,1,0:T(8,128)(2,1)} %bitcast.4), calls=%async_computation | async-start | bytes 4194304 | tf_op jit(solution)/shard_map/all_to_all | solution.py:310
  86.2 0.1 collective-permute-start.2
  86.3 47.6 %all-to-all-done.am_ref.bm_ref = bf16[8,8,2,16,512]{4,3,2,1,0:T(8,128)(2,1)S(1)} async-done(((bf16[8,8,2,16,512]{4,3,2,1,0:T(8,128)(2,1)}), bf16[8,8,2,16,512]{4,3,2,1,0:T(8,128)(2,1)S(1)}, u32[]{:S(2)}, u32[]{:S(2)}) %all-to-all-start) | async-done | bytes 2097184 | tf_op jit(solution)/shard_map/all_to_all | solution.py:310
  133.9 0.0 collective-permute-start.1
  133.9 0.0 copy-done.4
  133.9 0.1 copy.13.pb_ref
  134.0 0.0 collective-permute-done.2.ap_ref.bp_ref
  134.0 0.0 copy-start
  134.0 1.6 %copy-done = bf16[8,8,2,16,512]{4,3,2,1,0:T(8,128)(2,1)S(1)} copy-done((bf16[8,8,2,16,512]{4,3,2,1,0:T(8,128)(2,1)S(1)}, bf16[8,8,2,16,512]{4,3,2,1,0:T(8,128)(2,1)}, u32[]{:S(2)}) %copy-start) | copy-done | bytes 2097176
  135.6 10.1 %shard_map.57.rest_0_ = f32[8,16,2,128,128]{4,3,2,1,0:T(8,128)} custom-call(s32[8,2]{1,0:T(8,128)S(1)} %copy.13.pb_ref, s32[8]{0:T(128)S(1)} %copy-done.3, bf16[8,8,2,16,512]{4,3,2,1,0:T(8,128)(2,1)S(1)} %copy-done, bf16[8,8,2,16,512]{4,3,2,1,0:T(8,128)(2,1)} %collective-permute-done.2.ap_ref.bp_ref, bf16[8,8,2,16,512]{4,3,2,1,0:T(8,128)(2,1)S(1)} %copy-done, ...), custom_call_target="tpu_custom_call" | custom-call | flops 1073741824 | bytes 25165824 | tf_op jit(solution)/shard_map/pallas_call | solution.py:283
  145.6 0.0 collective-permute-done.1.ap_ref.bp_ref
  145.6 10.1 %shard_map.58 = f32[8,16,2,128,128]{4,3,2,1,0:T(8,128)} custom-call(s32[8,2]{1,0:T(8,128)S(1)} %copy.13.pb_ref, s32[8]{0:T(128)S(1)} %copy-done.3, bf16[8,8,2,16,512]{4,3,2,1,0:T(8,128)(2,1)S(1)} %all-to-all-done.am_ref.bm_ref, bf16[8,8,2,16,512]{4,3,2,1,0:T(8,128)(2,1)} %collective-permute-done.1.ap_ref.bp_ref, ...), custom_call_target="tpu_custom_call", output_to_operand_aliasing={{}: (6, {})} | custom-call | flops 1073741824 | bytes 25165824 | tf_op jit(solution)/shard_map/pallas_call | solution.py:283
  (3 shorter events, 0.1 us)
Async XLA Ops:
  0.0 7.7 %copy-start.2 = (bf16[512,256]{1,0:T(8,128)(2,1)S(1)}, bf16[512,256]{1,0:T(8,128)(2,1)}, u32[]{:S(2)}) copy-start(bf16[512,256]{1,0:T(8,128)(2,1)} %constant.6.clone.basis_ref) | copy-start | bytes 786436
  0.0 7.7 %copy-start.3 = (s32[8]{0:T(128)S(1)}, s32[8]{0:T(128)}, u32[]{:S(2)}) copy-start(s32[8]{0:T(128)} %kw_ref.3) | copy-start | bytes 100
  1.0 25.0 %collective-permute-start = (bf16[512,256]{1,0:T(8,128)(2,1)S(1)}, bf16[512,256]{1,0:T(8,128)(2,1)S(1)}, u32[]{:S(2)}, u32[]{:S(2)}) collective-permute-start(bf16[512,256]{1,0:T(8,128)(2,1)S(1)} %slice.6), channel_id=1, source_target_pairs={{0,2},{2,4},{4,6},{6,8},{8,10},{10,12},{12,14},{1,3},{3,5},{5,7},{... | collective-permute-start | bytes 786440 | tf_op jit(solution)/shard_map/ppermute | solution.py:25
  29.6 52.8 %copy-start.1 = (bf16[128,16,512]{2,1,0:T(8,128)(2,1)}, bf16[128,16,512]{2,1,0:T(8,128)(2,1)S(1)}, u32[]{:S(2)}) copy-start(bf16[128,16,512]{2,1,0:T(8,128)(2,1)S(1)} %get-tuple-element.13) | copy-start | bytes 6291460
  82.4 51.5 %copy-start.4 = (s32[8,2]{0,1:T(2,128)S(1)}, s32[8,2]{0,1:T(2,128)}, u32[]{:S(2)}) copy-start(s32[8,2]{0,1:T(2,128)} %param.8) | copy-start | bytes 196
  82.4 51.4 %all-to-all-start = ((bf16[8,8,2,16,512]{4,3,2,1,0:T(8,128)(2,1)}), bf16[8,8,2,16,512]{4,3,2,1,0:T(8,128)(2,1)S(1)}, u32[]{:S(2)}, u32[]{:S(2)}) async-start(bf16[8,8,2,16,512]{4,3,2,1,0:T(8,128)(2,1)} %bitcast.4), calls=%async_computation | async-start | bytes 4194304 | tf_op jit(solution)/shard_map/all_to_all | solution.py:310
  86.2 47.8 %collective-permute-start.2 = (bf16[8,8,2,16,512]{4,3,2,1,0:T(8,128)(2,1)}, bf16[8,8,2,16,512]{4,3,2,1,0:T(8,128)(2,1)}, u32[]{:S(2)}, u32[]{:S(2)}) collective-permute-start(bf16[8,8,2,16,512]{4,3,2,1,0:T(8,128)(2,1)} %all_to_all.10.am_ref.bm_ref), channel_id=1, source_target_pairs={{0,1},{1,0},{2,3},{3,2},{4,5},{5,4},{6,7},{7,6},{8,9},{9,8},{10,11... | collective-permute-start | bytes 6291464 | tf_op jit(solution)/shard_map/ppermute | solution.py:311
  133.9 11.8 %collective-permute-start.1 = (bf16[8,8,2,16,512]{4,3,2,1,0:T(8,128)(2,1)S(1)}, bf16[8,8,2,16,512]{4,3,2,1,0:T(8,128)(2,1)}, u32[]{:S(2)}, u32[]{:S(2)}) collective-permute-start(bf16[8,8,2,16,512]{4,3,2,1,0:T(8,128)(2,1)S(1)} %all-to-all-done.am_ref.bm_ref), channel_id=1, source_target_pairs={{0,1},{1,0},{2,3},{3,2},{4,5},{5,4},{6,7},{7,6},{8,9},{9,8},{10,11... | collective-permute-start | bytes 6291464 | tf_op jit(solution)/shard_map/ppermute | solution.py:311
  134.0 1.6 %copy-start = (bf16[8,8,2,16,512]{4,3,2,1,0:T(8,128)(2,1)S(1)}, bf16[8,8,2,16,512]{4,3,2,1,0:T(8,128)(2,1)}, u32[]{:S(2)}) copy-start(bf16[8,8,2,16,512]{4,3,2,1,0:T(8,128)(2,1)} %all_to_all.10.am_ref.bm_ref) | copy-start | bytes 6291460
